TPU v7x, 256 devices: a whole 4x4x8 slice. The times are simulated.
256 devices in a mesh: tok: 32 (over x, z), hid: 8 (over y, core).
Axes of the slice: x: 4, y: 4, z: 8, core: 2. Of those that a mesh axis runs over, the one named last changes fastest.
Arguments:
- tokens: bfloat16 [16384, 5376], P('tok', 'hid'), may hold values from -6 to 6
- norm_gain: bfloat16 [1, 5376], P(None, 'hid'), may hold values from 0.099609375 to 1.8984375
- w_query: bfloat16 [5376, 4096], P('tok', 'hid'), may hold values from -2 to 2
- w_key: bfloat16 [5376, 2048], P('tok', 'hid'), may hold values from -1 to 1
- value_matrix: bfloat16 [5376, 2048], P('tok', 'hid'), may hold values from -0.078125 to 0.078125
- q_norm_gain: bfloat16 [1, 128], replicated, may hold values from 0.1 to 8
- k_norm_gain: bfloat16 [1, 128], replicated, may hold values from 0.1 to 8
- w_out: bfloat16 [4096, 5376], P('hid'), may hold values from -0.125 to 0.125
Outputs:
- attended: bfloat16 [16384, 5376], P('tok', 'hid')
All inputs are finite; a program needn't handle non-finite values.
Results may differ from a plain program's by a relative error of at most 0.017.
Values may be sent and summed in bfloat16 or wider, within the bound.
No kernel may reach another device: no remote copies, remote signals or barrier semaphores. Data moves between devices by JAX's collectives and lax.ppermute only.
A program may use at most 64 MiB of HBM per device.

v0:
```python
import math

import jax
import jax.numpy as jnp
from jax import lax
from jax.sharding import PartitionSpec as P

HEAD_SIZE = 128
WINDOW = 1024


score_scale = 168.0 ** (-0.5)


def shifted(value, axis, steps):
    count = lax.axis_size(axis)
    leading, last = (max(0, -steps), min(count, count - steps))
    return lax.ppermute(value, axis, [(source, source + steps) for source in range(leading, last)])


def head_norm(field, gain):
    count = field.shape[0]
    heads = field.reshape(count, -1, HEAD_SIZE)
    mean_square = jnp.mean(heads * heads, axis=-1, keepdims=True)
    scaled = (
        heads * lax.rsqrt(mean_square + 1e-06) * gain.astype(jnp.float32).reshape(1, 1, HEAD_SIZE)
    )
    return scaled.reshape(count, -1)


def rotate(field, positions):
    count = field.shape[0]
    heads = field.reshape(count, -1, HEAD_SIZE)
    half = HEAD_SIZE // 2
    inverse = jnp.exp(-math.log(10000.0) * jnp.arange(half, dtype=jnp.float32) * 2.0 / HEAD_SIZE)
    angles = positions.astype(jnp.float32)[:, None] * inverse[None, :]
    cosine = jnp.cos(angles)[:, None, :]
    sine = jnp.sin(angles)[:, None, :]
    first = heads[..., :half]
    second = heads[..., half:]
    turned = jnp.concatenate(
        [first * cosine - second * sine, second * cosine + first * sine], axis=-1
    )
    return turned.reshape(count, -1)


def local(tokens, norm_gain, w_query, w_key, value_matrix, q_norm_gain, k_norm_gain, w_out):
    rows = tokens.shape[0]
    gathered, gain_row = (
        lax.all_gather(tokens, "hid", axis=1, tiled=True),
        lax.all_gather(norm_gain, "hid", axis=1, tiled=True),
    )
    values32 = gathered.astype(jnp.float32)
    scale_rows = lax.rsqrt(jnp.mean(values32 * values32, axis=1, keepdims=True) + 1e-06)
    normed = (values32 * scale_rows * gain_row.astype(jnp.float32)).astype(jnp.bfloat16)
    width_query = w_query.shape[1]
    width_kv = w_key.shape[1]
    pieces = (
        lax.all_gather(w_query, "tok", axis=0, tiled=True),
        lax.all_gather(w_key, "tok", axis=0, tiled=True),
        lax.all_gather(value_matrix, "tok", axis=0, tiled=True),
    )
    query_raw, key_raw, value_raw = tuple(
        (jnp.dot(normed, piece, preferred_element_type=jnp.float32) for piece in pieces)
    )
    tok_index = lax.axis_index("tok")
    positions = tok_index * rows + jnp.arange(rows, dtype=jnp.int32)
    query = rotate(head_norm(query_raw, q_norm_gain), positions).astype(jnp.bfloat16)
    key = rotate(head_norm(key_raw, k_norm_gain), positions).astype(jnp.bfloat16)
    value_rows = value_raw.astype(jnp.bfloat16)
    joined = jnp.concatenate([key, value_rows], axis=1)
    reach = (WINDOW - 1 + rows - 1) // rows
    earlier = []
    moving = joined
    for offset in range(reach):
        moving = shifted(moving, "tok", 1)
        earlier = [moving] + earlier
    window_kv = jnp.concatenate(earlier + [joined], axis=0)
    window_extent = window_kv.shape[0]
    key_pos = (tok_index - reach) * rows + jnp.arange(window_extent, dtype=jnp.int32)
    kv_heads = width_kv // HEAD_SIZE
    query_group_count = width_query // HEAD_SIZE // kv_heads
    query_four_axes = query.reshape(rows, kv_heads, query_group_count, HEAD_SIZE)
    keys_three_axes = window_kv[:, :width_kv].reshape(window_extent, kv_heads, HEAD_SIZE)
    values_three_axes = window_kv[:, width_kv:].reshape(window_extent, kv_heads, HEAD_SIZE)
    scores = (
        jnp.einsum(
            "tkgd,skd->kgts", query_four_axes, keys_three_axes, preferred_element_type=jnp.float32
        )
        * score_scale
    )
    allowed = (
        (key_pos[None, :] <= positions[:, None])
        & (key_pos[None, :] > positions[:, None] - WINDOW)
        & (key_pos[None, :] >= 0)
    )
    masked = jnp.where(allowed, scores, -1e30)
    top = jnp.max(masked, axis=-1, keepdims=True)
    weights = jnp.where(allowed, jnp.exp(masked - top), 0.0)
    total = jnp.sum(weights, axis=-1)
    probs = weights.astype(jnp.bfloat16)
    mixed = jnp.einsum(
        "kgts,skd->tkgd", probs, values_three_axes, preferred_element_type=jnp.float32
    )
    mixed = mixed / jnp.transpose(total, (2, 0, 1))[..., None]
    heads_out = mixed.reshape(rows, width_query).astype(jnp.bfloat16)
    partial_value = jnp.dot(heads_out, w_out, preferred_element_type=jnp.float32)
    return lax.psum_scatter(
        partial_value.astype(jnp.bfloat16), "hid", scatter_dimension=1, tiled=True
    )


def solution(mesh):
    in_specs = (
        P("tok", "hid"),
        P(None, "hid"),
        P("tok", "hid"),
        P("tok", "hid"),
        P("tok", "hid"),
        P(),
        P(),
        P("hid", None),
    )
    out_specs = P("tok", "hid")
    return jax.shard_map(local, mesh=mesh, in_specs=in_specs, out_specs=out_specs, check_vma=False)
```

profile of v0, /device:TPU:2, one launch (start us, length us, event | category | flops | bytes accessed | tf_op | source)
XLA Modules:
  0.0 373.7 jit_solution(16431467091909844304)
XLA Ops:
  6.5 0.0 all-gather.5.cloned.1.call-start
  6.5 0.7 all-gather.5.cloned.1.call-update
  7.3 0.0 all-gather.7.cloned.1.call-start
  7.3 0.7 all-gather.7.cloned.1.call-update
  8.0 0.0 all-gather.9.cloned.1.call-start
  8.1 0.7 all-gather.9.cloned.1.call-update
  8.7 0.0 all-gather.11.cloned.1.call-start
  8.8 0.5 all-gather.11.cloned.1.call-update
  9.3 0.0 reduce-scatter.2.cloned.1.call-start
  9.4 1.3 dynamic-slice
  11.3 0.7 reduce
  12.0 0.2 dynamic-update-slice
  12.3 27.5 %all-reduce = bf16[5376]{0:T(1024)(128)(2,1)S(1)} all-reduce(bf16[5376]{0:T(1024)(128)(2,1)S(1)} %dynamic-update-slice), channel_id=1, replica_groups=mesh['tok'=32,'hid'=8] {'hid'}, use_global_device_ids=true, to_apply=%add | all-reduce | flops 5376 | bytes 21504
  39.8 0.7 bitcast_convert_fusion.1
  40.5 0.7 bitcast_convert_fusion
  41.1 0.5 multiply_cosine_fusion
  41.7 10.7 %all-gather.5.cloned.1.call-done = bf16[512,5376]{0,1:T(8,128)(2,1)} async-done(((bf16[512,672]{0,1:T(8,128)(2,1)}), bf16[512,5376]{0,1:T(8,128)(2,1)}) %all-gather.5.cloned.1.call-update) | async-done | bytes 5505040 | tf_op jit(solution)/shard_map/all_gather | solution.py:50
  52.4 3.8 %fusion.1 = f32[512]{0:T(512)S(1)} fusion(bf16[512,5376]{0,1:T(8,128)(2,1)} %all-gather.5.cloned.1.call-done), kind=kLoop, calls=%fused_computation.5 | loop fusion | flops 8257024 | bytes 5507072 | tf_op jit(solution)/shard_map/reduce_sum | solution.py:54
  56.2 76.4 %all-gather.7.cloned.1.call-done = bf16[5376,256]{1,0:T(8,128)(2,1)} async-done(((bf16[168,256]{1,0:T(8,128)(2,1)}), bf16[5376,256]{1,0:T(8,128)(2,1)}) %all-gather.7.cloned.1.call-update) | async-done | bytes 2752528 | tf_op jit(solution)/shard_map/all_gather | solution.py:60
  132.6 5.4 %multiply_reduce_fusion.1 = (f32[512,2]{0,1:T(2,128)S(1)}, f32[512,256]{0,1:T(8,128)S(1)}) fusion(bf16[5376,256]{1,0:T(8,128)(2,1)} %all-gather.7.cloned.1.call-done, bf16[512,5376]{0,1:T(8,128)(2,1)} %all-gather.5.cloned.1.call-done, f32[5376]{0:T(1024)S(1)} %mul.219, f32[512]{0:T(512)S(1)} %add_rsqrt_fusion.2), kind=kOutput, calls=%fused_computation.29 | convolution fusion | flops 1420557312 | bytes 8809472 | tf_op jit(solution)/shard_map/dot_general | solution.py:64
  138.1 0.1 multiply_multiply_fusion.1
  138.2 0.1 subtract_convert_fusion.1
  138.3 72.7 %all-gather.9.cloned.1.call-done = bf16[5376,256]{1,0:T(8,128)(2,1)} async-done(((bf16[168,256]{1,0:T(8,128)(2,1)}), bf16[5376,256]{1,0:T(8,128)(2,1)}) %all-gather.9.cloned.1.call-update) | async-done | bytes 2752528 | tf_op jit(solution)/shard_map/all_gather | solution.py:61
  211.0 5.4 %convolution_convert_fusion.1 = bf16[512,256]{0,1:T(8,128)(2,1)S(1)} fusion(bf16[5376,256]{1,0:T(8,128)(2,1)} %all-gather.9.cloned.1.call-done, bf16[512,5376]{0,1:T(8,128)(2,1)} %all-gather.5.cloned.1.call-done, f32[5376]{0:T(1024)S(1)} %mul.219, f32[512]{0:T(512)S(1)} %add_rsqrt_fusion.2), kind=kOutput, calls=%fused_computation.21 | convolution fusion | flops 1420427264 | bytes 8543232 | tf_op jit(solution)/shard_map/dot_general | solution.py:64
  216.5 2.9 collective-permute-start
  219.4 1.1 and_and_fusion
  220.6 10.4 %collective-permute-done = bf16[512,512]{0,1:T(8,128)(2,1)S(1)} collective-permute-done((bf16[512,512]{0,1:T(8,128)(2,1)S(1)}, bf16[512,512]{0,1:T(8,128)(2,1)S(1)}, u32[]{:S(2)}, u32[]{:S(2)}) %collective-permute-start) | collective-permute-done | bytes 524320 | tf_op jit(solution)/shard_map/ppermute | solution.py:18
  231.0 2.1 collective-permute-start.1
  233.1 63.4 %all-gather.11.cloned.1.call-done = bf16[5376,512]{1,0:T(8,128)(2,1)} async-done(((bf16[168,512]{1,0:T(8,128)(2,1)}), bf16[5376,512]{1,0:T(8,128)(2,1)}) %all-gather.11.cloned.1.call-update) | async-done | bytes 5505040 | tf_op jit(solution)/shard_map/all_gather | solution.py:59
  296.5 7.6 %multiply_reduce_fusion = (f32[512,4]{0,1:T(4,128)S(1)}, f32[512,512]{0,1:T(8,128)S(1)}) fusion(bf16[5376,512]{1,0:T(8,128)(2,1)} %all-gather.11.cloned.1.call-done, bf16[512,5376]{0,1:T(8,128)(2,1)} %all-gather.5.cloned.1.call-done, f32[5376]{0:T(1024)S(1)} %mul.219, f32[512]{0:T(512)S(1)} %add_rsqrt_fusion.2), kind=kOutput, calls=%fused_computation.23 | convolution fusion | flops 2830104576 | bytes 12090368 | tf_op jit(solution)/shard_map/dot_general | solution.py:64
  304.1 0.2 multiply_multiply_fusion
  304.3 0.2 subtract_convert_fusion
  304.6 0.0 collective-permute-done.1
  304.6 0.1 maximum_maximum_fusion
  304.7 0.1 fusion.30
  304.8 8.5 %fusion.31 = (f32[2,2,512]{2,1,0:T(2,128)S(1)}, bf16[2,2,512,1536]{2,3,1,0:T(8,128)(2,1)}) fusion(pred[512,1536]{0,1:T(8,128)(4,1)S(1)} %and_and_fusion, bf16[1536,2,128,1]{0,2,3,1:T(8,128)(2,1)S(1)} %bitcast.59, bf16[512,2,2,128]{0,3,2,1:T(8,128)(2,1)S(1)} %bitcast.60), kind=kOutput, calls=%fused_computation.51 | convolution fusion | flops 824182272 | bytes 8396800 | tf_op jit(solution)/shard_map/sub | solution.py:99
  313.3 3.8 %fusion.18 = bf16[512,2,2,128]{0,3,2,1:T(8,128)(2,1)S(1)} fusion(bf16[1536,2,128,1]{0,2,3,1:T(8,128)(2,1)S(1)} %bitcast.58, bf16[2,2,512,1536]{2,3,1,0:T(8,128)(2,1)} %get-tuple-element.18, f32[512,2,2]{0,2,1:T(2,128)S(1)} %bitcast.62), kind=kOutput, calls=%fused_computation.20 | convolution fusion | flops 805830656 | bytes 7610368 | tf_op jit(solution)/shard_map/kgts,skd->tkgd/dot_general | solution.py:102
  317.1 8.6 %convolution_convert_fusion = bf16[512,5376]{0,1:T(8,128)(2,1)} fusion(bf16[512,512]{0,1:T(8,128)(2,1)S(1)} %bitcast.61, bf16[512,5376]{1,0:T(8,128)(2,1)} %param.15), kind=kOutput, calls=%fused_computation.9 | convolution fusion | flops 2821324800 | bytes 11534336 | tf_op jit(solution)/shard_map/dot_general | solution.py:107
  325.7 0.0 reduce-scatter.2.cloned.1.call-update
  325.7 41.5 %reduce-scatter.2.cloned.1.call-done = bf16[512,672]{0,1:T(8,128)(2,1)} async-done(((bf16[512,5376]{0,1:T(8,128)(2,1)}), bf16[512,672]{0,1:T(8,128)(2,1)}) %reduce-scatter.2.cloned.1.call-update) | async-done | bytes 688144 | tf_op jit(solution)/shard_map/reduce_scatter | solution.py:108
  (13 shorter events, 0.2 us)
Async XLA Ops:
  6.5 45.9 %all-gather.5.cloned.1.call-start = ((), (), s32[]{:S(2)}) async-start(), calls=%async_computation.1 | async-start | bytes 6193152 | tf_op jit(solution)/shard_map/all_gather | solution.py:50
  7.3 125.3 %all-gather.7.cloned.1.call-start = ((), (), s32[]{:S(2)}) async-start(), calls=%async_computation.2 | async-start | bytes 2838528 | tf_op jit(solution)/shard_map/all_gather | solution.py:60
  8.0 203.0 %all-gather.9.cloned.1.call-start = ((), (), s32[]{:S(2)}) async-start(), calls=%async_computation.3 | async-start | bytes 2838528 | tf_op jit(solution)/shard_map/all_gather | solution.py:61
  8.7 287.8 %all-gather.11.cloned.1.call-start = ((), (), s32[]{:S(2)}) async-start(), calls=%async_computation.4 | async-start | bytes 5677056 | tf_op jit(solution)/shard_map/all_gather | solution.py:59
  9.3 357.9 %reduce-scatter.2.cloned.1.call-start = ((), (), s32[]{:S(2)}) async-start(), calls=%async_computation.5 | async-start | bytes 6193152 | tf_op jit(solution)/shard_map/reduce_scatter | solution.py:108
  216.5 14.5 %collective-permute-start = (bf16[512,512]{0,1:T(8,128)(2,1)S(1)}, bf16[512,512]{0,1:T(8,128)(2,1)S(1)}, u32[]{:S(2)}, u32[]{:S(2)}) collective-permute-start(bf16[512,512]{0,1:T(8,128)(2,1)S(1)} %pad_maximum_fusion), channel_id=1, source_target_pairs={{0,8},{8,16},{16,24},{24,32},{32,40},{40,48},{48,56},{56,64},{64,7... | collective-permute-start | bytes 1572872 | tf_op jit(solution)/shard_map/ppermute | solution.py:18
  231.0 73.5 %collective-permute-start.1 = (bf16[512,512]{0,1:T(8,128)(2,1)S(1)}, bf16[512,512]{0,1:T(8,128)(2,1)S(1)}, u32[]{:S(2)}, u32[]{:S(2)}) collective-permute-start(bf16[512,512]{0,1:T(8,128)(2,1)S(1)} %collective-permute-done), channel_id=1, source_target_pairs={{0,8},{8,16},{16,24},{24,32},{32,40},{40,48},{48,56},{56,64},{64,7... | collective-permute-start | bytes 1572872 | tf_op jit(solution)/shard_map/ppermute | solution.py:18
Sparse Core Ops, SparseCore 0:
  9.2 43.1 all-gather.4
  55.0 77.5 all-gather.6
  135.2 75.7 all-gather.8
  213.4 83.0 all-gather.10
  325.9 41.3 reduce-scatter.1
where the time goes:
time: 374 us
  waiting for transfers between devices  278 us (74%)
  matrix products  39.4 us (11%)
  blocking collectives  27.5 us (7%)
  between operations  14 us (4%)
  other arithmetic  8.29 us (2%)
  starting transfers between devices  5.17 us (1%)
    all_gather x1, waiting for transfers between devices, local(): lax.all_gather(w_key, 'tok', axis=0, tiled=True)  76.4 us
    all_gather x1, waiting for transfers between devices, local(): lax.all_gather(value_matrix, 'tok', axis=0, tiled=True)  72.7 us
    all_gather x1, waiting for transfers between devices, local(): lax.all_gather(w_query, 'tok', axis=0, tiled=True)  63.4 us
    reduce_scatter x1, waiting for transfers between devices, local(): lax.psum_scatter(partial_value.astype(jnp.bfloat16), 'hid', scatter_dimen...  41.5 us
    unnamed x1, blocking collectives  27.5 us
    dot_general x3, matrix products, local(): jnp.dot(normed, piece, preferred_element_type=jnp.float32)  18.5 us
    all_gather x1, waiting for transfers between devices, local(): lax.all_gather(tokens, 'hid', axis=1, tiled=True)  10.7 us
    ppermute x2, waiting for transfers between devices, shifted(): lax.ppermute(value, axis, [(source, source + steps) for source in range(l...  10.4 us
  transfers between devices with their start and end apart: 7, of which 6 were waited for; matrix products, arithmetic and copies ran while one was open for 8% of the time, Pallas kernels for 0%

commit v1 on v0

--- a/solution.py
+++ b/solution.py
@@ -46,19 +46,21 @@
 
 def local(tokens, norm_gain, w_query, w_key, value_matrix, q_norm_gain, k_norm_gain, w_out):
     rows = tokens.shape[0]
-    gathered, gain_row = (
-        lax.all_gather(tokens, "hid", axis=1, tiled=True),
-        lax.all_gather(norm_gain, "hid", axis=1, tiled=True),
-    )
+    with_gain = jnp.concatenate([tokens, norm_gain], axis=0)
+    gathered_all = lax.all_gather(with_gain, "hid", axis=1, tiled=True)
+    gathered, gain_row = gathered_all[:rows], gathered_all[rows:]
     values32 = gathered.astype(jnp.float32)
     scale_rows = lax.rsqrt(jnp.mean(values32 * values32, axis=1, keepdims=True) + 1e-06)
     normed = (values32 * scale_rows * gain_row.astype(jnp.float32)).astype(jnp.bfloat16)
     width_query = w_query.shape[1]
     width_kv = w_key.shape[1]
+    stacked = lax.all_gather(
+        jnp.concatenate([w_query, w_key, value_matrix], axis=1), "tok", axis=0, tiled=True
+    )
     pieces = (
-        lax.all_gather(w_query, "tok", axis=0, tiled=True),
-        lax.all_gather(w_key, "tok", axis=0, tiled=True),
-        lax.all_gather(value_matrix, "tok", axis=0, tiled=True),
+        stacked[:, :width_query],
+        stacked[:, width_query : width_query + width_kv],
+        stacked[:, width_query + width_kv :],
     )
     query_raw, key_raw, value_raw = tuple(
         (jnp.dot(normed, piece, preferred_element_type=jnp.float32) for piece in pieces)

time: 374 us -> 282 us (0.75)
  waiting for transfers between devices: 278 us -> 194 us
  blocking collectives: 27.5 us -> 0 us
  local copies, waits for them, and re-layouts: 1.62 us -> 19.7 us
    all_gather x4 -> x2, waiting for transfers between devices: 223 us -> 132 us  [the longest x1 89.6 us: local(): lax.all_gather(jnp.concatenate([w_query, w_key, value_matrix], axis=1), '...]
    unnamed x1 -> x0, blocking collectives: 27.5 us -> none
    ppermute x2, waiting for transfers between devices: 10.4 us -> 22.6 us  [shifted(): lax.ppermute(value, axis, [(source, source + steps) for source in range(l...]
    unnamed x3 -> x6, local copies, waits for them, and re-layouts: 1.51 us -> 12.9 us
    all_gather x0 -> x1, local copies, waits for them, and re-layouts: none -> 6.7 us  [local(): gathered_all = lax.all_gather(with_gain, 'hid', axis=1, tiled=True)]
  transfers between devices with their start and end apart: 7 -> 5, of which waited for: 6 -> 5; matrix products, arithmetic and copies ran while one was open for 8% -> 12% of each run, Pallas kernels for 0% -> 0%
where the time goes in v1:
time: 282 us; the launch traced here: 281 us
  waiting for transfers between devices  194 us (69%)
  matrix products  38 us (13%)
  local copies, waits for them, and re-layouts  19.7 us (7%)
  between operations  13.3 us (5%)
  other arithmetic  11.9 us (4%)
  starting transfers between devices  4.1 us (1%)
    all_gather x1, waiting for transfers between devices, local(): lax.all_gather(jnp.concatenate([w_query, w_key, value_matrix], axis=1), '...  89.6 us
    all_gather x1, waiting for transfers between devices, local(): gathered_all = lax.all_gather(with_gain, 'hid', axis=1, tiled=True)  42 us
    reduce_scatter x1, waiting for transfers between devices, local(): lax.psum_scatter(partial_value.astype(jnp.bfloat16), 'hid', scatter_dimen...  39.8 us
    ppermute x2, waiting for transfers between devices, shifted(): lax.ppermute(value, axis, [(source, source + steps) for source in range(l...  22.6 us
    dot_general x3, matrix products, local(): jnp.dot(normed, piece, preferred_element_type=jnp.float32)  17.1 us
    unnamed x6, local copies, waits for them, and re-layouts  12.9 us
    dot_general x1, matrix products, local(): jnp.dot(heads_out, w_out, preferred_element_type=jnp.float32)  8.65 us
    sub x1, matrix products, local(): weights = jnp.where(allowed, jnp.exp(masked - top), 0.0)  8.48 us
  transfers between devices with their start and end apart: 5, of which 5 were waited for; matrix products, arithmetic and copies ran while one was open for 12% of the time, Pallas kernels for 0%

profile of v1, /device:TPU:2, one launch (start us, length us, event | category | flops | bytes accessed | tf_op | source)
XLA Modules:
  0.0 281.1 jit_solution(15965391210399001343)
XLA Ops:
  6.5 0.0 all-gather.6.cloned.1.call-start
  6.5 1.4 copy.22
  7.9 1.7 maximum_bitcast_fusion
  9.6 0.0 all-gather.6.cloned.1.call-update
  9.6 0.0 all-gather.4.cloned.1.call-start
  9.6 1.8 pad_maximum_fusion.2
  11.4 0.0 all-gather.4.cloned.1.call-update
  11.4 0.0 reduce-scatter.2.cloned.1.call-start
  11.6 0.7 bitcast_convert_fusion
  12.2 0.7 bitcast_convert_fusion.1
  12.9 0.5 multiply_cosine_fusion
  13.4 1.1 and_and_fusion
  14.6 42.0 %all-gather.6.cloned.1.call-done = bf16[8,672,513]{1,2,0:T(8,128)(2,1)} async-done(((bf16[1,672,513]{1,2,0:T(8,128)(2,1)}), bf16[8,672,513]{1,2,0:T(8,128)(2,1)}) %all-gather.6.cloned.1.call-update) | async-done | bytes 5515792 | tf_op jit(solution)/shard_map/all_gather | solution.py:50
  56.5 6.7 %copy.23 = bf16[8,672,513]{1,0,2:T(8,128)(2,1)} copy(bf16[8,672,513]{1,2,0:T(8,128)(2,1)} %all-gather.6.cloned.1.call-done) | data formatting | bytes 11031552 | tf_op jit(solution)/shard_map/all_gather | solution.py:50
  63.2 11.6 %reshape.129 = bf16[5376,513]{0,1:T(8,128)(2,1)} reshape(bf16[8,672,513]{1,0,2:T(8,128)(2,1)} %copy.23) | data formatting | bytes 11031552
  74.8 0.9 fusion.30
  75.7 3.7 %fusion.1 = f32[512]{0:T(512)S(1)} fusion(bf16[513,5376]{1,0:T(8,128)(2,1)} %bitcast.60), kind=kLoop, calls=%fused_computation.5 | loop fusion | flops 8257024 | bytes 5507072 | tf_op jit(solution)/shard_map/reduce_sum | solution.py:53
  79.5 89.6 %all-gather.4.cloned.1.call-done = bf16[5376,1024]{1,0:T(8,128)(2,1)} async-done(((bf16[168,1024]{1,0:T(8,128)(2,1)}), bf16[5376,1024]{1,0:T(8,128)(2,1)}) %all-gather.4.cloned.1.call-update) | async-done | bytes 11010064 | tf_op jit(solution)/shard_map/all_gather | solution.py:57
  169.1 5.8 %multiply_reduce_fusion.1 = (f32[512,2]{0,1:T(2,128)S(1)}, f32[512,256]{0,1:T(8,128)S(1)}) fusion(bf16[5376,1024]{1,0:T(8,128)(2,1)} %all-gather.4.cloned.1.call-done, f32[5376]{0:T(1024)S(1)} %fusion.30, f32[512]{0:T(512)S(1)} %add_rsqrt_fusion.2, bf16[513,5376]{1,0:T(8,128)(2,1)} %bitcast.61), kind=kOutput, calls=%fused_computation.36 | convolution fusion | flops 1420557312 | bytes 8809472 | tf_op jit(solution)/shard_map/dot_general | solution.py:66
  174.9 0.1 multiply_multiply_fusion.1
  175.0 0.1 subtract_convert_fusion.1
  175.1 0.0 slice-start
  175.1 0.0 slice-start.1
  175.1 5.5 %fusion.27 = bf16[512,256]{0,1:T(8,128)(2,1)S(1)} fusion(bf16[5376,1024]{1,0:T(8,128)(2,1)} %all-gather.4.cloned.1.call-done, f32[5376]{0:T(1024)S(1)} %fusion.30, f32[512]{0:T(512)S(1)} %add_rsqrt_fusion.2, bf16[513,5376]{1,0:T(8,128)(2,1)} %bitcast.62), kind=kOutput, calls=%fused_computation.27 | convolution fusion | flops 1420427264 | bytes 8543232 | tf_op jit(solution)/shard_map/dot_general | solution.py:66
  180.7 2.1 collective-permute-start
  182.8 0.0 slice-done
  182.8 0.0 slice-done.1
  182.8 5.9 %multiply_reduce_fusion = (f32[512,4]{0,1:T(4,128)S(1)}, f32[512,512]{0,1:T(8,128)S(1)}) fusion(bf16[5376,1024]{1,0:T(8,128)(2,1)} %all-gather.4.cloned.1.call-done, f32[5376]{0:T(1024)S(1)} %fusion.30, f32[512]{0:T(512)S(1)} %add_rsqrt_fusion.2, bf16[513,5376]{1,0:T(8,128)(2,1)S(1)} %bitcast.65), kind=kOutput, calls=%fused_computation.29 | convolution fusion | flops 2830104576 | bytes 12093440 | tf_op jit(solution)/shard_map/dot_general | solution.py:66
  188.7 8.9 %collective-permute-done = bf16[512,512]{0,1:T(8,128)(2,1)S(1)} collective-permute-done((bf16[512,512]{0,1:T(8,128)(2,1)S(1)}, bf16[512,512]{0,1:T(8,128)(2,1)S(1)}, u32[]{:S(2)}, u32[]{:S(2)}) %collective-permute-start) | collective-permute-done | bytes 524320 | tf_op jit(solution)/shard_map/ppermute | solution.py:18
  197.6 1.9 collective-permute-start.1
  199.5 0.2 multiply_multiply_fusion
  199.7 0.2 subtract_convert_fusion
  200.0 13.7 %collective-permute-done.1 = bf16[512,512]{0,1:T(8,128)(2,1)S(1)} collective-permute-done((bf16[512,512]{0,1:T(8,128)(2,1)S(1)}, bf16[512,512]{0,1:T(8,128)(2,1)S(1)}, u32[]{:S(2)}, u32[]{:S(2)}) %collective-permute-start.1) | collective-permute-done | bytes 524320 | tf_op jit(solution)/shard_map/ppermute | solution.py:18
  213.7 0.1 maximum_maximum_fusion
  213.8 0.1 fusion.38
  213.9 8.5 %fusion.39 = (f32[2,2,512]{2,1,0:T(2,128)S(1)}, bf16[2,2,512,1536]{2,3,1,0:T(8,128)(2,1)}) fusion(pred[512,1536]{0,1:T(8,128)(4,1)S(1)} %and_and_fusion, bf16[1536,2,128,1]{0,2,3,1:T(8,128)(2,1)S(1)} %bitcast.69, bf16[512,2,2,128]{0,3,2,1:T(8,128)(2,1)S(1)} %bitcast.70), kind=kOutput, calls=%fused_computation.59 | convolution fusion | flops 824182272 | bytes 8396800 | tf_op jit(solution)/shard_map/sub | solution.py:101
  222.4 3.8 %fusion.24 = bf16[512,2,2,128]{0,3,2,1:T(8,128)(2,1)S(1)} fusion(bf16[1536,2,128,1]{0,2,3,1:T(8,128)(2,1)S(1)} %bitcast.68, bf16[2,2,512,1536]{2,3,1,0:T(8,128)(2,1)} %get-tuple-element.18, f32[512,2,2]{0,2,1:T(2,128)S(1)} %bitcast.72), kind=kOutput, calls=%fused_computation.26 | convolution fusion | flops 805830656 | bytes 7610368 | tf_op jit(solution)/shard_map/kgts,skd->tkgd/dot_general | solution.py:104
  226.2 8.6 %convolution_convert_fusion = bf16[512,5376]{0,1:T(8,128)(2,1)} fusion(bf16[512,512]{0,1:T(8,128)(2,1)S(1)} %bitcast.71, bf16[512,5376]{1,0:T(8,128)(2,1)} %param.15), kind=kOutput, calls=%fused_computation.9 | convolution fusion | flops 2821324800 | bytes 11534336 | tf_op jit(solution)/shard_map/dot_general | solution.py:109
  234.8 0.0 reduce-scatter.2.cloned.1.call-update
  234.8 39.8 %reduce-scatter.2.cloned.1.call-done = bf16[512,672]{0,1:T(8,128)(2,1)} async-done(((bf16[512,5376]{0,1:T(8,128)(2,1)}), bf16[512,672]{0,1:T(8,128)(2,1)}) %reduce-scatter.2.cloned.1.call-update) | async-done | bytes 688144 | tf_op jit(solution)/shard_map/reduce_scatter | solution.py:110
  (12 shorter events, 0.2 us)
Async XLA Ops:
  6.5 50.0 %all-gather.6.cloned.1.call-start = ((), (), s32[]{:S(2)}) async-start(), calls=%async_computation.3 | async-start | bytes 7188480 | tf_op jit(solution)/shard_map/all_gather | solution.py:50
  9.6 159.5 %all-gather.4.cloned.1.call-start = ((), (), s32[]{:S(2)}) async-start(), calls=%async_computation.1 | async-start | bytes 11354112 | tf_op jit(solution)/shard_map/all_gather | solution.py:57
  11.4 263.2 %reduce-scatter.2.cloned.1.call-start = ((), (), s32[]{:S(2)}) async-start(), calls=%async_computation.2 | async-start | bytes 6193152 | tf_op jit(solution)/shard_map/reduce_scatter | solution.py:110
  175.1 7.7 %slice-start = ((s8[5591040]{0:T(1024)(128)(4,1)}), s8[4194304]{0:T(1024)(128)(4,1)S(1)}, s32[]{:S(2)}) async-start(s8[5591040]{0:T(1024)(128)(4,1)} %bitcast.63), calls=%async_computation.4 | async-start | bytes 8388608
  175.1 7.7 %slice-start.1 = ((s8[5591040]{0:T(1024)(128)(4,1)}), s8[1396736]{0:T(1024)(128)(4,1)S(1)}, s32[]{:S(2)}) async-start(s8[5591040]{0:T(1024)(128)(4,1)} %bitcast.63), calls=%async_computation.5 | async-start | bytes 2793472
  180.7 16.9 %collective-permute-start = (bf16[512,512]{0,1:T(8,128)(2,1)S(1)}, bf16[512,512]{0,1:T(8,128)(2,1)S(1)}, u32[]{:S(2)}, u32[]{:S(2)}) collective-permute-start(bf16[512,512]{0,1:T(8,128)(2,1)S(1)} %pad_maximum_fusion), channel_id=1, source_target_pairs={{0,8},{8,16},{16,24},{24,32},{32,40},{40,48},{48,56},{56,64},{64,7... | collective-permute-start | bytes 1572872 | tf_op jit(solution)/shard_map/ppermute | solution.py:18
  197.6 16.1 %collective-permute-start.1 = (bf16[512,512]{0,1:T(8,128)(2,1)S(1)}, bf16[512,512]{0,1:T(8,128)(2,1)S(1)}, u32[]{:S(2)}, u32[]{:S(2)}) collective-permute-start(bf16[512,512]{0,1:T(8,128)(2,1)S(1)} %collective-permute-done), channel_id=1, source_target_pairs={{0,8},{8,16},{16,24},{24,32},{32,40},{40,48},{48,56},{56,64},{64,7... | collective-permute-start | bytes 1572872 | tf_op jit(solution)/shard_map/ppermute | solution.py:18
Sparse Core Ops, SparseCore 0:
  9.7 46.7 all-gather.5
  59.1 109.9 all-gather.3
  235.0 39.6 reduce-scatter.1

commit v2 on v1

--- a/solution.py
+++ b/solution.py
@@ -47,7 +47,15 @@
 def local(tokens, norm_gain, w_query, w_key, value_matrix, q_norm_gain, k_norm_gain, w_out):
     rows = tokens.shape[0]
     with_gain = jnp.concatenate([tokens, norm_gain], axis=0)
-    gathered_all = lax.all_gather(with_gain, "hid", axis=1, tiled=True)
+    n_hid = lax.axis_size("hid")
+    hid_index = lax.axis_index("hid")
+    received = [with_gain] + [
+        lax.ppermute(with_gain, "hid", [(i, (i + k) % n_hid) for i in range(n_hid)])
+        for k in range(1, n_hid)
+    ]
+    by_shift = jnp.stack(received)
+    ordered = jnp.take(by_shift, (hid_index - jnp.arange(n_hid)) % n_hid, axis=0)
+    gathered_all = jnp.transpose(ordered, (1, 0, 2)).reshape(rows + 1, -1)
     gathered, gain_row = gathered_all[:rows], gathered_all[rows:]
     values32 = gathered.astype(jnp.float32)
     scale_rows = lax.rsqrt(jnp.mean(values32 * values32, axis=1, keepdims=True) + 1e-06)
@@ -72,11 +80,7 @@
     value_rows = value_raw.astype(jnp.bfloat16)
     joined = jnp.concatenate([key, value_rows], axis=1)
     reach = (WINDOW - 1 + rows - 1) // rows
-    earlier = []
-    moving = joined
-    for offset in range(reach):
-        moving = shifted(moving, "tok", 1)
-        earlier = [moving] + earlier
+    earlier = [shifted(joined, "tok", offset) for offset in range(reach, 0, -1)]
     window_kv = jnp.concatenate(earlier + [joined], axis=0)
     window_extent = window_kv.shape[0]
     key_pos = (tok_index - reach) * rows + jnp.arange(window_extent, dtype=jnp.int32)

time: 282 us -> 275 us (0.975)
  waiting for transfers between devices: 194 us -> 91.4 us
  local copies, waits for them, and re-layouts: 19.7 us -> 59.5 us
  starting transfers between devices: 4.1 us -> 33.3 us
  other arithmetic: 11.9 us -> 38.7 us
    all_gather x1, waiting for transfers between devices: 89.6 us -> 0.01 us  [local(): lax.all_gather(jnp.concatenate([w_query, w_key, value_matrix], axis=1), '...]
    all_gather x1 -> x0, waiting for transfers between devices: 42 us -> none  [local(): gathered_all = lax.all_gather(with_gain, 'hid', axis=1, tiled=True)]
    ppermute x0 -> x7, waiting for transfers between devices: none -> 32.8 us  [local(): lax.ppermute(with_gain, 'hid', [(i, (i + k) % n_hid) for i in range(n_hid)])]
    ppermute x0 -> x7, starting transfers between devices: none -> 24.1 us  [local(): lax.ppermute(with_gain, 'hid', [(i, (i + k) % n_hid) for i in range(n_hid)])]
    convert_element_type x0 -> x5, other arithmetic: none -> 20.7 us  [the longest x2 13 us: local(): (values32 * scale_rows * gain_row.astype(jnp.float32)).astype(jnp.bfloat16)]
    convert_element_type x0 -> x3, local copies, waits for them, and re-layouts: none -> 20.4 us  [the longest x1 12 us: local(): values32 = gathered.astype(jnp.float32)]
    ppermute x2, waiting for transfers between devices: 22.6 us -> 5.77 us  [shifted(): lax.ppermute(value, axis, [(source, source + steps) for source in range(l...]
    dot_general x0 -> x4, local copies, waits for them, and re-layouts: none -> 16.3 us  [local(): jnp.dot(normed, piece, preferred_element_type=jnp.float32)]
  transfers between devices with their start and end apart: 5 -> 11, of which waited for: 5 -> 6; matrix products, arithmetic and copies ran while one was open for 12% -> 34% of each run, Pallas kernels for 0% -> 0%
where the time goes in v2:
time: 275 us; the launch traced here: 274 us
  waiting for transfers between devices  91.4 us (33%)
  local copies, waits for them, and re-layouts  59.5 us (22%)
  other arithmetic  38.7 us (14%)
  matrix products  36.8 us (13%)
  starting transfers between devices  33.3 us (12%)
  between operations  13.7 us (5%)
    reduce_scatter x1, waiting for transfers between devices, local(): lax.psum_scatter(partial_value.astype(jnp.bfloat16), 'hid', scatter_dimen...  52.8 us
    ppermute x7, waiting for transfers between devices, local(): lax.ppermute(with_gain, 'hid', [(i, (i + k) % n_hid) for i in range(n_hid)])  32.8 us
    ppermute x7, starting transfers between devices, local(): lax.ppermute(with_gain, 'hid', [(i, (i + k) % n_hid) for i in range(n_hid)])  24.1 us
    dot_general x4, local copies, waits for them, and re-layouts, local(): jnp.dot(normed, piece, preferred_element_type=jnp.float32)  16.3 us
    dot_general x3, matrix products, local(): jnp.dot(normed, piece, preferred_element_type=jnp.float32)  16 us
    unnamed x16, local copies, waits for them, and re-layouts  15.4 us
    convert_element_type x2, other arithmetic, local(): (values32 * scale_rows * gain_row.astype(jnp.float32)).astype(jnp.bfloat16)  13 us
    convert_element_type x1, local copies, waits for them, and re-layouts, local(): values32 = gathered.astype(jnp.float32)  12 us
  transfers between devices with their start and end apart: 11, of which 6 were waited for; matrix products, arithmetic and copies ran while one was open for 34% of the time, Pallas kernels for 0%

profile of v2, /device:TPU:2, one launch (start us, length us, event | category | flops | bytes accessed | tf_op | source)
XLA Modules:
  0.0 273.5 jit_solution(17270343113919855901)
XLA Ops:
  6.5 1.8 pad_maximum_fusion.3
  8.4 1.4 copy.23
  9.8 0.8 pad_maximum_fusion
  10.6 1.7 collective-permute-start.1
  12.2 2.2 collective-permute-start.2
  14.4 1.8 collective-permute-start.3
  16.3 1.8 collective-permute-start.4
  18.7 1.9 and_and_fusion
  21.9 1.7 bitcast_dynamic-update-slice_fusion.7
  23.6 7.7 %collective-permute-done = bf16[513,672]{1,0:T(8,128)(2,1)} collective-permute-done((bf16[513,672]{1,0:T(8,128)(2,1)S(1)}, bf16[513,672]{1,0:T(8,128)(2,1)}, u32[]{:S(2)}, u32[]{:S(2)}) %collective-permute-start) | collective-permute-done | bytes 689504 | tf_op jit(solution)/shard_map/ppermute | solution.py:53
  31.3 1.8 collective-permute-start.5
  33.1 2.1 bitcast_dynamic-update-slice_fusion.6
  35.2 14.7 %collective-permute-start.6 = (bf16[513,672]{1,0:T(8,128)(2,1)S(1)}, bf16[513,672]{1,0:T(8,128)(2,1)S(1)}, u32[]{:S(2)}, u32[]{:S(2)}) collective-permute-start(bf16[513,672]{1,0:T(8,128)(2,1)S(1)} %pad_maximum_fusion), channel_id=1, source_target_pairs={{0,7},{1,0},{2,1},{3,2},{4,3},{5,4},{6,5},{7,6},{8,15},{9,8},{10,9... | collective-permute-start | bytes 2068424 | tf_op jit(solution)/shard_map/ppermute | solution.py:53
  49.9 2.1 bitcast_dynamic-update-slice_fusion.5
  52.0 14.8 %collective-permute-done.2 = bf16[513,672]{1,0:T(8,128)(2,1)} collective-permute-done((bf16[513,672]{1,0:T(8,128)(2,1)S(1)}, bf16[513,672]{1,0:T(8,128)(2,1)}, u32[]{:S(2)}, u32[]{:S(2)}) %collective-permute-start.2) | collective-permute-done | bytes 689504 | tf_op jit(solution)/shard_map/ppermute | solution.py:53
  66.8 2.1 bitcast_dynamic-update-slice_fusion.4
  68.8 2.1 bitcast_dynamic-update-slice_fusion.3
  70.9 10.2 %collective-permute-done.4 = bf16[513,672]{1,0:T(8,128)(2,1)S(1)} collective-permute-done((bf16[513,672]{1,0:T(8,128)(2,1)S(1)}, bf16[513,672]{1,0:T(8,128)(2,1)S(1)}, u32[]{:S(2)}, u32[]{:S(2)}) %collective-permute-start.4) | collective-permute-done | bytes 689504 | tf_op jit(solution)/shard_map/ppermute | solution.py:53
  81.1 0.9 bitcast_dynamic-update-slice_fusion.2
  82.1 1.0 bitcast_dynamic-update-slice_fusion.1
  83.1 0.9 bitcast_dynamic-update-slice_fusion
  84.1 6.5 %gather_fusion = bf16[8,513,672]{2,1,0:T(8,128)(2,1)} fusion(bf16[8,513,672]{2,1,0:T(8,128)(2,1)} %bitcast_dynamic-update-slice_fusion, s32[1024]{0:T(1024)S(1)} %pad_clamp_fusion), kind=kCustom, calls=%fused_computation | custom fusion | bytes 11031584 | tf_op jit(solution)/shard_map/jit(_take)/gather | solution.py:57
  90.6 3.7 %select_bitcast_fusion = bf16[513,8,672]{2,0,1:T(8,128)(2,1)S(1)} fusion(bf16[8,513,672]{2,1,0:T(8,128)(2,1)} %gather_fusion, pred[8]{0:T(512)(128)(4,1)S(1)} %compare_and_fusion), kind=kLoop, calls=%fused_computation.11 | loop fusion | flops 2757888 | bytes 11031560 | tf_op jit(solution)/shard_map/jit(_take)/select_n | solution.py:57
  94.3 2.6 copy-done
  96.9 5.7 %slice_convert_fusion = f32[512,8,672]{2,0,1:T(8,128)} fusion(bf16[513,8,672]{2,0,1:T(8,128)(2,1)S(1)} %select_bitcast_fusion), kind=kLoop, calls=%fused_computation.12 | loop fusion | flops 2752512 | bytes 16515072 | tf_op jit(solution)/shard_map/convert_element_type | solution.py:60
  102.5 12.0 %copy.27 = f32[512,8,672]{0,2,1:T(8,128)} copy(f32[512,8,672]{2,0,1:T(8,128)} %slice_convert_fusion) | data formatting | bytes 22020096 | tf_op jit(solution)/shard_map/convert_element_type | solution.py:60
  114.6 1.0 fusion.32
  115.6 1.1 slice_convert_fusion.1
  116.7 4.4 %multiply_reduce_fusion = f32[512]{0:T(512)S(1)} fusion(bf16[513,8,672]{2,0,1:T(8,128)(2,1)} %copy-done), kind=kLoop, calls=%fused_computation.5 | loop fusion | flops 8257024 | bytes 5507072 | tf_op jit(solution)/shard_map/reduce_sum | solution.py:61
  121.1 4.7 %multiply_convert_fusion = bf16[512,8,672]{2,0,1:T(8,128)(2,1)} fusion(f32[8,672]{1,0:T(8,128)S(1)} %bitcast.98, f32[512]{0:T(512)S(1)} %add_rsqrt_fusion.2, bf16[513,8,672]{2,0,1:T(8,128)(2,1)S(1)} %copy-done.1), kind=kLoop, calls=%fused_computation.4 | loop fusion | flops 11010048 | bytes 11033600 | tf_op jit(solution)/shard_map/convert_element_type | solution.py:62
  125.8 8.3 %copy.24 = bf16[512,8,672]{0,2,1:T(8,128)(2,1)} copy(bf16[512,8,672]{2,0,1:T(8,128)(2,1)} %multiply_convert_fusion) | data formatting | bytes 11010048 | tf_op jit(solution)/shard_map/convert_element_type | solution.py:62
  134.1 8.3 %fusion.2 = bf16[512,5376]{0,1:T(8,128)(2,1)} fusion(f32[512,8,672]{0,2,1:T(8,128)} %copy.27, f32[5376]{0:T(1024)S(1)} %reshape.217, f32[512]{0:T(512)S(1)} %add_rsqrt_fusion.2), kind=kLoop, calls=%fused_computation.8 | loop fusion | flops 8257536 | bytes 16538624 | tf_op jit(solution)/shard_map/convert_element_type | solution.py:62
  142.4 2.0 slice_bitcast_fusion.1
  144.3 3.0 %copy.25 = bf16[256,5376]{1,0:T(8,128)(2,1)} copy(bf16[256,5376]{0,1:T(8,128)(2,1)S(1)} %slice_bitcast_fusion.1) | data formatting | bytes 5505024 | tf_op jit(solution)/shard_map/dot_general | solution.py:74
  147.4 5.1 %multiply_reduce_fusion.2 = (f32[512,2]{0,1:T(2,128)S(1)}, f32[512,2,128]{0,2,1:T(8,128)S(1)}) fusion(bf16[512,5376,1]{0,1,2:T(8,128)(2,1)} %bitcast.89, bf16[2,128,5376]{2,1,0:T(8,128)(2,1)} %bitcast.92), kind=kOutput, calls=%fused_computation.45 | convolution fusion | flops 1409547264 | bytes 8785920 | tf_op jit(solution)/shard_map/dot_general | solution.py:74
  152.7 1.1 copy-done.2
  153.9 4.2 %fusion.22 = bf16[512,256]{0,1:T(8,128)(2,1)S(1)} fusion(bf16[512,5376]{0,1:T(8,128)(2,1)} %fusion.2, bf16[5376,1024]{1,0:T(8,128)(2,1)S(1)} %copy-done.2), kind=kOutput, calls=%fused_computation.28 | convolution fusion | flops 1409417216 | bytes 8519680 | tf_op jit(solution)/shard_map/dot_general | solution.py:74
  158.1 3.7 %collective-permute-start.8 = (bf16[512,512]{0,1:T(8,128)(2,1)S(1)}, bf16[512,512]{0,1:T(8,128)(2,1)}, u32[]{:S(2)}, u32[]{:S(2)}) collective-permute-start(bf16[512,512]{0,1:T(8,128)(2,1)S(1)} %pad_maximum_fusion.1), channel_id=1, source_target_pairs={{0,8},{8,16},{16,24},{24,32},{32,40},{40,48},{48,56},{56,64},{64,7... | collective-permute-start | bytes 1572872 | tf_op jit(solution)/shard_map/ppermute | solution.py:18
  161.8 5.5 %collective-permute-start.7 = (bf16[512,512]{0,1:T(8,128)(2,1)S(1)}, bf16[512,512]{0,1:T(8,128)(2,1)}, u32[]{:S(2)}, u32[]{:S(2)}) collective-permute-start(bf16[512,512]{0,1:T(8,128)(2,1)S(1)} %pad_maximum_fusion.1), channel_id=1, source_target_pairs={{0,16},{8,24},{16,32},{24,40},{32,48},{40,56},{48,64},{56,72},{64,... | collective-permute-start | bytes 1572872 | tf_op jit(solution)/shard_map/ppermute | solution.py:18
  167.3 3.1 %slice_bitcast_fusion = bf16[512,5376]{0,1:T(8,128)(2,1)} fusion(bf16[5376,1024]{1,0:T(8,128)(2,1)S(1)} %copy-done.2), kind=kLoop, calls=%fused_computation.18 | loop fusion | bytes 11010048 | tf_op jit(solution)/shard_map/dot_general | solution.py:74
  170.4 8.3 %copy.28 = bf16[512,5376]{1,0:T(8,128)(2,1)} copy(bf16[512,5376]{0,1:T(8,128)(2,1)} %slice_bitcast_fusion) | data formatting | bytes 11010048 | tf_op jit(solution)/shard_map/dot_general | solution.py:74
  178.7 6.6 %multiply_reduce_fusion.1 = (f32[512,4]{0,1:T(4,128)S(1)}, f32[512,4,128]{0,2,1:T(8,128)S(1)}) fusion(bf16[512,5376,1]{0,1,2:T(8,128)(2,1)} %bitcast.90, bf16[4,128,5376]{2,1,0:T(8,128)(2,1)} %bitcast.91), kind=kOutput, calls=%fused_computation.30 | convolution fusion | flops 2819094528 | bytes 12066816 | tf_op jit(solution)/shard_map/dot_general | solution.py:74
  185.7 5.8 %collective-permute-done.7 = bf16[512,512]{0,1:T(8,128)(2,1)} collective-permute-done((bf16[512,512]{0,1:T(8,128)(2,1)S(1)}, bf16[512,512]{0,1:T(8,128)(2,1)}, u32[]{:S(2)}, u32[]{:S(2)}) %collective-permute-start.7) | collective-permute-done | bytes 524320 | tf_op jit(solution)/shard_map/ppermute | solution.py:18
  191.5 1.3 maximum_maximum_fusion
  192.9 8.5 %fusion.34 = (f32[2,2,512]{2,1,0:T(2,128)S(1)}, bf16[2,2,512,1536]{2,3,1,0:T(8,128)(2,1)}) fusion(pred[512,1536]{0,1:T(8,128)(4,1)S(1)} %copy-done.3, bf16[1536,2,128,1]{0,2,3,1:T(8,128)(2,1)S(1)} %bitcast.96, bf16[512,2,2,128]{0,3,2,1:T(8,128)(2,1)S(1)} %bitcast.97), kind=kOutput, calls=%fused_computation.82 | convolution fusion | flops 824182272 | bytes 8396800 | tf_op jit(solution)/shard_map/sub | solution.py:105
  201.4 3.8 %fusion.19 = bf16[512,2,2,128]{0,3,2,1:T(8,128)(2,1)S(1)} fusion(bf16[1536,2,128,1]{0,2,3,1:T(8,128)(2,1)S(1)} %bitcast.95, bf16[2,2,512,1536]{2,3,1,0:T(8,128)(2,1)} %get-tuple-element.18, f32[512,2,2]{0,2,1:T(2,128)S(1)} %bitcast.100), kind=kOutput, calls=%fused_computation.27 | convolution fusion | flops 805830656 | bytes 7610368 | tf_op jit(solution)/shard_map/kgts,skd->tkgd/dot_general | solution.py:108
  205.2 8.6 %convolution_convert_fusion = bf16[512,5376]{0,1:T(8,128)(2,1)} fusion(bf16[512,512]{0,1:T(8,128)(2,1)S(1)} %bitcast.99, bf16[512,5376]{1,0:T(8,128)(2,1)} %param.15), kind=kOutput, calls=%fused_computation.10 | convolution fusion | flops 2821324800 | bytes 11534336 | tf_op jit(solution)/shard_map/dot_general | solution.py:113
  213.9 52.8 %reduce-scatter.2.cloned.1.call-done = bf16[512,672]{0,1:T(8,128)(2,1)} async-done(((bf16[512,5376]{0,1:T(8,128)(2,1)}), bf16[512,672]{0,1:T(8,128)(2,1)}) %reduce-scatter.2.cloned.1.call-update) | async-done | bytes 688144 | tf_op jit(solution)/shard_map/reduce_scatter | solution.py:114
  (41 shorter events, 3.0 us)
Async XLA Ops:
  6.5 135.9 %all-gather.2.cloned.1.call-start = ((), (), s32[]{:S(2)}) async-start(), calls=%async_computation.1 | async-start | bytes 11354112 | tf_op jit(solution)/shard_map/all_gather | solution.py:65
  8.3 258.3 %reduce-scatter.2.cloned.1.call-start = ((), (), s32[]{:S(2)}) async-start(), calls=%async_computation.2 | async-start | bytes 6193152 | tf_op jit(solution)/shard_map/reduce_scatter | solution.py:114
  10.5 20.8 %collective-permute-start = (bf16[513,672]{1,0:T(8,128)(2,1)S(1)}, bf16[513,672]{1,0:T(8,128)(2,1)}, u32[]{:S(2)}, u32[]{:S(2)}) collective-permute-start(bf16[513,672]{1,0:T(8,128)(2,1)S(1)} %pad_maximum_fusion), channel_id=1, source_target_pairs={{0,1},{1,2},{2,3},{3,4},{4,5},{5,6},{6,7},{7,0},{8,9},{9,10},{10,1... | collective-permute-start | bytes 2068424 | tf_op jit(solution)/shard_map/ppermute | solution.py:53
  10.6 24.6 %collective-permute-start.1 = (bf16[513,672]{1,0:T(8,128)(2,1)S(1)}, bf16[513,672]{1,0:T(8,128)(2,1)}, u32[]{:S(2)}, u32[]{:S(2)}) collective-permute-start(bf16[513,672]{1,0:T(8,128)(2,1)S(1)} %pad_maximum_fusion), channel_id=1, source_target_pairs={{0,2},{1,3},{2,4},{3,5},{4,6},{5,7},{6,0},{7,1},{8,10},{9,11},{10,... | collective-permute-start | bytes 2068424 | tf_op jit(solution)/shard_map/ppermute | solution.py:53
  12.2 54.6 %collective-permute-start.2 = (bf16[513,672]{1,0:T(8,128)(2,1)S(1)}, bf16[513,672]{1,0:T(8,128)(2,1)}, u32[]{:S(2)}, u32[]{:S(2)}) collective-permute-start(bf16[513,672]{1,0:T(8,128)(2,1)S(1)} %pad_maximum_fusion), channel_id=1, source_target_pairs={{0,3},{1,4},{2,5},{3,6},{4,7},{5,0},{6,1},{7,2},{8,11},{9,12},{10,... | collective-permute-start | bytes 2068424 | tf_op jit(solution)/shard_map/ppermute | solution.py:53
  14.4 54.4 %collective-permute-start.3 = (bf16[513,672]{1,0:T(8,128)(2,1)S(1)}, bf16[513,672]{1,0:T(8,128)(2,1)}, u32[]{:S(2)}, u32[]{:S(2)}) collective-permute-start(bf16[513,672]{1,0:T(8,128)(2,1)S(1)} %pad_maximum_fusion), channel_id=1, source_target_pairs={{0,4},{1,5},{2,6},{3,7},{4,0},{5,1},{6,2},{7,3},{8,12},{9,13},{10,... | collective-permute-start | bytes 2068424 | tf_op jit(solution)/shard_map/ppermute | solution.py:53
  16.3 64.9 %collective-permute-start.4 = (bf16[513,672]{1,0:T(8,128)(2,1)S(1)}, bf16[513,672]{1,0:T(8,128)(2,1)S(1)}, u32[]{:S(2)}, u32[]{:S(2)}) collective-permute-start(bf16[513,672]{1,0:T(8,128)(2,1)S(1)} %pad_maximum_fusion), channel_id=1, source_target_pairs={{0,5},{1,6},{2,7},{3,0},{4,1},{5,2},{6,3},{7,4},{8,13},{9,14},{10,... | collective-permute-start | bytes 2068424 | tf_op jit(solution)/shard_map/ppermute | solution.py:53
  31.3 50.8 %collective-permute-start.5 = (bf16[513,672]{1,0:T(8,128)(2,1)S(1)}, bf16[513,672]{1,0:T(8,128)(2,1)S(1)}, u32[]{:S(2)}, u32[]{:S(2)}) collective-permute-start(bf16[513,672]{1,0:T(8,128)(2,1)S(1)} %pad_maximum_fusion), channel_id=1, source_target_pairs={{0,6},{1,7},{2,0},{3,1},{4,2},{5,3},{6,4},{7,5},{8,14},{9,15},{10,... | collective-permute-start | bytes 2068424 | tf_op jit(solution)/shard_map/ppermute | solution.py:53
  35.2 47.9 %collective-permute-start.6 = (bf16[513,672]{1,0:T(8,128)(2,1)S(1)}, bf16[513,672]{1,0:T(8,128)(2,1)S(1)}, u32[]{:S(2)}, u32[]{:S(2)}) collective-permute-start(bf16[513,672]{1,0:T(8,128)(2,1)S(1)} %pad_maximum_fusion), channel_id=1, source_target_pairs={{0,7},{1,0},{2,1},{3,2},{4,3},{5,4},{6,5},{7,6},{8,15},{9,8},{10,9... | collective-permute-start | bytes 2068424 | tf_op jit(solution)/shard_map/ppermute | solution.py:53
  94.3 2.6 copy-start
  115.6 5.5 %copy-start.1 = (bf16[513,8,672]{2,0,1:T(8,128)(2,1)S(1)}, bf16[513,8,672]{2,0,1:T(8,128)(2,1)}, u32[]{:S(2)}) copy-start(bf16[513,8,672]{2,0,1:T(8,128)(2,1)} %copy-done) | copy-start | bytes 16547332
  147.3 6.5 %copy-start.2 = (bf16[5376,1024]{1,0:T(8,128)(2,1)S(1)}, bf16[5376,1024]{1,0:T(8,128)(2,1)}, u32[]{:S(2)}) copy-start(bf16[5376,1024]{1,0:T(8,128)(2,1)} %all-gather.2.cloned.1.call-done) | copy-start | bytes 33030148
  158.1 27.6 %collective-permute-start.8 = (bf16[512,512]{0,1:T(8,128)(2,1)S(1)}, bf16[512,512]{0,1:T(8,128)(2,1)}, u32[]{:S(2)}, u32[]{:S(2)}) collective-permute-start(bf16[512,512]{0,1:T(8,128)(2,1)S(1)} %pad_maximum_fusion.1), channel_id=1, source_target_pairs={{0,8},{8,16},{16,24},{24,32},{32,40},{40,48},{48,56},{56,64},{64,7... | collective-permute-start | bytes 1572872 | tf_op jit(solution)/shard_map/ppermute | solution.py:18
  161.8 29.7 %collective-permute-start.7 = (bf16[512,512]{0,1:T(8,128)(2,1)S(1)}, bf16[512,512]{0,1:T(8,128)(2,1)}, u32[]{:S(2)}, u32[]{:S(2)}) collective-permute-start(bf16[512,512]{0,1:T(8,128)(2,1)S(1)} %pad_maximum_fusion.1), channel_id=1, source_target_pairs={{0,16},{8,24},{16,32},{24,40},{32,48},{40,56},{48,64},{56,72},{64,... | collective-permute-start | bytes 1572872 | tf_op jit(solution)/shard_map/ppermute | solution.py:18
  185.3 7.6 %copy-start.3 = (pred[512,1536]{0,1:T(8,128)(4,1)S(1)}, pred[512,1536]{0,1:T(8,128)(4,1)}, u32[]{:S(2)}) copy-start(pred[512,1536]{0,1:T(8,128)(4,1)} %and_and_fusion) | copy-start | bytes 2359300
Sparse Core Ops, SparseCore 0:
  9.9 112.7 all-gather.1
  214.0 52.6 reduce-scatter.1

commit v3 on v2

--- a/solution.py
+++ b/solution.py
@@ -55,24 +55,25 @@
     ]
     by_shift = jnp.stack(received)
     ordered = jnp.take(by_shift, (hid_index - jnp.arange(n_hid)) % n_hid, axis=0)
-    gathered_all = jnp.transpose(ordered, (1, 0, 2)).reshape(rows + 1, -1)
-    gathered, gain_row = gathered_all[:rows], gathered_all[rows:]
-    values32 = gathered.astype(jnp.float32)
-    scale_rows = lax.rsqrt(jnp.mean(values32 * values32, axis=1, keepdims=True) + 1e-06)
-    normed = (values32 * scale_rows * gain_row.astype(jnp.float32)).astype(jnp.bfloat16)
+    values32 = ordered[:, :rows].astype(jnp.float32)
+    gain_rows = ordered[:, rows:].astype(jnp.float32)
+    mean_square = jnp.sum(values32 * values32, axis=(0, 2)) / (n_hid * values32.shape[2])
+    scale_rows = lax.rsqrt(mean_square + 1e-06)[None, :, None]
+    normed = (values32 * scale_rows * gain_rows).astype(jnp.bfloat16)
     width_query = w_query.shape[1]
     width_kv = w_key.shape[1]
     stacked = lax.all_gather(
         jnp.concatenate([w_query, w_key, value_matrix], axis=1), "tok", axis=0, tiled=True
     )
-    pieces = (
-        stacked[:, :width_query],
-        stacked[:, width_query : width_query + width_kv],
-        stacked[:, width_query + width_kv :],
+    projected = jnp.einsum(
+        "jrc,jcn->rn",
+        normed,
+        stacked.reshape(n_hid, normed.shape[2], stacked.shape[1]),
+        preferred_element_type=jnp.float32,
     )
-    query_raw, key_raw, value_raw = tuple(
-        (jnp.dot(normed, piece, preferred_element_type=jnp.float32) for piece in pieces)
-    )
+    query_raw = projected[:, :width_query]
+    key_raw = projected[:, width_query : width_query + width_kv]
+    value_raw = projected[:, width_query + width_kv :]
     tok_index = lax.axis_index("tok")
     positions = tok_index * rows + jnp.arange(rows, dtype=jnp.int32)
     query = rotate(head_norm(query_raw, q_norm_gain), positions).astype(jnp.bfloat16)

time: 275 us -> 251 us (0.913)
  local copies, waits for them, and re-layouts: 59.5 us -> 24.1 us
  waiting for transfers between devices: 91.4 us -> 126 us
  other arithmetic: 38.7 us -> 21.5 us
  matrix products: 36.8 us -> 33.3 us
    all_gather x1, waiting for transfers between devices: 0.01 us -> 24.4 us  [local(): lax.all_gather(jnp.concatenate([w_query, w_key, value_matrix], axis=1), '...]
    ppermute x2, waiting for transfers between devices: 5.77 us -> 27.1 us  [shifted(): lax.ppermute(value, axis, [(source, source + steps) for source in range(l...]
    convert_element_type x5 -> x0, other arithmetic: 20.7 us -> none  [the longest x2 13 us: local(): (values32 * scale_rows * gain_row.astype(jnp.float32)).astype(jnp.bfloat16)]
    convert_element_type x3 -> x0, local copies, waits for them, and re-layouts: 20.4 us -> none  [the longest x1 12 us: local(): values32 = gathered.astype(jnp.float32)]
    dot_general x4 -> x0, local copies, waits for them, and re-layouts: 16.3 us -> none  [local(): jnp.dot(normed, piece, preferred_element_type=jnp.float32)]
    reduce_scatter x1, waiting for transfers between devices: 52.8 us -> 42.3 us  [local(): lax.psum_scatter(partial_value.astype(jnp.bfloat16), 'hid', scatter_dimen...]
    dot_general x3 -> x1, matrix products: 16 us -> 10.9 us  [local(): jnp.einsum('jrc,jcn->rn', normed, stacked.reshape(n_hid, normed.shape[2],...]
    unnamed x16 -> x13, local copies, waits for them, and re-layouts: 15.4 us -> 14.4 us
  transfers between devices with their start and end apart: 11 -> 11, of which waited for: 6 -> 8; matrix products, arithmetic and copies ran while one was open for 34% -> 14% of each run, Pallas kernels for 0% -> 0%
where the time goes in v3:
time: 251 us; the launch traced here: 250 us
  waiting for transfers between devices  126 us (50%)
  matrix products  33.3 us (13%)
  starting transfers between devices  31.7 us (13%)
  local copies, waits for them, and re-layouts  24.1 us (10%)
  other arithmetic  21.5 us (9%)
  between operations  13.7 us (5%)
    reduce_scatter x1, waiting for transfers between devices, local(): lax.psum_scatter(partial_value.astype(jnp.bfloat16), 'hid', scatter_dimen...  42.3 us
    ppermute x7, waiting for transfers between devices, local(): lax.ppermute(with_gain, 'hid', [(i, (i + k) % n_hid) for i in range(n_hid)])  32.2 us
    ppermute x2, waiting for transfers between devices, shifted(): lax.ppermute(value, axis, [(source, source + steps) for source in range(l...  27.1 us
    all_gather x1, waiting for transfers between devices, local(): lax.all_gather(jnp.concatenate([w_query, w_key, value_matrix], axis=1), '...  24.4 us
    ppermute x7, starting transfers between devices, local(): lax.ppermute(with_gain, 'hid', [(i, (i + k) % n_hid) for i in range(n_hid)])  24.1 us
    unnamed x13, local copies, waits for them, and re-layouts  14.4 us
    dot_general x1, matrix products, local(): jnp.einsum('jrc,jcn->rn', normed, stacked.reshape(n_hid, normed.shape[2],...  10.9 us
    sub x1, matrix products, local(): weights = jnp.where(allowed, jnp.exp(masked - top), 0.0)  9.99 us
  transfers between devices with their start and end apart: 11, of which 8 were waited for; matrix products, arithmetic and copies ran while one was open for 14% of the time, Pallas kernels for 0%

profile of v3, /device:TPU:2, one launch (start us, length us, event | category | flops | bytes accessed | tf_op | source)
XLA Modules:
  0.0 250.4 jit_solution(14127907636103873428)
XLA Ops:
  6.5 1.8 pad_maximum_fusion.3
  8.4 1.4 copy.34
  9.8 0.8 pad_maximum_fusion
  10.6 1.7 collective-permute-start.1
  12.2 2.2 collective-permute-start.2
  14.4 1.8 collective-permute-start.3
  16.3 1.8 collective-permute-start.4
  18.2 1.0 multiply_cosine_fusion
  19.2 1.9 and_and_fusion
  21.0 0.7 bitcast_convert_fusion
  21.7 0.7 bitcast_convert_fusion.1
  22.4 1.6 bitcast_dynamic-update-slice_fusion.7
  24.0 7.3 %collective-permute-done = bf16[513,672]{1,0:T(8,128)(2,1)} collective-permute-done((bf16[513,672]{1,0:T(8,128)(2,1)S(1)}, bf16[513,672]{1,0:T(8,128)(2,1)}, u32[]{:S(2)}, u32[]{:S(2)}) %collective-permute-start) | collective-permute-done | bytes 689504 | tf_op jit(solution)/shard_map/ppermute | solution.py:53
  31.3 1.8 collective-permute-start.5
  33.1 2.1 bitcast_dynamic-update-slice_fusion.6
  35.2 14.7 %collective-permute-start.6 = (bf16[513,672]{1,0:T(8,128)(2,1)S(1)}, bf16[513,672]{1,0:T(8,128)(2,1)S(1)}, u32[]{:S(2)}, u32[]{:S(2)}) collective-permute-start(bf16[513,672]{1,0:T(8,128)(2,1)S(1)} %pad_maximum_fusion), channel_id=1, source_target_pairs={{0,7},{1,0},{2,1},{3,2},{4,3},{5,4},{6,5},{7,6},{8,15},{9,8},{10,9... | collective-permute-start | bytes 2068424 | tf_op jit(solution)/shard_map/ppermute | solution.py:53
  49.9 2.1 bitcast_dynamic-update-slice_fusion.5
  52.1 14.7 %collective-permute-done.2 = bf16[513,672]{1,0:T(8,128)(2,1)} collective-permute-done((bf16[513,672]{1,0:T(8,128)(2,1)S(1)}, bf16[513,672]{1,0:T(8,128)(2,1)}, u32[]{:S(2)}, u32[]{:S(2)}) %collective-permute-start.2) | collective-permute-done | bytes 689504 | tf_op jit(solution)/shard_map/ppermute | solution.py:53
  66.8 2.1 bitcast_dynamic-update-slice_fusion.4
  68.8 2.1 bitcast_dynamic-update-slice_fusion.3
  71.0 10.2 %collective-permute-done.4 = bf16[513,672]{1,0:T(8,128)(2,1)S(1)} collective-permute-done((bf16[513,672]{1,0:T(8,128)(2,1)S(1)}, bf16[513,672]{1,0:T(8,128)(2,1)S(1)}, u32[]{:S(2)}, u32[]{:S(2)}) %collective-permute-start.4) | collective-permute-done | bytes 689504 | tf_op jit(solution)/shard_map/ppermute | solution.py:53
  81.1 0.9 bitcast_dynamic-update-slice_fusion.2
  82.1 1.0 bitcast_dynamic-update-slice_fusion.1
  83.1 0.9 bitcast_dynamic-update-slice_fusion
  84.1 6.5 %gather_fusion = bf16[8,513,672]{2,1,0:T(8,128)(2,1)} fusion(bf16[8,513,672]{2,1,0:T(8,128)(2,1)} %bitcast_dynamic-update-slice_fusion, s32[1024]{0:T(1024)S(1)} %pad_clamp_fusion), kind=kCustom, calls=%fused_computation | custom fusion | bytes 11031584 | tf_op jit(solution)/shard_map/jit(_take)/gather | solution.py:57
  90.6 3.7 %broadcast_select_fusion = bf16[8,513,672]{2,1,0:T(8,128)(2,1)S(1)} fusion(bf16[8,513,672]{2,1,0:T(8,128)(2,1)} %gather_fusion, pred[8]{0:T(512)(128)(4,1)S(1)} %compare_and_fusion), kind=kLoop, calls=%fused_computation.11 | loop fusion | flops 2757888 | bytes 11031560 | tf_op jit(solution)/shard_map/jit(_take)/select_n | solution.py:57
  94.3 2.6 %copy-done = bf16[8,513,672]{2,1,0:T(8,128)(2,1)} copy-done((bf16[8,513,672]{2,1,0:T(8,128)(2,1)}, bf16[8,513,672]{2,1,0:T(8,128)(2,1)S(1)}, u32[]{:S(2)}) %copy-start) | copy-done | bytes 5515800
  96.9 1.4 fusion.1
  98.3 24.4 %all-gather.2.cloned.1.call-done = bf16[5376,1024]{1,0:T(8,128)(2,1)} async-done(((bf16[168,1024]{1,0:T(8,128)(2,1)}), bf16[5376,1024]{1,0:T(8,128)(2,1)}) %all-gather.2.cloned.1.call-update) | async-done | bytes 11010064 | tf_op jit(solution)/shard_map/all_gather | solution.py:65
  122.7 10.9 %fusion.15 = f32[512,1024]{1,0:T(8,128)S(1)} fusion(bf16[8,672,1024]{2,1,0:T(8,128)(2,1)} %bitcast.74, f32[8,672]{1,0:T(8,128)S(1)} %bitcast.73, f32[512]{0:T(512)S(1)} %add_rsqrt_fusion.2, bf16[8,513,672]{2,1,0:T(8,128)(2,1)} %copy-done), kind=kOutput, calls=%fused_computation.22 | convolution fusion | flops 5648154624 | bytes 19422208 | tf_op jit(solution)/shard_map/jrc,jcn->rn/dot_general | solution.py:68
  134.1 0.6 multiply_reduce_fusion.1
  134.8 0.7 multiply_multiply_fusion.1
  135.5 0.8 subtract_convert_fusion.1
  136.3 0.7 pad_maximum_fusion.4
  137.1 0.8 pad_maximum_fusion.1
  137.9 2.7 %collective-permute-start.7 = (bf16[512,512]{1,0:T(8,128)(2,1)}, bf16[512,512]{1,0:T(8,128)(2,1)}, u32[]{:S(2)}, u32[]{:S(2)}) collective-permute-start(bf16[512,512]{1,0:T(8,128)(2,1)} %pad_maximum_fusion.1), channel_id=1, source_target_pairs={{0,16},{8,24},{16,32},{24,40},{32,48},{40,56},{48,64},{56,72},{64,... | collective-permute-start | bytes 1572872 | tf_op jit(solution)/shard_map/ppermute | solution.py:18
  140.6 4.9 %collective-permute-start.8 = (bf16[512,512]{1,0:T(8,128)(2,1)}, bf16[512,512]{1,0:T(8,128)(2,1)}, u32[]{:S(2)}, u32[]{:S(2)}) collective-permute-start(bf16[512,512]{1,0:T(8,128)(2,1)} %pad_maximum_fusion.1), channel_id=1, source_target_pairs={{0,8},{8,16},{16,24},{24,32},{32,40},{40,48},{48,56},{56,64},{64,7... | collective-permute-start | bytes 1572872 | tf_op jit(solution)/shard_map/ppermute | solution.py:18
  146.5 0.7 multiply_multiply_fusion
  147.3 0.8 subtract_convert_fusion
  148.1 0.7 pad_maximum_fusion.2
  148.9 0.9 copy.40
  149.7 18.6 %collective-permute-done.7 = bf16[512,512]{1,0:T(8,128)(2,1)} collective-permute-done((bf16[512,512]{1,0:T(8,128)(2,1)}, bf16[512,512]{1,0:T(8,128)(2,1)}, u32[]{:S(2)}, u32[]{:S(2)}) %collective-permute-start.7) | collective-permute-done | bytes 524320 | tf_op jit(solution)/shard_map/ppermute | solution.py:18
  168.4 8.5 %collective-permute-done.8 = bf16[512,512]{1,0:T(8,128)(2,1)} collective-permute-done((bf16[512,512]{1,0:T(8,128)(2,1)}, bf16[512,512]{1,0:T(8,128)(2,1)}, u32[]{:S(2)}, u32[]{:S(2)}) %collective-permute-start.8) | collective-permute-done | bytes 524320 | tf_op jit(solution)/shard_map/ppermute | solution.py:18
  176.9 1.3 maximum_maximum_fusion
  178.8 10.0 %fusion.44 = (f32[2,2,512]{2,1,0:T(2,128)S(1)}, bf16[2,2,512,1536]{2,3,1,0:T(8,128)(2,1)}) fusion(pred[512,1536]{0,1:T(8,128)(4,1)S(1)} %copy-done.1, bf16[512,2,2,128]{3,0,2,1:T(8,128)(2,1)} %bitcast.72, bf16[1536,2,128,1]{2,1,0,3:T(2,128)(2,1)S(1)} %bitcast.70), kind=kOutput, calls=%fused_computation.85 | convolution fusion | flops 824182272 | bytes 8396800 | tf_op jit(solution)/shard_map/sub | solution.py:106
  188.8 3.8 %fusion.26 = bf16[512,2,2,128]{0,3,2,1:T(8,128)(2,1)S(1)} fusion(bf16[1536,2,128,1]{0,2,3,1:T(8,128)(2,1)S(1)} %bitcast.71, bf16[2,2,512,1536]{2,3,1,0:T(8,128)(2,1)} %get-tuple-element.14, f32[512,2,2]{0,2,1:T(2,128)S(1)} %bitcast.76), kind=kOutput, calls=%fused_computation.27 | convolution fusion | flops 805830656 | bytes 7610368 | tf_op jit(solution)/shard_map/kgts,skd->tkgd/dot_general | solution.py:109
  192.5 8.6 %convolution_convert_fusion = bf16[512,5376]{0,1:T(8,128)(2,1)} fusion(bf16[512,512]{0,1:T(8,128)(2,1)S(1)} %bitcast.75, bf16[512,5376]{1,0:T(8,128)(2,1)} %param.15), kind=kOutput, calls=%fused_computation.10 | convolution fusion | flops 2821324800 | bytes 11534336 | tf_op jit(solution)/shard_map/dot_general | solution.py:114
  201.2 42.3 %reduce-scatter.2.cloned.1.call-done = bf16[512,672]{0,1:T(8,128)(2,1)} async-done(((bf16[512,5376]{0,1:T(8,128)(2,1)}), bf16[512,672]{0,1:T(8,128)(2,1)}) %reduce-scatter.2.cloned.1.call-update) | async-done | bytes 688144 | tf_op jit(solution)/shard_map/reduce_scatter | solution.py:115
  (35 shorter events, 2.4 us)
Async XLA Ops:
  6.5 116.2 %all-gather.2.cloned.1.call-start = ((), (), s32[]{:S(2)}) async-start(), calls=%async_computation.1 | async-start | bytes 11354112 | tf_op jit(solution)/shard_map/all_gather | solution.py:65
  8.3 235.2 %reduce-scatter.2.cloned.1.call-start = ((), (), s32[]{:S(2)}) async-start(), calls=%async_computation.2 | async-start | bytes 6193152 | tf_op jit(solution)/shard_map/reduce_scatter | solution.py:115
  10.5 20.8 %collective-permute-start = (bf16[513,672]{1,0:T(8,128)(2,1)S(1)}, bf16[513,672]{1,0:T(8,128)(2,1)}, u32[]{:S(2)}, u32[]{:S(2)}) collective-permute-start(bf16[513,672]{1,0:T(8,128)(2,1)S(1)} %pad_maximum_fusion), channel_id=1, source_target_pairs={{0,1},{1,2},{2,3},{3,4},{4,5},{5,6},{6,7},{7,0},{8,9},{9,10},{10,1... | collective-permute-start | bytes 2068424 | tf_op jit(solution)/shard_map/ppermute | solution.py:53
  10.6 24.7 %collective-permute-start.1 = (bf16[513,672]{1,0:T(8,128)(2,1)S(1)}, bf16[513,672]{1,0:T(8,128)(2,1)}, u32[]{:S(2)}, u32[]{:S(2)}) collective-permute-start(bf16[513,672]{1,0:T(8,128)(2,1)S(1)} %pad_maximum_fusion), channel_id=1, source_target_pairs={{0,2},{1,3},{2,4},{3,5},{4,6},{5,7},{6,0},{7,1},{8,10},{9,11},{10,... | collective-permute-start | bytes 2068424 | tf_op jit(solution)/shard_map/ppermute | solution.py:53
  12.2 54.6 %collective-permute-start.2 = (bf16[513,672]{1,0:T(8,128)(2,1)S(1)}, bf16[513,672]{1,0:T(8,128)(2,1)}, u32[]{:S(2)}, u32[]{:S(2)}) collective-permute-start(bf16[513,672]{1,0:T(8,128)(2,1)S(1)} %pad_maximum_fusion), channel_id=1, source_target_pairs={{0,3},{1,4},{2,5},{3,6},{4,7},{5,0},{6,1},{7,2},{8,11},{9,12},{10,... | collective-permute-start | bytes 2068424 | tf_op jit(solution)/shard_map/ppermute | solution.py:53
  14.4 54.4 %collective-permute-start.3 = (bf16[513,672]{1,0:T(8,128)(2,1)S(1)}, bf16[513,672]{1,0:T(8,128)(2,1)}, u32[]{:S(2)}, u32[]{:S(2)}) collective-permute-start(bf16[513,672]{1,0:T(8,128)(2,1)S(1)} %pad_maximum_fusion), channel_id=1, source_target_pairs={{0,4},{1,5},{2,6},{3,7},{4,0},{5,1},{6,2},{7,3},{8,12},{9,13},{10,... | collective-permute-start | bytes 2068424 | tf_op jit(solution)/shard_map/ppermute | solution.py:53
  16.3 64.9 %collective-permute-start.4 = (bf16[513,672]{1,0:T(8,128)(2,1)S(1)}, bf16[513,672]{1,0:T(8,128)(2,1)S(1)}, u32[]{:S(2)}, u32[]{:S(2)}) collective-permute-start(bf16[513,672]{1,0:T(8,128)(2,1)S(1)} %pad_maximum_fusion), channel_id=1, source_target_pairs={{0,5},{1,6},{2,7},{3,0},{4,1},{5,2},{6,3},{7,4},{8,13},{9,14},{10,... | collective-permute-start | bytes 2068424 | tf_op jit(solution)/shard_map/ppermute | solution.py:53
  31.3 50.8 %collective-permute-start.5 = (bf16[513,672]{1,0:T(8,128)(2,1)S(1)}, bf16[513,672]{1,0:T(8,128)(2,1)S(1)}, u32[]{:S(2)}, u32[]{:S(2)}) collective-permute-start(bf16[513,672]{1,0:T(8,128)(2,1)S(1)} %pad_maximum_fusion), channel_id=1, source_target_pairs={{0,6},{1,7},{2,0},{3,1},{4,2},{5,3},{6,4},{7,5},{8,14},{9,15},{10,... | collective-permute-start | bytes 2068424 | tf_op jit(solution)/shard_map/ppermute | solution.py:53
  35.2 47.9 %collective-permute-start.6 = (bf16[513,672]{1,0:T(8,128)(2,1)S(1)}, bf16[513,672]{1,0:T(8,128)(2,1)S(1)}, u32[]{:S(2)}, u32[]{:S(2)}) collective-permute-start(bf16[513,672]{1,0:T(8,128)(2,1)S(1)} %pad_maximum_fusion), channel_id=1, source_target_pairs={{0,7},{1,0},{2,1},{3,2},{4,3},{5,4},{6,5},{7,6},{8,15},{9,8},{10,9... | collective-permute-start | bytes 2068424 | tf_op jit(solution)/shard_map/ppermute | solution.py:53
  94.3 2.6 %copy-start = (bf16[8,513,672]{2,1,0:T(8,128)(2,1)}, bf16[8,513,672]{2,1,0:T(8,128)(2,1)S(1)}, u32[]{:S(2)}) copy-start(bf16[8,513,672]{2,1,0:T(8,128)(2,1)S(1)} %broadcast_select_fusion) | copy-start | bytes 16547332
  137.9 30.5 %collective-permute-start.7 = (bf16[512,512]{1,0:T(8,128)(2,1)}, bf16[512,512]{1,0:T(8,128)(2,1)}, u32[]{:S(2)}, u32[]{:S(2)}) collective-permute-start(bf16[512,512]{1,0:T(8,128)(2,1)} %pad_maximum_fusion.1), channel_id=1, source_target_pairs={{0,16},{8,24},{16,32},{24,40},{32,48},{40,56},{48,64},{56,72},{64,... | collective-permute-start | bytes 1572872 | tf_op jit(solution)/shard_map/ppermute | solution.py:18
  140.6 36.3 %collective-permute-start.8 = (bf16[512,512]{1,0:T(8,128)(2,1)}, bf16[512,512]{1,0:T(8,128)(2,1)}, u32[]{:S(2)}, u32[]{:S(2)}) collective-permute-start(bf16[512,512]{1,0:T(8,128)(2,1)} %pad_maximum_fusion.1), channel_id=1, source_target_pairs={{0,8},{8,16},{16,24},{24,32},{32,40},{40,48},{48,56},{56,64},{64,7... | collective-permute-start | bytes 1572872 | tf_op jit(solution)/shard_map/ppermute | solution.py:18
  148.1 30.6 %copy-start.1 = (pred[512,1536]{0,1:T(8,128)(4,1)S(1)}, pred[512,1536]{0,1:T(8,128)(4,1)}, u32[]{:S(2)}) copy-start(pred[512,1536]{0,1:T(8,128)(4,1)} %and_and_fusion) | copy-start | bytes 2359300
Sparse Core Ops, SparseCore 0:
  9.9 112.7 all-gather.1
  201.3 42.1 reduce-scatter.1

commit v4 on v3

--- a/solution.py
+++ b/solution.py
@@ -65,23 +65,24 @@
     stacked = lax.all_gather(
         jnp.concatenate([w_query, w_key, value_matrix], axis=1), "tok", axis=0, tiled=True
     )
-    projected = jnp.einsum(
-        "jrc,jcn->rn",
-        normed,
-        stacked.reshape(n_hid, normed.shape[2], stacked.shape[1]),
-        preferred_element_type=jnp.float32,
+    weights3 = stacked.reshape(n_hid, normed.shape[2], stacked.shape[1])
+    projected_kv = jnp.einsum(
+        "jrc,jcn->rn", normed, weights3[:, :, width_query:], preferred_element_type=jnp.float32
     )
-    query_raw = projected[:, :width_query]
-    key_raw = projected[:, width_query : width_query + width_kv]
-    value_raw = projected[:, width_query + width_kv :]
+    key_raw = projected_kv[:, :width_kv]
+    value_raw = projected_kv[:, width_kv:]
     tok_index = lax.axis_index("tok")
     positions = tok_index * rows + jnp.arange(rows, dtype=jnp.int32)
-    query = rotate(head_norm(query_raw, q_norm_gain), positions).astype(jnp.bfloat16)
     key = rotate(head_norm(key_raw, k_norm_gain), positions).astype(jnp.bfloat16)
     value_rows = value_raw.astype(jnp.bfloat16)
     joined = jnp.concatenate([key, value_rows], axis=1)
     reach = (WINDOW - 1 + rows - 1) // rows
     earlier = [shifted(joined, "tok", offset) for offset in range(reach, 0, -1)]
+    normed_late, _ = lax.optimization_barrier((normed, joined))
+    query_raw = jnp.einsum(
+        "jrc,jcn->rn", normed_late, weights3[:, :, :width_query], preferred_element_type=jnp.float32
+    )
+    query = rotate(head_norm(query_raw, q_norm_gain), positions).astype(jnp.bfloat16)
     window_kv = jnp.concatenate(earlier + [joined], axis=0)
     window_extent = window_kv.shape[0]
     key_pos = (tok_index - reach) * rows + jnp.arange(window_extent, dtype=jnp.int32)

time: 251 us -> 241 us (0.960)
  local copies, waits for them, and re-layouts: 24.1 us -> 18.2 us
  waiting for transfers between devices: 126 us -> 123 us
  other arithmetic: 21.5 us -> 18.7 us
    convert_element_type x0 -> x1, other arithmetic: none -> 4.68 us  [local(): normed = (values32 * scale_rows * gain_rows).astype(jnp.bfloat16)]
    unnamed x13 -> x12, local copies, waits for them, and re-layouts: 14.4 us -> 10.6 us
    dot_general x1 -> x2, matrix products: 10.9 us -> 13.9 us  [the longest x1 8.35 us: local(): jnp.einsum('jrc,jcn->rn', normed, weights3[:, :, width_query:], preferred...]
  transfers between devices with their start and end apart: 11 -> 11, of which waited for: 8 -> 8; matrix products, arithmetic and copies ran while one was open for 14% -> 17% of each run, Pallas kernels for 0% -> 0%
where the time goes in v4:
time: 241 us; the launch traced here: 240 us
  waiting for transfers between devices  123 us (51%)
  matrix products  34.8 us (14%)
  starting transfers between devices  31.7 us (13%)
  other arithmetic  18.7 us (8%)
  local copies, waits for them, and re-layouts  18.2 us (8%)
  between operations  13.6 us (6%)
    reduce_scatter x1, waiting for transfers between devices, local(): lax.psum_scatter(partial_value.astype(jnp.bfloat16), 'hid', scatter_dimen...  42.2 us
    ppermute x7, waiting for transfers between devices, local(): lax.ppermute(with_gain, 'hid', [(i, (i + k) % n_hid) for i in range(n_hid)])  33.8 us
    ppermute x2, waiting for transfers between devices, shifted(): lax.ppermute(value, axis, [(source, source + steps) for source in range(l...  24.9 us
    ppermute x7, starting transfers between devices, local(): lax.ppermute(with_gain, 'hid', [(i, (i + k) % n_hid) for i in range(n_hid)])  24.1 us
    all_gather x1, waiting for transfers between devices, local(): lax.all_gather(jnp.concatenate([w_query, w_key, value_matrix], axis=1), '...  22.4 us
    unnamed x12, local copies, waits for them, and re-layouts  10.6 us
    dot_general x1, matrix products, local(): jnp.dot(heads_out, w_out, preferred_element_type=jnp.float32)  8.64 us
    sub x1, matrix products, local(): weights = jnp.where(allowed, jnp.exp(masked - top), 0.0)  8.51 us
  transfers between devices with their start and end apart: 11, of which 8 were waited for; matrix products, arithmetic and copies ran while one was open for 17% of the time, Pallas kernels for 0%

profile of v4, /device:TPU:2, one launch (start us, length us, event | category | flops | bytes accessed | tf_op | source)
XLA Modules:
  0.0 240.4 jit_solution(15395777152723076451)
XLA Ops:
  6.5 1.8 pad_maximum_fusion.3
  8.4 1.4 copy.19
  9.8 0.8 pad_maximum_fusion
  10.6 1.7 collective-permute-start.1
  12.2 2.2 collective-permute-start.2
  14.4 1.8 collective-permute-start.3
  16.3 1.8 collective-permute-start.4
  18.2 0.5 multiply_cosine_fusion
  18.7 1.9 and_and_fusion
  20.6 0.7 bitcast_convert_fusion.1
  21.2 0.7 bitcast_convert_fusion
  21.9 1.6 bitcast_dynamic-update-slice_fusion.7
  23.6 7.7 %collective-permute-done = bf16[513,672]{1,0:T(8,128)(2,1)} collective-permute-done((bf16[513,672]{1,0:T(8,128)(2,1)S(1)}, bf16[513,672]{1,0:T(8,128)(2,1)}, u32[]{:S(2)}, u32[]{:S(2)}) %collective-permute-start) | collective-permute-done | bytes 689504 | tf_op jit(solution)/shard_map/ppermute | solution.py:53
  31.3 1.8 collective-permute-start.5
  33.1 2.1 bitcast_dynamic-update-slice_fusion.6
  35.2 14.7 %collective-permute-start.6 = (bf16[513,672]{1,0:T(8,128)(2,1)S(1)}, bf16[513,672]{1,0:T(8,128)(2,1)S(1)}, u32[]{:S(2)}, u32[]{:S(2)}) collective-permute-start(bf16[513,672]{1,0:T(8,128)(2,1)S(1)} %pad_maximum_fusion), channel_id=1, source_target_pairs={{0,7},{1,0},{2,1},{3,2},{4,3},{5,4},{6,5},{7,6},{8,15},{9,8},{10,9... | collective-permute-start | bytes 2068424 | tf_op jit(solution)/shard_map/ppermute | solution.py:53
  49.9 2.1 bitcast_dynamic-update-slice_fusion.5
  52.1 14.7 %collective-permute-done.2 = bf16[513,672]{1,0:T(8,128)(2,1)} collective-permute-done((bf16[513,672]{1,0:T(8,128)(2,1)S(1)}, bf16[513,672]{1,0:T(8,128)(2,1)}, u32[]{:S(2)}, u32[]{:S(2)}) %collective-permute-start.2) | collective-permute-done | bytes 689504 | tf_op jit(solution)/shard_map/ppermute | solution.py:53
  66.8 2.1 bitcast_dynamic-update-slice_fusion.4
  68.8 1.0 bitcast_dynamic-update-slice_fusion.3
  69.8 11.3 %collective-permute-done.4 = bf16[513,672]{1,0:T(8,128)(2,1)S(1)} collective-permute-done((bf16[513,672]{1,0:T(8,128)(2,1)S(1)}, bf16[513,672]{1,0:T(8,128)(2,1)S(1)}, u32[]{:S(2)}, u32[]{:S(2)}) %collective-permute-start.4) | collective-permute-done | bytes 689504 | tf_op jit(solution)/shard_map/ppermute | solution.py:53
  81.1 0.9 bitcast_dynamic-update-slice_fusion.2
  82.1 1.0 bitcast_dynamic-update-slice_fusion.1
  83.1 0.1 collective-permute-done.6
  83.1 0.9 bitcast_dynamic-update-slice_fusion
  84.1 6.5 %gather_fusion = bf16[8,513,672]{2,1,0:T(8,128)(2,1)} fusion(bf16[8,513,672]{2,1,0:T(8,128)(2,1)} %bitcast_dynamic-update-slice_fusion, s32[1024]{0:T(1024)S(1)} %pad_clamp_fusion), kind=kCustom, calls=%fused_computation | custom fusion | bytes 11031584 | tf_op jit(solution)/shard_map/jit(_take)/gather | solution.py:57
  90.6 3.7 %broadcast_select_fusion = bf16[8,513,672]{2,1,0:T(8,128)(2,1)S(1)} fusion(bf16[8,513,672]{2,1,0:T(8,128)(2,1)} %gather_fusion, pred[8]{0:T(512)(128)(4,1)S(1)} %compare_and_fusion), kind=kLoop, calls=%fused_computation.11 | loop fusion | flops 2757888 | bytes 11031560 | tf_op jit(solution)/shard_map/jit(_take)/select_n | solution.py:57
  94.3 1.4 fusion.1
  95.7 4.7 %fusion.3 = bf16[8,512,672]{2,1,0:T(8,128)(2,1)} fusion(f32[8,672]{1,0:T(8,128)S(1)} %bitcast.85, f32[512]{0:T(512)S(1)} %add_rsqrt_fusion.2, bf16[8,513,672]{2,1,0:T(8,128)(2,1)S(1)} %broadcast_select_fusion), kind=kLoop, calls=%fused_computation.6 | loop fusion | flops 11010048 | bytes 11033600 | tf_op jit(solution)/shard_map/convert_element_type | solution.py:62
  100.4 22.4 %all-gather.2.cloned.1.call-done = bf16[5376,1024]{1,0:T(8,128)(2,1)} async-done(((bf16[168,1024]{1,0:T(8,128)(2,1)}), bf16[5376,1024]{1,0:T(8,128)(2,1)}) %all-gather.2.cloned.1.call-update) | async-done | bytes 11010064 | tf_op jit(solution)/shard_map/all_gather | solution.py:65
  122.7 8.4 %fusion.14 = f32[512,512]{0,1:T(8,128)S(1)} fusion(bf16[8,512,672]{2,1,0:T(8,128)(2,1)} %fusion.3, bf16[8,672,1024]{2,1,0:T(8,128)(2,1)} %bitcast.86), kind=kOutput, calls=%fused_computation.23 | convolution fusion | flops 2818572288 | bytes 12845056 | tf_op jit(solution)/shard_map/jrc,jcn->rn/dot_general | solution.py:69
  131.1 0.1 multiply_reduce_fusion.1
  131.2 0.1 multiply_multiply_fusion.1
  131.3 0.1 subtract_convert_fusion.1
  131.5 2.7 %collective-permute-start.7 = (bf16[512,512]{0,1:T(8,128)(2,1)S(1)}, bf16[512,512]{0,1:T(8,128)(2,1)S(1)}, u32[]{:S(2)}, u32[]{:S(2)}) collective-permute-start(bf16[512,512]{0,1:T(8,128)(2,1)S(1)} %pad_maximum_fusion.1), channel_id=1, source_target_pairs={{0,16},{8,24},{16,32},{24,40},{32,48},{40,56},{48,64},{56,72},{64,... | collective-permute-start | bytes 1572872 | tf_op jit(solution)/shard_map/ppermute | solution.py:18
  134.2 4.9 %collective-permute-start.8 = (bf16[512,512]{0,1:T(8,128)(2,1)S(1)}, bf16[512,512]{0,1:T(8,128)(2,1)S(1)}, u32[]{:S(2)}, u32[]{:S(2)}) collective-permute-start(bf16[512,512]{0,1:T(8,128)(2,1)S(1)} %pad_maximum_fusion.1), channel_id=1, source_target_pairs={{0,8},{8,16},{16,24},{24,32},{32,40},{40,48},{48,56},{56,64},{64,7... | collective-permute-start | bytes 1572872 | tf_op jit(solution)/shard_map/ppermute | solution.py:18
  139.1 5.5 %fusion.10 = f32[512,512,1]{0,1,2:T(8,128)S(1)} fusion(bf16[8,512,672]{2,1,0:T(8,128)(2,1)S(1)} %copy-done, bf16[8,672,1024]{2,1,0:T(8,128)(2,1)} %bitcast.87), kind=kOutput, calls=%fused_computation.17 | convolution fusion | flops 2818572288 | bytes 12058624 | tf_op jit(solution)/shard_map/jrc,jcn->rn/dot_general | solution.py:82
  144.7 0.1 multiply_reduce_fusion
  144.8 0.2 multiply_multiply_fusion
  145.0 0.2 subtract_convert_fusion
  145.2 16.4 %collective-permute-done.7 = bf16[512,512]{0,1:T(8,128)(2,1)S(1)} collective-permute-done((bf16[512,512]{0,1:T(8,128)(2,1)S(1)}, bf16[512,512]{0,1:T(8,128)(2,1)S(1)}, u32[]{:S(2)}, u32[]{:S(2)}) %collective-permute-start.7) | collective-permute-done | bytes 524320 | tf_op jit(solution)/shard_map/ppermute | solution.py:18
  161.7 8.5 %collective-permute-done.8 = bf16[512,512]{0,1:T(8,128)(2,1)S(1)} collective-permute-done((bf16[512,512]{0,1:T(8,128)(2,1)S(1)}, bf16[512,512]{0,1:T(8,128)(2,1)S(1)}, u32[]{:S(2)}, u32[]{:S(2)}) %collective-permute-start.8) | collective-permute-done | bytes 524320 | tf_op jit(solution)/shard_map/ppermute | solution.py:18
  170.1 0.1 maximum_maximum_fusion
  170.3 0.1 fusion.35
  170.4 8.5 %fusion.36 = (f32[2,2,512]{2,1,0:T(2,128)S(1)}, bf16[2,2,512,1536]{2,3,1,0:T(8,128)(2,1)}) fusion(pred[512,1536]{0,1:T(8,128)(4,1)S(1)} %copy-done.1, bf16[1536,2,128,1]{0,2,3,1:T(8,128)(2,1)S(1)} %bitcast.83, bf16[512,2,2,128]{0,3,2,1:T(8,128)(2,1)S(1)} %bitcast.84), kind=kOutput, calls=%fused_computation.81 | convolution fusion | flops 824182272 | bytes 8396800 | tf_op jit(solution)/shard_map/sub | solution.py:107
  178.9 3.8 %fusion.25 = bf16[512,2,2,128]{0,3,2,1:T(8,128)(2,1)S(1)} fusion(bf16[1536,2,128,1]{0,2,3,1:T(8,128)(2,1)S(1)} %bitcast.82, bf16[2,2,512,1536]{2,3,1,0:T(8,128)(2,1)} %get-tuple-element.16, f32[512,2,2]{0,2,1:T(2,128)S(1)} %bitcast.89), kind=kOutput, calls=%fused_computation.27 | convolution fusion | flops 805830656 | bytes 7610368 | tf_op jit(solution)/shard_map/kgts,skd->tkgd/dot_general | solution.py:110
  182.7 8.6 %convolution_convert_fusion = bf16[512,5376]{0,1:T(8,128)(2,1)} fusion(bf16[512,512]{0,1:T(8,128)(2,1)S(1)} %bitcast.88, bf16[512,5376]{1,0:T(8,128)(2,1)} %param.15), kind=kOutput, calls=%fused_computation.10 | convolution fusion | flops 2821324800 | bytes 11534336 | tf_op jit(solution)/shard_map/dot_general | solution.py:115
  191.3 42.2 %reduce-scatter.2.cloned.1.call-done = bf16[512,672]{0,1:T(8,128)(2,1)} async-done(((bf16[512,5376]{0,1:T(8,128)(2,1)}), bf16[512,672]{0,1:T(8,128)(2,1)}) %reduce-scatter.2.cloned.1.call-update) | async-done | bytes 688144 | tf_op jit(solution)/shard_map/reduce_scatter | solution.py:116
  (29 shorter events, 0.4 us)
Async XLA Ops:
  6.5 116.2 %all-gather.2.cloned.1.call-start = ((), (), s32[]{:S(2)}) async-start(), calls=%async_computation.1 | async-start | bytes 11354112 | tf_op jit(solution)/shard_map/all_gather | solution.py:65
  8.3 225.2 %reduce-scatter.2.cloned.1.call-start = ((), (), s32[]{:S(2)}) async-start(), calls=%async_computation.2 | async-start | bytes 6193152 | tf_op jit(solution)/shard_map/reduce_scatter | solution.py:116
  10.5 20.8 %collective-permute-start = (bf16[513,672]{1,0:T(8,128)(2,1)S(1)}, bf16[513,672]{1,0:T(8,128)(2,1)}, u32[]{:S(2)}, u32[]{:S(2)}) collective-permute-start(bf16[513,672]{1,0:T(8,128)(2,1)S(1)} %pad_maximum_fusion), channel_id=1, source_target_pairs={{0,1},{1,2},{2,3},{3,4},{4,5},{5,6},{6,7},{7,0},{8,9},{9,10},{10,1... | collective-permute-start | bytes 2068424 | tf_op jit(solution)/shard_map/ppermute | solution.py:53
  10.6 24.7 %collective-permute-start.1 = (bf16[513,672]{1,0:T(8,128)(2,1)S(1)}, bf16[513,672]{1,0:T(8,128)(2,1)}, u32[]{:S(2)}, u32[]{:S(2)}) collective-permute-start(bf16[513,672]{1,0:T(8,128)(2,1)S(1)} %pad_maximum_fusion), channel_id=1, source_target_pairs={{0,2},{1,3},{2,4},{3,5},{4,6},{5,7},{6,0},{7,1},{8,10},{9,11},{10,... | collective-permute-start | bytes 2068424 | tf_op jit(solution)/shard_map/ppermute | solution.py:53
  12.2 54.6 %collective-permute-start.2 = (bf16[513,672]{1,0:T(8,128)(2,1)S(1)}, bf16[513,672]{1,0:T(8,128)(2,1)}, u32[]{:S(2)}, u32[]{:S(2)}) collective-permute-start(bf16[513,672]{1,0:T(8,128)(2,1)S(1)} %pad_maximum_fusion), channel_id=1, source_target_pairs={{0,3},{1,4},{2,5},{3,6},{4,7},{5,0},{6,1},{7,2},{8,11},{9,12},{10,... | collective-permute-start | bytes 2068424 | tf_op jit(solution)/shard_map/ppermute | solution.py:53
  14.4 54.4 %collective-permute-start.3 = (bf16[513,672]{1,0:T(8,128)(2,1)S(1)}, bf16[513,672]{1,0:T(8,128)(2,1)S(1)}, u32[]{:S(2)}, u32[]{:S(2)}) collective-permute-start(bf16[513,672]{1,0:T(8,128)(2,1)S(1)} %pad_maximum_fusion), channel_id=1, source_target_pairs={{0,4},{1,5},{2,6},{3,7},{4,0},{5,1},{6,2},{7,3},{8,12},{9,13},{10,... | collective-permute-start | bytes 2068424 | tf_op jit(solution)/shard_map/ppermute | solution.py:53
  16.3 64.9 %collective-permute-start.4 = (bf16[513,672]{1,0:T(8,128)(2,1)S(1)}, bf16[513,672]{1,0:T(8,128)(2,1)S(1)}, u32[]{:S(2)}, u32[]{:S(2)}) collective-permute-start(bf16[513,672]{1,0:T(8,128)(2,1)S(1)} %pad_maximum_fusion), channel_id=1, source_target_pairs={{0,5},{1,6},{2,7},{3,0},{4,1},{5,2},{6,3},{7,4},{8,13},{9,14},{10,... | collective-permute-start | bytes 2068424 | tf_op jit(solution)/shard_map/ppermute | solution.py:53
  31.3 50.8 %collective-permute-start.5 = (bf16[513,672]{1,0:T(8,128)(2,1)S(1)}, bf16[513,672]{1,0:T(8,128)(2,1)S(1)}, u32[]{:S(2)}, u32[]{:S(2)}) collective-permute-start(bf16[513,672]{1,0:T(8,128)(2,1)S(1)} %pad_maximum_fusion), channel_id=1, source_target_pairs={{0,6},{1,7},{2,0},{3,1},{4,2},{5,3},{6,4},{7,5},{8,14},{9,15},{10,... | collective-permute-start | bytes 2068424 | tf_op jit(solution)/shard_map/ppermute | solution.py:53
  35.2 47.9 %collective-permute-start.6 = (bf16[513,672]{1,0:T(8,128)(2,1)S(1)}, bf16[513,672]{1,0:T(8,128)(2,1)S(1)}, u32[]{:S(2)}, u32[]{:S(2)}) collective-permute-start(bf16[513,672]{1,0:T(8,128)(2,1)S(1)} %pad_maximum_fusion), channel_id=1, source_target_pairs={{0,7},{1,0},{2,1},{3,2},{4,3},{5,4},{6,5},{7,6},{8,15},{9,8},{10,9... | collective-permute-start | bytes 2068424 | tf_op jit(solution)/shard_map/ppermute | solution.py:53
  122.7 16.4 %copy-start = (bf16[8,512,672]{2,1,0:T(8,128)(2,1)S(1)}, bf16[8,512,672]{2,1,0:T(8,128)(2,1)}, u32[]{:S(2)}) copy-start(bf16[8,512,672]{2,1,0:T(8,128)(2,1)} %fusion.3) | copy-start | bytes 16515076
  131.5 30.2 %collective-permute-start.7 = (bf16[512,512]{0,1:T(8,128)(2,1)S(1)}, bf16[512,512]{0,1:T(8,128)(2,1)S(1)}, u32[]{:S(2)}, u32[]{:S(2)}) collective-permute-start(bf16[512,512]{0,1:T(8,128)(2,1)S(1)} %pad_maximum_fusion.1), channel_id=1, source_target_pairs={{0,16},{8,24},{16,32},{24,40},{32,48},{40,56},{48,64},{56,72},{64,... | collective-permute-start | bytes 1572872 | tf_op jit(solution)/shard_map/ppermute | solution.py:18
  134.2 35.9 %collective-permute-start.8 = (bf16[512,512]{0,1:T(8,128)(2,1)S(1)}, bf16[512,512]{0,1:T(8,128)(2,1)S(1)}, u32[]{:S(2)}, u32[]{:S(2)}) collective-permute-start(bf16[512,512]{0,1:T(8,128)(2,1)S(1)} %pad_maximum_fusion.1), channel_id=1, source_target_pairs={{0,8},{8,16},{16,24},{24,32},{32,40},{40,48},{48,56},{56,64},{64,7... | collective-permute-start | bytes 1572872 | tf_op jit(solution)/shard_map/ppermute | solution.py:18
  144.6 25.7 %copy-start.1 = (pred[512,1536]{0,1:T(8,128)(4,1)S(1)}, pred[512,1536]{0,1:T(8,128)(4,1)}, u32[]{:S(2)}) copy-start(pred[512,1536]{0,1:T(8,128)(4,1)} %and_and_fusion) | copy-start | bytes 2359300
Sparse Core Ops, SparseCore 0:
  9.9 112.7 all-gather.1
  191.5 42.0 reduce-scatter.1

commit v5 on v4

--- a/solution.py
+++ b/solution.py
@@ -7,6 +7,8 @@
 
 HEAD_SIZE = 128
 WINDOW = 1024
+TOK = ("tx", "tz")
+HID = ("hy", "hc")
 
 
 score_scale = 168.0 ** (-0.5)
@@ -47,10 +49,10 @@
 def local(tokens, norm_gain, w_query, w_key, value_matrix, q_norm_gain, k_norm_gain, w_out):
     rows = tokens.shape[0]
     with_gain = jnp.concatenate([tokens, norm_gain], axis=0)
-    n_hid = lax.axis_size("hid")
-    hid_index = lax.axis_index("hid")
+    n_hid = lax.axis_size(HID)
+    hid_index = lax.axis_index(HID)
     received = [with_gain] + [
-        lax.ppermute(with_gain, "hid", [(i, (i + k) % n_hid) for i in range(n_hid)])
+        lax.ppermute(with_gain, HID, [(i, (i + k) % n_hid) for i in range(n_hid)])
         for k in range(1, n_hid)
     ]
     by_shift = jnp.stack(received)
@@ -63,7 +65,12 @@
     width_query = w_query.shape[1]
     width_kv = w_key.shape[1]
     stacked = lax.all_gather(
-        jnp.concatenate([w_query, w_key, value_matrix], axis=1), "tok", axis=0, tiled=True
+        lax.all_gather(
+            jnp.concatenate([w_query, w_key, value_matrix], axis=1), "tz", axis=0, tiled=True
+        ),
+        "tx",
+        axis=0,
+        tiled=True,
     )
     weights3 = stacked.reshape(n_hid, normed.shape[2], stacked.shape[1])
     projected_kv = jnp.einsum(
@@ -71,13 +78,13 @@
     )
     key_raw = projected_kv[:, :width_kv]
     value_raw = projected_kv[:, width_kv:]
-    tok_index = lax.axis_index("tok")
+    tok_index = lax.axis_index(TOK)
     positions = tok_index * rows + jnp.arange(rows, dtype=jnp.int32)
     key = rotate(head_norm(key_raw, k_norm_gain), positions).astype(jnp.bfloat16)
     value_rows = value_raw.astype(jnp.bfloat16)
     joined = jnp.concatenate([key, value_rows], axis=1)
     reach = (WINDOW - 1 + rows - 1) // rows
-    earlier = [shifted(joined, "tok", offset) for offset in range(reach, 0, -1)]
+    earlier = [shifted(joined, TOK, offset) for offset in range(reach, 0, -1)]
     normed_late, _ = lax.optimization_barrier((normed, joined))
     query_raw = jnp.einsum(
         "jrc,jcn->rn", normed_late, weights3[:, :, :width_query], preferred_element_type=jnp.float32
@@ -114,20 +121,27 @@
     heads_out = mixed.reshape(rows, width_query).astype(jnp.bfloat16)
     partial_value = jnp.dot(heads_out, w_out, preferred_element_type=jnp.float32)
     return lax.psum_scatter(
-        partial_value.astype(jnp.bfloat16), "hid", scatter_dimension=1, tiled=True
+        partial_value.astype(jnp.bfloat16), HID, scatter_dimension=1, tiled=True
     )
 
 
 def solution(mesh):
+    devices = mesh.devices
+    n_x = len({d.coords[0] for d in devices.flat})
+    n_y = len({d.coords[1] for d in devices.flat})
+    split = jax.sharding.Mesh(
+        devices.reshape(n_x, devices.shape[0] // n_x, n_y, devices.shape[1] // n_y),
+        ("tx", "tz", "hy", "hc"),
+    )
     in_specs = (
-        P("tok", "hid"),
-        P(None, "hid"),
-        P("tok", "hid"),
-        P("tok", "hid"),
-        P("tok", "hid"),
+        P(TOK, HID),
+        P(None, HID),
+        P(TOK, HID),
+        P(TOK, HID),
+        P(TOK, HID),
         P(),
         P(),
-        P("hid", None),
+        P(HID, None),
     )
-    out_specs = P("tok", "hid")
-    return jax.shard_map(local, mesh=mesh, in_specs=in_specs, out_specs=out_specs, check_vma=False)
+    out_specs = P(TOK, HID)
+    return jax.shard_map(local, mesh=split, in_specs=in_specs, out_specs=out_specs, check_vma=False)

time: 241 us -> 283 us (1.17)
  waiting for transfers between devices: 123 us -> 168 us
    all_gather x1, waiting for transfers between devices: 22.4 us -> 46.3 us  [local(): lax.all_gather(jnp.concatenate([w_query, w_key, value_matrix], axis=1), '...]
    all_gather x0 -> x1, waiting for transfers between devices: none -> 16.5 us  [local(): lax.all_gather(lax.all_gather(jnp.concatenate([w_query, w_key, value_matr...]
    unnamed x12 -> x18, local copies, waits for them, and re-layouts: 10.6 us -> 10.6 us
  transfers between devices with their start and end apart: 11 -> 12, of which waited for: 8 -> 9; matrix products, arithmetic and copies ran while one was open for 17% -> 13% of each run, Pallas kernels for 0% -> 0%
where the time goes in v5:
time: 283 us
  waiting for transfers between devices  168 us (59%)
  matrix products  34.7 us (12%)
  starting transfers between devices  31.7 us (11%)
  local copies, waits for them, and re-layouts  18.2 us (6%)
  other arithmetic  16.6 us (6%)
  between operations  13.4 us (5%)
    all_gather x1, waiting for transfers between devices, local(): lax.all_gather(jnp.concatenate([w_query, w_key, value_matrix], axis=1), '...  46.3 us
    reduce_scatter x1, waiting for transfers between devices, local(): lax.psum_scatter(partial_value.astype(jnp.bfloat16), HID, scatter_dimensi...  42.5 us
    ppermute x7, waiting for transfers between devices, local(): lax.ppermute(with_gain, HID, [(i, (i + k) % n_hid) for i in range(n_hid)])  36.3 us
    ppermute x2, waiting for transfers between devices, shifted(): lax.ppermute(value, axis, [(source, source + steps) for source in range(l...  26.6 us
    ppermute x7, starting transfers between devices, local(): lax.ppermute(with_gain, HID, [(i, (i + k) % n_hid) for i in range(n_hid)])  23.5 us
    all_gather x1, waiting for transfers between devices, local(): lax.all_gather(lax.all_gather(jnp.concatenate([w_query, w_key, value_matr...  16.5 us
    unnamed x18, local copies, waits for them, and re-layouts  10.6 us
    dot_general x1, matrix products, local(): jnp.dot(heads_out, w_out, preferred_element_type=jnp.float32)  8.63 us
  transfers between devices with their start and end apart: 12, of which 9 were waited for; matrix products, arithmetic and copies ran while one was open for 13% of the time, Pallas kernels for 0%

profile of v5, /device:TPU:2, one launch (start us, length us, event | category | flops | bytes accessed | tf_op | source)
XLA Modules:
  0.0 282.9 jit_solution(6416758314910907047)
XLA Ops:
  6.5 1.8 pad_maximum_fusion.3
  8.4 0.0 all-gather.5.cloned.1.call-start
  8.4 46.3 %all-gather.3.cloned.1.call-done = bf16[1344,1024]{1,0:T(8,128)(2,1)} async-done(((bf16[168,1024]{1,0:T(8,128)(2,1)}), bf16[1344,1024]{1,0:T(8,128)(2,1)}) %all-gather.3.cloned.1.call-update) | async-done | bytes 2752528 | tf_op jit(solution)/shard_map/all_gather | solution.py:68
  54.8 1.4 copy.19
  56.2 0.8 pad_maximum_fusion
  57.0 1.6 collective-permute-start.1
  58.6 2.0 collective-permute-start.2
  60.6 2.0 collective-permute-start.3
  62.6 1.6 collective-permute-start.4
  64.3 0.5 multiply_cosine_fusion
  64.9 1.9 and_and_fusion
  66.8 1.0 bitcast_dynamic-update-slice_fusion.7
  67.8 9.9 %collective-permute-done = bf16[513,672]{1,0:T(8,128)(2,1)} collective-permute-done((bf16[513,672]{1,0:T(8,128)(2,1)S(1)}, bf16[513,672]{1,0:T(8,128)(2,1)}, u32[]{:S(2)}, u32[]{:S(2)}) %collective-permute-start) | collective-permute-done | bytes 689504 | tf_op jit(solution)/shard_map/ppermute | solution.py:55
  77.7 1.5 collective-permute-start.5
  79.3 2.1 bitcast_dynamic-update-slice_fusion.6
  81.4 14.7 %collective-permute-start.6 = (bf16[513,672]{1,0:T(8,128)(2,1)S(1)}, bf16[513,672]{1,0:T(8,128)(2,1)S(1)}, u32[]{:S(2)}, u32[]{:S(2)}) collective-permute-start(bf16[513,672]{1,0:T(8,128)(2,1)S(1)} %pad_maximum_fusion), channel_id=1, source_target_pairs={{0,7},{1,0},{2,1},{3,2},{4,3},{5,4},{6,5},{7,6},{8,15},{9,8},{10,9... | collective-permute-start | bytes 2068424 | tf_op jit(solution)/shard_map/ppermute | solution.py:55
  96.1 2.1 bitcast_dynamic-update-slice_fusion.5
  98.2 14.7 %collective-permute-done.2 = bf16[513,672]{1,0:T(8,128)(2,1)} collective-permute-done((bf16[513,672]{1,0:T(8,128)(2,1)S(1)}, bf16[513,672]{1,0:T(8,128)(2,1)}, u32[]{:S(2)}, u32[]{:S(2)}) %collective-permute-start.2) | collective-permute-done | bytes 689504 | tf_op jit(solution)/shard_map/ppermute | solution.py:55
  112.9 2.1 bitcast_dynamic-update-slice_fusion.4
  115.0 1.0 bitcast_dynamic-update-slice_fusion.3
  116.0 11.4 %collective-permute-done.4 = bf16[513,672]{1,0:T(8,128)(2,1)S(1)} collective-permute-done((bf16[513,672]{1,0:T(8,128)(2,1)S(1)}, bf16[513,672]{1,0:T(8,128)(2,1)S(1)}, u32[]{:S(2)}, u32[]{:S(2)}) %collective-permute-start.4) | collective-permute-done | bytes 689504 | tf_op jit(solution)/shard_map/ppermute | solution.py:55
  127.4 1.0 bitcast_dynamic-update-slice_fusion.2
  128.4 1.0 bitcast_dynamic-update-slice_fusion.1
  129.4 0.2 collective-permute-done.6
  129.6 0.9 bitcast_dynamic-update-slice_fusion
  130.5 6.5 %gather_fusion = bf16[8,513,672]{2,1,0:T(8,128)(2,1)} fusion(bf16[8,513,672]{2,1,0:T(8,128)(2,1)} %bitcast_dynamic-update-slice_fusion, s32[1024]{0:T(1024)S(1)} %pad_clamp_fusion), kind=kCustom, calls=%fused_computation | custom fusion | bytes 11031584 | tf_op jit(solution)/shard_map/jit(_take)/gather | solution.py:59
  137.0 3.5 %broadcast_select_fusion = bf16[8,513,672]{2,1,0:T(8,128)(2,1)S(1)} fusion(bf16[8,513,672]{2,1,0:T(8,128)(2,1)} %gather_fusion, pred[8]{0:T(512)(128)(4,1)S(1)} %compare_and_fusion), kind=kLoop, calls=%fused_computation.11 | loop fusion | flops 2757888 | bytes 11031560 | tf_op jit(solution)/shard_map/jit(_take)/select_n | solution.py:59
  140.6 1.4 fusion.1
  142.0 4.7 %fusion.3 = bf16[8,512,672]{2,1,0:T(8,128)(2,1)} fusion(f32[8,672]{1,0:T(8,128)S(1)} %bitcast.85, f32[512]{0:T(512)S(1)} %add_rsqrt_fusion.2, bf16[8,513,672]{2,1,0:T(8,128)(2,1)S(1)} %broadcast_select_fusion), kind=kLoop, calls=%fused_computation.6 | loop fusion | flops 11010048 | bytes 11033600 | tf_op jit(solution)/shard_map/convert_element_type | solution.py:64
  146.6 16.5 %all-gather.5.cloned.1.call-done = bf16[5376,1024]{1,0:T(8,128)(2,1)} async-done(((bf16[1344,1024]{1,0:T(8,128)(2,1)}), bf16[5376,1024]{1,0:T(8,128)(2,1)}) %all-gather.5.cloned.1.call-update) | async-done | bytes 11010064 | tf_op jit(solution)/shard_map/all_gather | solution.py:67
  163.1 8.3 %fusion.14 = f32[512,512]{0,1:T(8,128)S(1)} fusion(bf16[8,512,672]{2,1,0:T(8,128)(2,1)} %fusion.3, bf16[8,672,1024]{2,1,0:T(8,128)(2,1)} %bitcast.86), kind=kOutput, calls=%fused_computation.23 | convolution fusion | flops 2818572288 | bytes 12845056 | tf_op jit(solution)/shard_map/jrc,jcn->rn/dot_general | solution.py:76
  171.4 0.1 multiply_reduce_fusion.1
  171.6 0.1 multiply_multiply_fusion.1
  171.7 0.1 subtract_convert_fusion.1
  171.8 4.5 %collective-permute-start.7 = (bf16[512,512]{0,1:T(8,128)(2,1)S(1)}, bf16[512,512]{0,1:T(8,128)(2,1)S(1)}, u32[]{:S(2)}, u32[]{:S(2)}) collective-permute-start(bf16[512,512]{0,1:T(8,128)(2,1)S(1)} %pad_maximum_fusion.1), channel_id=1, source_target_pairs={{0,16},{8,24},{16,32},{24,40},{32,48},{40,56},{48,64},{56,72},{64,... | collective-permute-start | bytes 1572872 | tf_op jit(solution)/shard_map/ppermute | solution.py:20
  176.3 3.7 %collective-permute-start.8 = (bf16[512,512]{0,1:T(8,128)(2,1)S(1)}, bf16[512,512]{0,1:T(8,128)(2,1)S(1)}, u32[]{:S(2)}, u32[]{:S(2)}) collective-permute-start(bf16[512,512]{0,1:T(8,128)(2,1)S(1)} %pad_maximum_fusion.1), channel_id=1, source_target_pairs={{0,8},{8,16},{16,24},{24,32},{32,40},{40,48},{48,56},{56,64},{64,7... | collective-permute-start | bytes 1572872 | tf_op jit(solution)/shard_map/ppermute | solution.py:20
  180.0 5.5 %fusion.10 = f32[512,512,1]{0,1,2:T(8,128)S(1)} fusion(bf16[8,512,672]{2,1,0:T(8,128)(2,1)S(1)} %copy-done, bf16[8,672,1024]{2,1,0:T(8,128)(2,1)} %bitcast.87), kind=kOutput, calls=%fused_computation.17 | convolution fusion | flops 2818572288 | bytes 12058624 | tf_op jit(solution)/shard_map/jrc,jcn->rn/dot_general | solution.py:89
  185.6 0.1 multiply_reduce_fusion
  185.7 0.2 multiply_multiply_fusion
  185.9 0.2 subtract_convert_fusion
  186.1 15.8 %collective-permute-done.7 = bf16[512,512]{0,1:T(8,128)(2,1)S(1)} collective-permute-done((bf16[512,512]{0,1:T(8,128)(2,1)S(1)}, bf16[512,512]{0,1:T(8,128)(2,1)S(1)}, u32[]{:S(2)}, u32[]{:S(2)}) %collective-permute-start.7) | collective-permute-done | bytes 524320 | tf_op jit(solution)/shard_map/ppermute | solution.py:20
  201.9 10.8 %collective-permute-done.8 = bf16[512,512]{0,1:T(8,128)(2,1)S(1)} collective-permute-done((bf16[512,512]{0,1:T(8,128)(2,1)S(1)}, bf16[512,512]{0,1:T(8,128)(2,1)S(1)}, u32[]{:S(2)}, u32[]{:S(2)}) %collective-permute-start.8) | collective-permute-done | bytes 524320 | tf_op jit(solution)/shard_map/ppermute | solution.py:20
  212.7 0.1 maximum_maximum_fusion
  212.8 0.1 fusion.35
  212.9 8.5 %fusion.36 = (f32[2,2,512]{2,1,0:T(2,128)S(1)}, bf16[2,2,512,1536]{2,3,1,0:T(8,128)(2,1)}) fusion(pred[512,1536]{0,1:T(8,128)(4,1)S(1)} %copy-done.1, bf16[1536,2,128,1]{0,2,3,1:T(8,128)(2,1)S(1)} %bitcast.83, bf16[512,2,2,128]{0,3,2,1:T(8,128)(2,1)S(1)} %bitcast.84), kind=kOutput, calls=%fused_computation.81 | convolution fusion | flops 824182272 | bytes 8396800 | tf_op jit(solution)/shard_map/sub | solution.py:114
  221.4 3.8 %fusion.25 = bf16[512,2,2,128]{0,3,2,1:T(8,128)(2,1)S(1)} fusion(bf16[1536,2,128,1]{0,2,3,1:T(8,128)(2,1)S(1)} %bitcast.82, bf16[2,2,512,1536]{2,3,1,0:T(8,128)(2,1)} %get-tuple-element.16, f32[512,2,2]{0,2,1:T(2,128)S(1)} %bitcast.89), kind=kOutput, calls=%fused_computation.27 | convolution fusion | flops 805830656 | bytes 7610368 | tf_op jit(solution)/shard_map/kgts,skd->tkgd/dot_general | solution.py:117
  225.2 8.6 %convolution_convert_fusion = bf16[512,5376]{0,1:T(8,128)(2,1)} fusion(bf16[512,512]{0,1:T(8,128)(2,1)S(1)} %bitcast.88, bf16[512,5376]{1,0:T(8,128)(2,1)} %param.15), kind=kOutput, calls=%fused_computation.10 | convolution fusion | flops 2821324800 | bytes 11534336 | tf_op jit(solution)/shard_map/dot_general | solution.py:122
  233.9 42.5 %reduce-scatter.2.cloned.1.call-done = bf16[512,672]{0,1:T(8,128)(2,1)} async-done(((bf16[512,5376]{0,1:T(8,128)(2,1)}), bf16[512,672]{0,1:T(8,128)(2,1)}) %reduce-scatter.2.cloned.1.call-update) | async-done | bytes 688144 | tf_op jit(solution)/shard_map/reduce_scatter | solution.py:123
  (38 shorter events, 0.4 us)
Async XLA Ops:
  6.5 60.3 %copy-start.2 = (bf16[1,672]{1,0:T(2,128)(2,1)S(1)}, bf16[1,672]{1,0:T(2,128)(2,1)}, u32[]{:S(2)}) copy-start(bf16[1,672]{1,0:T(2,128)(2,1)} %param.9) | copy-start | bytes 4036
  6.5 60.3 %copy-start.3 = (bf16[1,128]{1,0:T(2,128)(2,1)S(1)}, bf16[1,128]{1,0:T(2,128)(2,1)}, u32[]{:S(2)}) copy-start(bf16[1,128]{1,0:T(2,128)(2,1)} %param.14) | copy-start | bytes 772
  6.5 60.3 %copy-start.4 = (bf16[1,128]{1,0:T(2,128)(2,1)S(1)}, bf16[1,128]{1,0:T(2,128)(2,1)}, u32[]{:S(2)}) copy-start(bf16[1,128]{1,0:T(2,128)(2,1)} %param.13) | copy-start | bytes 772
  6.5 48.2 %all-gather.3.cloned.1.call-start = ((), (), s32[]{:S(2)}) async-start(), calls=%async_computation.1 | async-start | bytes 3096576 | tf_op jit(solution)/shard_map/all_gather | solution.py:68
  8.4 154.7 %all-gather.5.cloned.1.call-start = ((), (), s32[]{:S(2)}) async-start(), calls=%async_computation.2 | async-start | bytes 13762560 | tf_op jit(solution)/shard_map/all_gather | solution.py:67
  54.8 221.6 %reduce-scatter.2.cloned.1.call-start = ((), (), s32[]{:S(2)}) async-start(), calls=%async_computation.3 | async-start | bytes 6193152 | tf_op jit(solution)/shard_map/reduce_scatter | solution.py:123
  57.0 20.8 %collective-permute-start = (bf16[513,672]{1,0:T(8,128)(2,1)S(1)}, bf16[513,672]{1,0:T(8,128)(2,1)}, u32[]{:S(2)}, u32[]{:S(2)}) collective-permute-start(bf16[513,672]{1,0:T(8,128)(2,1)S(1)} %pad_maximum_fusion), channel_id=1, source_target_pairs={{0,1},{1,2},{2,3},{3,4},{4,5},{5,6},{6,7},{7,0},{8,9},{9,10},{10,1... | collective-permute-start | bytes 2068424 | tf_op jit(solution)/shard_map/ppermute | solution.py:55
  57.0 24.4 %collective-permute-start.1 = (bf16[513,672]{1,0:T(8,128)(2,1)S(1)}, bf16[513,672]{1,0:T(8,128)(2,1)}, u32[]{:S(2)}, u32[]{:S(2)}) collective-permute-start(bf16[513,672]{1,0:T(8,128)(2,1)S(1)} %pad_maximum_fusion), channel_id=1, source_target_pairs={{0,2},{1,3},{2,4},{3,5},{4,6},{5,7},{6,0},{7,1},{8,10},{9,11},{10,... | collective-permute-start | bytes 2068424 | tf_op jit(solution)/shard_map/ppermute | solution.py:55
  58.6 54.4 %collective-permute-start.2 = (bf16[513,672]{1,0:T(8,128)(2,1)S(1)}, bf16[513,672]{1,0:T(8,128)(2,1)}, u32[]{:S(2)}, u32[]{:S(2)}) collective-permute-start(bf16[513,672]{1,0:T(8,128)(2,1)S(1)} %pad_maximum_fusion), channel_id=1, source_target_pairs={{0,3},{1,4},{2,5},{3,6},{4,7},{5,0},{6,1},{7,2},{8,11},{9,12},{10,... | collective-permute-start | bytes 2068424 | tf_op jit(solution)/shard_map/ppermute | solution.py:55
  60.6 54.4 %collective-permute-start.3 = (bf16[513,672]{1,0:T(8,128)(2,1)S(1)}, bf16[513,672]{1,0:T(8,128)(2,1)S(1)}, u32[]{:S(2)}, u32[]{:S(2)}) collective-permute-start(bf16[513,672]{1,0:T(8,128)(2,1)S(1)} %pad_maximum_fusion), channel_id=1, source_target_pairs={{0,4},{1,5},{2,6},{3,7},{4,0},{5,1},{6,2},{7,3},{8,12},{9,13},{10,... | collective-permute-start | bytes 2068424 | tf_op jit(solution)/shard_map/ppermute | solution.py:55
  62.6 64.8 %collective-permute-start.4 = (bf16[513,672]{1,0:T(8,128)(2,1)S(1)}, bf16[513,672]{1,0:T(8,128)(2,1)S(1)}, u32[]{:S(2)}, u32[]{:S(2)}) collective-permute-start(bf16[513,672]{1,0:T(8,128)(2,1)S(1)} %pad_maximum_fusion), channel_id=1, source_target_pairs={{0,5},{1,6},{2,7},{3,0},{4,1},{5,2},{6,3},{7,4},{8,13},{9,14},{10,... | collective-permute-start | bytes 2068424 | tf_op jit(solution)/shard_map/ppermute | solution.py:55
  77.7 50.7 %collective-permute-start.5 = (bf16[513,672]{1,0:T(8,128)(2,1)S(1)}, bf16[513,672]{1,0:T(8,128)(2,1)S(1)}, u32[]{:S(2)}, u32[]{:S(2)}) collective-permute-start(bf16[513,672]{1,0:T(8,128)(2,1)S(1)} %pad_maximum_fusion), channel_id=1, source_target_pairs={{0,6},{1,7},{2,0},{3,1},{4,2},{5,3},{6,4},{7,5},{8,14},{9,15},{10,... | collective-permute-start | bytes 2068424 | tf_op jit(solution)/shard_map/ppermute | solution.py:55
  81.4 48.2 %collective-permute-start.6 = (bf16[513,672]{1,0:T(8,128)(2,1)S(1)}, bf16[513,672]{1,0:T(8,128)(2,1)S(1)}, u32[]{:S(2)}, u32[]{:S(2)}) collective-permute-start(bf16[513,672]{1,0:T(8,128)(2,1)S(1)} %pad_maximum_fusion), channel_id=1, source_target_pairs={{0,7},{1,0},{2,1},{3,2},{4,3},{5,4},{6,5},{7,6},{8,15},{9,8},{10,9... | collective-permute-start | bytes 2068424 | tf_op jit(solution)/shard_map/ppermute | solution.py:55
  163.1 16.9 %copy-start = (bf16[8,512,672]{2,1,0:T(8,128)(2,1)S(1)}, bf16[8,512,672]{2,1,0:T(8,128)(2,1)}, u32[]{:S(2)}) copy-start(bf16[8,512,672]{2,1,0:T(8,128)(2,1)} %fusion.3) | copy-start | bytes 16515076
  171.8 30.0 %collective-permute-start.7 = (bf16[512,512]{0,1:T(8,128)(2,1)S(1)}, bf16[512,512]{0,1:T(8,128)(2,1)S(1)}, u32[]{:S(2)}, u32[]{:S(2)}) collective-permute-start(bf16[512,512]{0,1:T(8,128)(2,1)S(1)} %pad_maximum_fusion.1), channel_id=1, source_target_pairs={{0,16},{8,24},{16,32},{24,40},{32,48},{40,56},{48,64},{56,72},{64,... | collective-permute-start | bytes 1572872 | tf_op jit(solution)/shard_map/ppermute | solution.py:20
  176.3 36.4 %collective-permute-start.8 = (bf16[512,512]{0,1:T(8,128)(2,1)S(1)}, bf16[512,512]{0,1:T(8,128)(2,1)S(1)}, u32[]{:S(2)}, u32[]{:S(2)}) collective-permute-start(bf16[512,512]{0,1:T(8,128)(2,1)S(1)} %pad_maximum_fusion.1), channel_id=1, source_target_pairs={{0,8},{8,16},{16,24},{24,32},{32,40},{40,48},{48,56},{56,64},{64,7... | collective-permute-start | bytes 1572872 | tf_op jit(solution)/shard_map/ppermute | solution.py:20
  185.5 27.4 %copy-start.1 = (pred[512,1536]{0,1:T(8,128)(4,1)S(1)}, pred[512,1536]{0,1:T(8,128)(4,1)}, u32[]{:S(2)}) copy-start(pred[512,1536]{0,1:T(8,128)(4,1)} %and_and_fusion) | copy-start | bytes 2359300
Sparse Core Ops, SparseCore 0:
  9.1 45.5 all-gather.2
  56.6 106.4 all-gather.4
  234.0 42.3 reduce-scatter.1

commit v6 on v5

--- a/solution.py
+++ b/solution.py
@@ -65,12 +65,7 @@
     width_query = w_query.shape[1]
     width_kv = w_key.shape[1]
     stacked = lax.all_gather(
-        lax.all_gather(
-            jnp.concatenate([w_query, w_key, value_matrix], axis=1), "tz", axis=0, tiled=True
-        ),
-        "tx",
-        axis=0,
-        tiled=True,
+        jnp.concatenate([w_query, w_key, value_matrix], axis=1), TOK, axis=0, tiled=True
     )
     weights3 = stacked.reshape(n_hid, normed.shape[2], stacked.shape[1])
     projected_kv = jnp.einsum(
@@ -119,10 +114,15 @@
     )
     mixed = mixed / jnp.transpose(total, (2, 0, 1))[..., None]
     heads_out = mixed.reshape(rows, width_query).astype(jnp.bfloat16)
-    partial_value = jnp.dot(heads_out, w_out, preferred_element_type=jnp.float32)
-    return lax.psum_scatter(
-        partial_value.astype(jnp.bfloat16), HID, scatter_dimension=1, tiled=True
+    n_y, n_c = lax.axis_size("hy"), lax.axis_size("hc")
+    by_core = w_out.reshape(w_out.shape[0], n_y, n_c, -1).transpose(0, 2, 1, 3)
+    partial_value = jnp.dot(
+        heads_out, by_core.reshape(w_out.shape), preferred_element_type=jnp.float32
     )
+    on_chip = lax.psum_scatter(
+        partial_value.astype(jnp.bfloat16), "hc", scatter_dimension=1, tiled=True
+    )
+    return lax.psum_scatter(on_chip, "hy", scatter_dimension=1, tiled=True)
 
 
 def solution(mesh):

time: 283 us -> 266 us (0.940)
  waiting for transfers between devices: 168 us -> 133 us
  local copies, waits for them, and re-layouts: 18.2 us -> 40.2 us
  starting transfers between devices: 31.7 us -> 26.4 us
    unnamed x3 -> x5, waiting for transfers between devices: 0.05 us -> 59.4 us
    reduce_scatter x1 -> x0, waiting for transfers between devices: 42.5 us -> none  [local(): lax.psum_scatter(partial_value.astype(jnp.bfloat16), HID, scatter_dimensi...]
    all_gather x2 -> x1, waiting for transfers between devices: 62.8 us -> 22.4 us  [local(): lax.all_gather(jnp.concatenate([w_query, w_key, value_matrix], axis=1), T...]
    unnamed x18 -> x16, local copies, waits for them, and re-layouts: 10.6 us -> 27.2 us
    ppermute x7, waiting for transfers between devices: 36.3 us -> 26.1 us  [local(): lax.ppermute(with_gain, HID, [(i, (i + k) % n_hid) for i in range(n_hid)])]
    transpose x0 -> x1, local copies, waits for them, and re-layouts: none -> 5.35 us  [local(): by_core = w_out.reshape(w_out.shape[0], n_y, n_c, -1).transpose(0, 2, 1, 3)]
    ppermute x7, starting transfers between devices: 23.5 us -> 18.7 us  [local(): lax.ppermute(with_gain, HID, [(i, (i + k) % n_hid) for i in range(n_hid)])]
  transfers between devices with their start and end apart: 12 -> 12, of which waited for: 9 -> 8; matrix products, arithmetic and copies ran while one was open for 13% -> 20% of each run, Pallas kernels for 0% -> 0%
where the time goes in v6:
time: 266 us; the launch traced here: 264 us
  waiting for transfers between devices  133 us (50%)
  local copies, waits for them, and re-layouts  40.2 us (15%)
  matrix products  33.6 us (13%)
  starting transfers between devices  26.4 us (10%)
  other arithmetic  18 us (7%)
  between operations  13.4 us (5%)
    unnamed x5, waiting for transfers between devices  59.4 us
    unnamed x16, local copies, waits for them, and re-layouts  27.2 us
    ppermute x7, waiting for transfers between devices, local(): lax.ppermute(with_gain, HID, [(i, (i + k) % n_hid) for i in range(n_hid)])  26.1 us
    ppermute x2, waiting for transfers between devices, shifted(): lax.ppermute(value, axis, [(source, source + steps) for source in range(l...  24.9 us
    all_gather x1, waiting for transfers between devices, local(): lax.all_gather(jnp.concatenate([w_query, w_key, value_matrix], axis=1), T...  22.4 us
    ppermute x7, starting transfers between devices, local(): lax.ppermute(with_gain, HID, [(i, (i + k) % n_hid) for i in range(n_hid)])  18.7 us
    sub x1, matrix products, local(): weights = jnp.where(allowed, jnp.exp(masked - top), 0.0)  8.48 us
    dot_general x1, matrix products, local(): jnp.einsum('jrc,jcn->rn', normed, weights3[:, :, width_query:], preferred...  8.34 us
  transfers between devices with their start and end apart: 12, of which 8 were waited for; matrix products, arithmetic and copies ran while one was open for 20% of the time, Pallas kernels for 0%

profile of v6, /device:TPU:2, one launch (start us, length us, event | category | flops | bytes accessed | tf_op | source)
XLA Modules:
  0.0 264.5 jit_solution(1757479938800573751)
XLA Ops:
  6.5 1.8 pad_maximum_fusion.3
  8.4 1.4 copy.32
  9.8 0.8 pad_maximum_fusion
  10.6 1.7 collective-permute-start.1
  12.2 2.2 collective-permute-start.2
  14.4 1.8 collective-permute-start.3
  16.3 1.8 collective-permute-start.4
  18.2 0.5 multiply_cosine_fusion
  18.7 1.9 and_and_fusion
  20.6 0.7 bitcast_convert_fusion.1
  21.3 0.7 bitcast_convert_fusion
  22.0 8.3 %copy.38 = bf16[512,5376]{0,1:T(8,128)(2,1)} copy(bf16[512,5376]{1,0:T(8,128)(2,1)} %param.15) | data formatting | bytes 11010048 | tf_op args[7]
  30.3 5.4 %copy.39 = bf16[512,2,4,672]{0,3,2,1:T(8,128)(2,1)} copy(bf16[512,2,4,672]{0,3,1,2:T(8,128)(2,1)} %bitcast.88) | data formatting | bytes 11010048 | tf_op jit(solution)/shard_map/transpose | solution.py:118
  35.7 1.0 bitcast_dynamic-update-slice_fusion.7
  36.6 1.3 collective-permute-start.5
  37.9 2.1 bitcast_dynamic-update-slice_fusion.6
  40.0 9.9 %collective-permute-start.6 = (bf16[513,672]{1,0:T(8,128)(2,1)S(1)}, bf16[513,672]{1,0:T(8,128)(2,1)S(1)}, u32[]{:S(2)}, u32[]{:S(2)}) collective-permute-start(bf16[513,672]{1,0:T(8,128)(2,1)S(1)} %pad_maximum_fusion), channel_id=1, source_target_pairs={{0,7},{1,0},{2,1},{3,2},{4,3},{5,4},{6,5},{7,6},{8,15},{9,8},{10,9... | collective-permute-start | bytes 2068424 | tf_op jit(solution)/shard_map/ppermute | solution.py:55
  49.9 2.1 bitcast_dynamic-update-slice_fusion.5
  52.1 14.7 %collective-permute-done.2 = bf16[513,672]{1,0:T(8,128)(2,1)} collective-permute-done((bf16[513,672]{1,0:T(8,128)(2,1)S(1)}, bf16[513,672]{1,0:T(8,128)(2,1)}, u32[]{:S(2)}, u32[]{:S(2)}) %collective-permute-start.2) | collective-permute-done | bytes 689504 | tf_op jit(solution)/shard_map/ppermute | solution.py:55
  66.8 2.1 bitcast_dynamic-update-slice_fusion.4
  68.8 1.0 bitcast_dynamic-update-slice_fusion.3
  69.8 11.3 %collective-permute-done.4 = bf16[513,672]{1,0:T(8,128)(2,1)S(1)} collective-permute-done((bf16[513,672]{1,0:T(8,128)(2,1)S(1)}, bf16[513,672]{1,0:T(8,128)(2,1)S(1)}, u32[]{:S(2)}, u32[]{:S(2)}) %collective-permute-start.4) | collective-permute-done | bytes 689504 | tf_op jit(solution)/shard_map/ppermute | solution.py:55
  81.1 0.9 bitcast_dynamic-update-slice_fusion.2
  82.1 1.0 bitcast_dynamic-update-slice_fusion.1
  83.1 1.0 bitcast_dynamic-update-slice_fusion
  84.1 6.5 %gather_fusion = bf16[8,513,672]{2,1,0:T(8,128)(2,1)} fusion(bf16[8,513,672]{2,1,0:T(8,128)(2,1)} %bitcast_dynamic-update-slice_fusion, s32[1024]{0:T(1024)S(1)} %pad_clamp_fusion), kind=kCustom, calls=%fused_computation | custom fusion | bytes 11031584 | tf_op jit(solution)/shard_map/jit(_take)/gather | solution.py:59
  90.6 3.7 %broadcast_select_fusion = bf16[8,513,672]{2,1,0:T(8,128)(2,1)S(1)} fusion(bf16[8,513,672]{2,1,0:T(8,128)(2,1)} %gather_fusion, pred[8]{0:T(512)(128)(4,1)S(1)} %compare_and_fusion), kind=kLoop, calls=%fused_computation.11 | loop fusion | flops 2757888 | bytes 11031560 | tf_op jit(solution)/shard_map/jit(_take)/select_n | solution.py:59
  94.3 1.4 fusion.1
  95.7 4.7 %fusion.3 = bf16[8,512,672]{2,1,0:T(8,128)(2,1)} fusion(f32[8,672]{1,0:T(8,128)S(1)} %bitcast.97, f32[512]{0:T(512)S(1)} %add_rsqrt_fusion.2, bf16[8,513,672]{2,1,0:T(8,128)(2,1)S(1)} %broadcast_select_fusion), kind=kLoop, calls=%fused_computation.6 | loop fusion | flops 11010048 | bytes 11033600 | tf_op jit(solution)/shard_map/convert_element_type | solution.py:64
  100.4 22.4 %all-gather.2.cloned.1.call-done = bf16[5376,1024]{1,0:T(8,128)(2,1)} async-done(((bf16[168,1024]{1,0:T(8,128)(2,1)}), bf16[5376,1024]{1,0:T(8,128)(2,1)}) %all-gather.2.cloned.1.call-update) | async-done | bytes 11010064 | tf_op jit(solution)/shard_map/all_gather | solution.py:67
  122.7 8.3 %fusion.14 = f32[512,512]{0,1:T(8,128)S(1)} fusion(bf16[8,512,672]{2,1,0:T(8,128)(2,1)} %fusion.3, bf16[8,672,1024]{2,1,0:T(8,128)(2,1)} %bitcast.98), kind=kOutput, calls=%fused_computation.23 | convolution fusion | flops 2818572288 | bytes 12845056 | tf_op jit(solution)/shard_map/jrc,jcn->rn/dot_general | solution.py:71
  131.2 0.1 multiply_multiply_fusion.1
  131.5 2.7 %collective-permute-start.7 = (bf16[512,512]{0,1:T(8,128)(2,1)S(1)}, bf16[512,512]{0,1:T(8,128)(2,1)S(1)}, u32[]{:S(2)}, u32[]{:S(2)}) collective-permute-start(bf16[512,512]{0,1:T(8,128)(2,1)S(1)} %pad_maximum_fusion.1), channel_id=1, source_target_pairs={{0,16},{8,24},{16,32},{24,40},{32,48},{40,56},{48,64},{56,72},{64,... | collective-permute-start | bytes 1572872 | tf_op jit(solution)/shard_map/ppermute | solution.py:20
  134.2 4.9 %collective-permute-start.8 = (bf16[512,512]{0,1:T(8,128)(2,1)S(1)}, bf16[512,512]{0,1:T(8,128)(2,1)S(1)}, u32[]{:S(2)}, u32[]{:S(2)}) collective-permute-start(bf16[512,512]{0,1:T(8,128)(2,1)S(1)} %pad_maximum_fusion.1), channel_id=1, source_target_pairs={{0,8},{8,16},{16,24},{24,32},{32,40},{40,48},{48,56},{56,64},{64,7... | collective-permute-start | bytes 1572872 | tf_op jit(solution)/shard_map/ppermute | solution.py:20
  139.1 5.5 %fusion.10 = f32[512,512,1]{0,1,2:T(8,128)S(1)} fusion(bf16[8,512,672]{2,1,0:T(8,128)(2,1)S(1)} %copy-done, bf16[8,672,1024]{2,1,0:T(8,128)(2,1)} %bitcast.99), kind=kOutput, calls=%fused_computation.17 | convolution fusion | flops 2818572288 | bytes 12058624 | tf_op jit(solution)/shard_map/jrc,jcn->rn/dot_general | solution.py:84
  144.6 0.1 multiply_reduce_fusion
  144.8 0.2 multiply_multiply_fusion
  145.0 0.2 subtract_convert_fusion
  145.2 16.4 %collective-permute-done.7 = bf16[512,512]{0,1:T(8,128)(2,1)S(1)} collective-permute-done((bf16[512,512]{0,1:T(8,128)(2,1)S(1)}, bf16[512,512]{0,1:T(8,128)(2,1)S(1)}, u32[]{:S(2)}, u32[]{:S(2)}) %collective-permute-start.7) | collective-permute-done | bytes 524320 | tf_op jit(solution)/shard_map/ppermute | solution.py:20
  161.7 8.5 %collective-permute-done.8 = bf16[512,512]{0,1:T(8,128)(2,1)S(1)} collective-permute-done((bf16[512,512]{0,1:T(8,128)(2,1)S(1)}, bf16[512,512]{0,1:T(8,128)(2,1)S(1)}, u32[]{:S(2)}, u32[]{:S(2)}) %collective-permute-start.8) | collective-permute-done | bytes 524320 | tf_op jit(solution)/shard_map/ppermute | solution.py:20
  170.1 0.1 maximum_maximum_fusion
  170.2 0.1 fusion.35
  170.4 8.5 %fusion.36 = (f32[2,2,512]{2,1,0:T(2,128)S(1)}, bf16[2,2,512,1536]{2,3,1,0:T(8,128)(2,1)}) fusion(pred[512,1536]{0,1:T(8,128)(4,1)S(1)} %copy-done.1, bf16[1536,2,128,1]{0,2,3,1:T(8,128)(2,1)S(1)} %bitcast.95, bf16[512,2,2,128]{0,3,2,1:T(8,128)(2,1)S(1)} %bitcast.96), kind=kOutput, calls=%fused_computation.81 | convolution fusion | flops 824182272 | bytes 8396800 | tf_op jit(solution)/shard_map/sub | solution.py:109
  178.9 3.8 %fusion.25 = bf16[512,2,2,128]{0,3,2,1:T(8,128)(2,1)S(1)} fusion(bf16[1536,2,128,1]{0,2,3,1:T(8,128)(2,1)S(1)} %bitcast.94, bf16[2,2,512,1536]{2,3,1,0:T(8,128)(2,1)} %get-tuple-element.16, f32[512,2,2]{0,2,1:T(2,128)S(1)} %bitcast.101), kind=kOutput, calls=%fused_computation.27 | convolution fusion | flops 805830656 | bytes 7610368 | tf_op jit(solution)/shard_map/kgts,skd->tkgd/dot_general | solution.py:112
  182.6 7.5 %convolution_convert_fusion = bf16[512,5376]{1,0:T(8,128)(2,1)} fusion(bf16[512,512]{0,1:T(8,128)(2,1)S(1)} %bitcast.100, bf16[512,5376]{0,1:T(8,128)(2,1)} %bitcast.89), kind=kOutput, calls=%fused_computation.10 | convolution fusion | flops 2821324800 | bytes 11534336 | tf_op jit(solution)/shard_map/dot_general | solution.py:119
  190.1 8.3 %copy.48 = bf16[512,5376]{0,1:T(8,128)(2,1)} copy(bf16[512,5376]{1,0:T(8,128)(2,1)} %convolution_convert_fusion) | data formatting | bytes 11010048
  198.5 17.9 %reduce-scatter.7.cloned.1.call-done = bf16[2688,512]{1,0:T(8,128)(2,1)} async-done(((bf16[5376,512]{1,0:T(8,128)(2,1)}), bf16[2688,512]{1,0:T(8,128)(2,1)}) %reduce-scatter.7.cloned.1.call-update) | async-done | bytes 2752528
  216.4 41.5 %reduce-scatter.9.cloned.1.call-done = bf16[672,512]{1,0:T(8,128)(2,1)} async-done(((bf16[2688,512]{1,0:T(8,128)(2,1)}), bf16[672,512]{1,0:T(8,128)(2,1)}) %reduce-scatter.9.cloned.1.call-update) | async-done | bytes 688144
  (37 shorter events, 0.7 us)
Async XLA Ops:
  6.5 116.2 %all-gather.2.cloned.1.call-start = ((), (), s32[]{:S(2)}) async-start(), calls=%async_computation.2 | async-start | bytes 11354112 | tf_op jit(solution)/shard_map/all_gather | solution.py:67
  8.3 208.1 %reduce-scatter.7.cloned.1.call-start = ((), (), s32[]{:S(2)}) async-start(), calls=%async_computation.3 | async-start | bytes 8257536
  10.5 26.1 %collective-permute-start = (bf16[513,672]{1,0:T(8,128)(2,1)S(1)}, bf16[513,672]{1,0:T(8,128)(2,1)}, u32[]{:S(2)}, u32[]{:S(2)}) collective-permute-start(bf16[513,672]{1,0:T(8,128)(2,1)S(1)} %pad_maximum_fusion), channel_id=1, source_target_pairs={{0,1},{1,2},{2,3},{3,4},{4,5},{5,6},{6,7},{7,0},{8,9},{9,10},{10,1... | collective-permute-start | bytes 2068424 | tf_op jit(solution)/shard_map/ppermute | solution.py:55
  10.6 29.4 %collective-permute-start.1 = (bf16[513,672]{1,0:T(8,128)(2,1)S(1)}, bf16[513,672]{1,0:T(8,128)(2,1)}, u32[]{:S(2)}, u32[]{:S(2)}) collective-permute-start(bf16[513,672]{1,0:T(8,128)(2,1)S(1)} %pad_maximum_fusion), channel_id=1, source_target_pairs={{0,2},{1,3},{2,4},{3,5},{4,6},{5,7},{6,0},{7,1},{8,10},{9,11},{10,... | collective-permute-start | bytes 2068424 | tf_op jit(solution)/shard_map/ppermute | solution.py:55
  12.2 54.6 %collective-permute-start.2 = (bf16[513,672]{1,0:T(8,128)(2,1)S(1)}, bf16[513,672]{1,0:T(8,128)(2,1)}, u32[]{:S(2)}, u32[]{:S(2)}) collective-permute-start(bf16[513,672]{1,0:T(8,128)(2,1)S(1)} %pad_maximum_fusion), channel_id=1, source_target_pairs={{0,3},{1,4},{2,5},{3,6},{4,7},{5,0},{6,1},{7,2},{8,11},{9,12},{10,... | collective-permute-start | bytes 2068424 | tf_op jit(solution)/shard_map/ppermute | solution.py:55
  14.4 54.4 %collective-permute-start.3 = (bf16[513,672]{1,0:T(8,128)(2,1)S(1)}, bf16[513,672]{1,0:T(8,128)(2,1)S(1)}, u32[]{:S(2)}, u32[]{:S(2)}) collective-permute-start(bf16[513,672]{1,0:T(8,128)(2,1)S(1)} %pad_maximum_fusion), channel_id=1, source_target_pairs={{0,4},{1,5},{2,6},{3,7},{4,0},{5,1},{6,2},{7,3},{8,12},{9,13},{10,... | collective-permute-start | bytes 2068424 | tf_op jit(solution)/shard_map/ppermute | solution.py:55
  16.3 64.9 %collective-permute-start.4 = (bf16[513,672]{1,0:T(8,128)(2,1)S(1)}, bf16[513,672]{1,0:T(8,128)(2,1)S(1)}, u32[]{:S(2)}, u32[]{:S(2)}) collective-permute-start(bf16[513,672]{1,0:T(8,128)(2,1)S(1)} %pad_maximum_fusion), channel_id=1, source_target_pairs={{0,5},{1,6},{2,7},{3,0},{4,1},{5,2},{6,3},{7,4},{8,13},{9,14},{10,... | collective-permute-start | bytes 2068424 | tf_op jit(solution)/shard_map/ppermute | solution.py:55
  30.3 5.4 %copy-start.2 = (bf16[1,672]{1,0:T(2,128)(2,1)S(1)}, bf16[1,672]{1,0:T(2,128)(2,1)}, u32[]{:S(2)}) copy-start(bf16[1,672]{1,0:T(2,128)(2,1)} %param.9) | copy-start | bytes 4036
  36.6 45.5 %collective-permute-start.5 = (bf16[513,672]{1,0:T(8,128)(2,1)S(1)}, bf16[513,672]{1,0:T(8,128)(2,1)S(1)}, u32[]{:S(2)}, u32[]{:S(2)}) collective-permute-start(bf16[513,672]{1,0:T(8,128)(2,1)S(1)} %pad_maximum_fusion), channel_id=1, source_target_pairs={{0,6},{1,7},{2,0},{3,1},{4,2},{5,3},{6,4},{7,5},{8,14},{9,15},{10,... | collective-permute-start | bytes 2068424 | tf_op jit(solution)/shard_map/ppermute | solution.py:55
  40.0 43.1 %collective-permute-start.6 = (bf16[513,672]{1,0:T(8,128)(2,1)S(1)}, bf16[513,672]{1,0:T(8,128)(2,1)S(1)}, u32[]{:S(2)}, u32[]{:S(2)}) collective-permute-start(bf16[513,672]{1,0:T(8,128)(2,1)S(1)} %pad_maximum_fusion), channel_id=1, source_target_pairs={{0,7},{1,0},{2,1},{3,2},{4,3},{5,4},{6,5},{7,6},{8,15},{9,8},{10,9... | collective-permute-start | bytes 2068424 | tf_op jit(solution)/shard_map/ppermute | solution.py:55
  122.7 16.4 %copy-start = (bf16[8,512,672]{2,1,0:T(8,128)(2,1)S(1)}, bf16[8,512,672]{2,1,0:T(8,128)(2,1)}, u32[]{:S(2)}) copy-start(bf16[8,512,672]{2,1,0:T(8,128)(2,1)} %fusion.3) | copy-start | bytes 16515076
  131.5 30.2 %collective-permute-start.7 = (bf16[512,512]{0,1:T(8,128)(2,1)S(1)}, bf16[512,512]{0,1:T(8,128)(2,1)S(1)}, u32[]{:S(2)}, u32[]{:S(2)}) collective-permute-start(bf16[512,512]{0,1:T(8,128)(2,1)S(1)} %pad_maximum_fusion.1), channel_id=1, source_target_pairs={{0,16},{8,24},{16,32},{24,40},{32,48},{40,56},{48,64},{56,72},{64,... | collective-permute-start | bytes 1572872 | tf_op jit(solution)/shard_map/ppermute | solution.py:20
  134.2 35.9 %collective-permute-start.8 = (bf16[512,512]{0,1:T(8,128)(2,1)S(1)}, bf16[512,512]{0,1:T(8,128)(2,1)S(1)}, u32[]{:S(2)}, u32[]{:S(2)}) collective-permute-start(bf16[512,512]{0,1:T(8,128)(2,1)S(1)} %pad_maximum_fusion.1), channel_id=1, source_target_pairs={{0,8},{8,16},{16,24},{24,32},{32,40},{40,48},{48,56},{56,64},{64,7... | collective-permute-start | bytes 1572872 | tf_op jit(solution)/shard_map/ppermute | solution.py:20
  144.6 25.7 %copy-start.1 = (pred[512,1536]{0,1:T(8,128)(4,1)S(1)}, pred[512,1536]{0,1:T(8,128)(4,1)}, u32[]{:S(2)}) copy-start(pred[512,1536]{0,1:T(8,128)(4,1)} %and_and_fusion) | copy-start | bytes 2359300
  198.5 59.5 %reduce-scatter.9.cloned.1.call-start = ((), (), s32[]{:S(2)}) async-start(), calls=%async_computation.4 | async-start | bytes 3440640
Sparse Core Ops, SparseCore 0:
  9.9 112.7 all-gather.1
  198.6 17.7 reduce-scatter.6
  219.0 38.9 reduce-scatter.8

commit v7 on v4

--- a/solution.py
+++ b/solution.py
@@ -75,22 +75,23 @@
     positions = tok_index * rows + jnp.arange(rows, dtype=jnp.int32)
     key = rotate(head_norm(key_raw, k_norm_gain), positions).astype(jnp.bfloat16)
     value_rows = value_raw.astype(jnp.bfloat16)
-    joined = jnp.concatenate([key, value_rows], axis=1)
     reach = (WINDOW - 1 + rows - 1) // rows
-    earlier = [shifted(joined, "tok", offset) for offset in range(reach, 0, -1)]
-    normed_late, _ = lax.optimization_barrier((normed, joined))
+    earlier_keys = [shifted(key, "tok", offset) for offset in range(reach, 0, -1)]
+    earlier_values = [shifted(value_rows, "tok", offset) for offset in range(reach, 0, -1)]
+    normed_late, _ = lax.optimization_barrier((normed, earlier_keys[0]))
     query_raw = jnp.einsum(
         "jrc,jcn->rn", normed_late, weights3[:, :, :width_query], preferred_element_type=jnp.float32
     )
     query = rotate(head_norm(query_raw, q_norm_gain), positions).astype(jnp.bfloat16)
-    window_kv = jnp.concatenate(earlier + [joined], axis=0)
-    window_extent = window_kv.shape[0]
+    window_keys = jnp.concatenate(earlier_keys + [key], axis=0)
+    window_values = jnp.concatenate(earlier_values + [value_rows], axis=0)
+    window_extent = window_keys.shape[0]
     key_pos = (tok_index - reach) * rows + jnp.arange(window_extent, dtype=jnp.int32)
     kv_heads = width_kv // HEAD_SIZE
     query_group_count = width_query // HEAD_SIZE // kv_heads
     query_four_axes = query.reshape(rows, kv_heads, query_group_count, HEAD_SIZE)
-    keys_three_axes = window_kv[:, :width_kv].reshape(window_extent, kv_heads, HEAD_SIZE)
-    values_three_axes = window_kv[:, width_kv:].reshape(window_extent, kv_heads, HEAD_SIZE)
+    keys_three_axes = window_keys.reshape(window_extent, kv_heads, HEAD_SIZE)
+    values_three_axes = window_values.reshape(window_extent, kv_heads, HEAD_SIZE)
     scores = (
         jnp.einsum(
             "tkgd,skd->kgts", query_four_axes, keys_three_axes, preferred_element_type=jnp.float32

time: 241 us -> 229 us (0.950)
  waiting for transfers between devices: 123 us -> 110 us
  starting transfers between devices: 31.7 us -> 37.7 us
  matrix products: 34.8 us -> 31.2 us
    ppermute x2 -> x4, waiting for transfers between devices: 24.9 us -> 9.23 us  [shifted(): lax.ppermute(value, axis, [(source, source + steps) for source in range(l...]
    ppermute x2 -> x4, starting transfers between devices: 7.59 us -> 13.5 us  [shifted(): lax.ppermute(value, axis, [(source, source + steps) for source in range(l...]
    dot_general x1, matrix products: 8.64 us -> 4.95 us  [local(): jnp.dot(heads_out, w_out, preferred_element_type=jnp.float32)]
    ppermute x7, waiting for transfers between devices: 33.8 us -> 36.3 us  [local(): lax.ppermute(with_gain, 'hid', [(i, (i + k) % n_hid) for i in range(n_hid)])]
    unnamed x12 -> x16, local copies, waits for them, and re-layouts: 10.6 us -> 10.6 us
  transfers between devices with their start and end apart: 11 -> 13, of which waited for: 8 -> 9; matrix products, arithmetic and copies ran while one was open for 17% -> 21% of each run, Pallas kernels for 0% -> 0%
where the time goes in v7:
time: 229 us; the launch traced here: 228 us
  waiting for transfers between devices  110 us (48%)
  starting transfers between devices  37.7 us (16%)
  matrix products  31.2 us (14%)
  local copies, waits for them, and re-layouts  18.1 us (8%)
  other arithmetic  17.3 us (8%)
  between operations  13.7 us (6%)
    reduce_scatter x1, waiting for transfers between devices, local(): lax.psum_scatter(partial_value.astype(jnp.bfloat16), 'hid', scatter_dimen...  42.2 us
    ppermute x7, waiting for transfers between devices, local(): lax.ppermute(with_gain, 'hid', [(i, (i + k) % n_hid) for i in range(n_hid)])  36.3 us
    ppermute x7, starting transfers between devices, local(): lax.ppermute(with_gain, 'hid', [(i, (i + k) % n_hid) for i in range(n_hid)])  24.1 us
    all_gather x1, waiting for transfers between devices, local(): lax.all_gather(jnp.concatenate([w_query, w_key, value_matrix], axis=1), '...  22.4 us
    ppermute x4, starting transfers between devices, shifted(): lax.ppermute(value, axis, [(source, source + steps) for source in range(l...  13.5 us
    unnamed x16, local copies, waits for them, and re-layouts  10.6 us
    ppermute x4, waiting for transfers between devices, shifted(): lax.ppermute(value, axis, [(source, source + steps) for source in range(l...  9.23 us
    sub x1, matrix products, local(): weights = jnp.where(allowed, jnp.exp(masked - top), 0.0)  8.49 us
  transfers between devices with their start and end apart: 13, of which 9 were waited for; matrix products, arithmetic and copies ran while one was open for 21% of the time, Pallas kernels for 0%

profile of v7, /device:TPU:2, one launch (start us, length us, event | category | flops | bytes accessed | tf_op | source)
XLA Modules:
  0.0 228.1 jit_solution(16565904309670403537)
XLA Ops:
  6.5 1.8 pad_maximum_fusion.4
  8.4 1.4 copy.18
  9.8 0.8 pad_maximum_fusion
  10.6 1.7 collective-permute-start.1
  12.2 2.2 collective-permute-start.2
  14.4 1.8 collective-permute-start.3
  16.3 1.8 collective-permute-start.4
  18.2 0.5 multiply_cosine_fusion
  18.7 0.7 bitcast_convert_fusion.1
  19.4 1.6 bitcast_dynamic-update-slice_fusion.7
  21.0 10.3 %collective-permute-done = bf16[513,672]{1,0:T(8,128)(2,1)} collective-permute-done((bf16[513,672]{1,0:T(8,128)(2,1)S(1)}, bf16[513,672]{1,0:T(8,128)(2,1)}, u32[]{:S(2)}, u32[]{:S(2)}) %collective-permute-start) | collective-permute-done | bytes 689504 | tf_op jit(solution)/shard_map/ppermute | solution.py:53
  31.3 1.8 collective-permute-start.5
  33.1 2.1 bitcast_dynamic-update-slice_fusion.6
  35.2 14.7 %collective-permute-start.6 = (bf16[513,672]{1,0:T(8,128)(2,1)S(1)}, bf16[513,672]{1,0:T(8,128)(2,1)S(1)}, u32[]{:S(2)}, u32[]{:S(2)}) collective-permute-start(bf16[513,672]{1,0:T(8,128)(2,1)S(1)} %pad_maximum_fusion), channel_id=1, source_target_pairs={{0,7},{1,0},{2,1},{3,2},{4,3},{5,4},{6,5},{7,6},{8,15},{9,8},{10,9... | collective-permute-start | bytes 2068424 | tf_op jit(solution)/shard_map/ppermute | solution.py:53
  49.9 2.1 bitcast_dynamic-update-slice_fusion.5
  52.1 14.7 %collective-permute-done.2 = bf16[513,672]{1,0:T(8,128)(2,1)} collective-permute-done((bf16[513,672]{1,0:T(8,128)(2,1)S(1)}, bf16[513,672]{1,0:T(8,128)(2,1)}, u32[]{:S(2)}, u32[]{:S(2)}) %collective-permute-start.2) | collective-permute-done | bytes 689504 | tf_op jit(solution)/shard_map/ppermute | solution.py:53
  66.8 2.1 bitcast_dynamic-update-slice_fusion.4
  68.9 0.9 bitcast_dynamic-update-slice_fusion.3
  69.8 11.3 %collective-permute-done.4 = bf16[513,672]{1,0:T(8,128)(2,1)S(1)} collective-permute-done((bf16[513,672]{1,0:T(8,128)(2,1)S(1)}, bf16[513,672]{1,0:T(8,128)(2,1)S(1)}, u32[]{:S(2)}, u32[]{:S(2)}) %collective-permute-start.4) | collective-permute-done | bytes 689504 | tf_op jit(solution)/shard_map/ppermute | solution.py:53
  81.1 1.0 bitcast_dynamic-update-slice_fusion.2
  82.1 1.0 bitcast_dynamic-update-slice_fusion.1
  83.1 0.1 collective-permute-done.6
  83.1 1.0 bitcast_dynamic-update-slice_fusion
  84.1 6.5 %gather_fusion = bf16[8,513,672]{2,1,0:T(8,128)(2,1)} fusion(bf16[8,513,672]{2,1,0:T(8,128)(2,1)} %bitcast_dynamic-update-slice_fusion, s32[1024]{0:T(1024)S(1)} %pad_clamp_fusion), kind=kCustom, calls=%fused_computation | custom fusion | bytes 11031584 | tf_op jit(solution)/shard_map/jit(_take)/gather | solution.py:57
  90.6 3.7 %broadcast_select_fusion = bf16[8,513,672]{2,1,0:T(8,128)(2,1)S(1)} fusion(bf16[8,513,672]{2,1,0:T(8,128)(2,1)} %gather_fusion, pred[8]{0:T(512)(128)(4,1)S(1)} %compare_and_fusion), kind=kLoop, calls=%fused_computation.11 | loop fusion | flops 2757888 | bytes 11031560 | tf_op jit(solution)/shard_map/jit(_take)/select_n | solution.py:57
  94.3 1.4 fusion.1
  95.7 4.7 %fusion.3 = bf16[8,512,672]{2,1,0:T(8,128)(2,1)} fusion(f32[8,672]{1,0:T(8,128)S(1)} %bitcast.86, f32[512]{0:T(512)S(1)} %add_rsqrt_fusion.2, bf16[8,513,672]{2,1,0:T(8,128)(2,1)S(1)} %broadcast_select_fusion), kind=kLoop, calls=%fused_computation.6 | loop fusion | flops 11010048 | bytes 11033600 | tf_op jit(solution)/shard_map/convert_element_type | solution.py:62
  100.4 22.4 %all-gather.2.cloned.1.call-done = bf16[5376,1024]{1,0:T(8,128)(2,1)} async-done(((bf16[168,1024]{1,0:T(8,128)(2,1)}), bf16[5376,1024]{1,0:T(8,128)(2,1)}) %all-gather.2.cloned.1.call-update) | async-done | bytes 11010064 | tf_op jit(solution)/shard_map/all_gather | solution.py:65
  122.7 8.3 %fusion.14 = f32[512,512]{0,1:T(8,128)S(1)} fusion(bf16[8,512,672]{2,1,0:T(8,128)(2,1)} %fusion.3, bf16[8,672,1024]{2,1,0:T(8,128)(2,1)} %bitcast.87), kind=kOutput, calls=%fused_computation.22 | convolution fusion | flops 2818572288 | bytes 12845056 | tf_op jit(solution)/shard_map/jrc,jcn->rn/dot_general | solution.py:69
  131.1 0.1 multiply_reduce_fusion.1
  131.2 0.1 multiply_multiply_fusion.1
  131.3 0.1 subtract_convert_fusion.1
  131.4 2.7 %collective-permute-start.9 = (bf16[512,256]{0,1:T(8,128)(2,1)S(1)}, bf16[512,256]{0,1:T(8,128)(2,1)S(1)}, u32[]{:S(2)}, u32[]{:S(2)}) collective-permute-start(bf16[512,256]{0,1:T(8,128)(2,1)S(1)} %bitcast.80), channel_id=1, source_target_pairs={{0,16},{8,24},{16,32},{24,40},{32,48},{40,56},{48,64},{56,72},{64,... | collective-permute-start | bytes 786440 | tf_op jit(solution)/shard_map/ppermute | solution.py:18
  134.1 1.1 and_and_fusion
  135.3 4.7 %collective-permute-start.10 = (bf16[512,256]{0,1:T(8,128)(2,1)S(1)}, bf16[512,256]{0,1:T(8,128)(2,1)S(1)}, u32[]{:S(2)}, u32[]{:S(2)}) collective-permute-start(bf16[512,256]{0,1:T(8,128)(2,1)S(1)} %bitcast.81), channel_id=1, source_target_pairs={{0,8},{8,16},{16,24},{24,32},{32,40},{40,48},{48,56},{56,64},{64,7... | collective-permute-start | bytes 786440 | tf_op jit(solution)/shard_map/ppermute | solution.py:18
  140.0 3.4 %collective-permute-start.7 = (bf16[512,256]{0,1:T(8,128)(2,1)S(1)}, bf16[512,256]{0,1:T(8,128)(2,1)S(1)}, u32[]{:S(2)}, u32[]{:S(2)}) collective-permute-start(bf16[512,256]{0,1:T(8,128)(2,1)S(1)} %slice.73), channel_id=1, source_target_pairs={{0,16},{8,24},{16,32},{24,40},{32,48},{40,56},{48,64},{56,72},{64,... | collective-permute-start | bytes 786440 | tf_op jit(solution)/shard_map/ppermute | solution.py:18
  143.4 2.8 %collective-permute-start.8 = (bf16[512,256]{0,1:T(8,128)(2,1)S(1)}, bf16[512,256]{0,1:T(8,128)(2,1)S(1)}, u32[]{:S(2)}, u32[]{:S(2)}) collective-permute-start(bf16[512,256]{0,1:T(8,128)(2,1)S(1)} %slice.73), channel_id=1, source_target_pairs={{0,8},{8,16},{16,24},{24,32},{32,40},{40,48},{48,56},{56,64},{64,7... | collective-permute-start | bytes 786440 | tf_op jit(solution)/shard_map/ppermute | solution.py:18
  146.2 4.1 %collective-permute-done.9 = bf16[512,256]{0,1:T(8,128)(2,1)S(1)} collective-permute-done((bf16[512,256]{0,1:T(8,128)(2,1)S(1)}, bf16[512,256]{0,1:T(8,128)(2,1)S(1)}, u32[]{:S(2)}, u32[]{:S(2)}) %collective-permute-start.9) | collective-permute-done | bytes 262176 | tf_op jit(solution)/shard_map/ppermute | solution.py:18
  150.2 5.5 %fusion.10 = f32[512,512,1]{0,1,2:T(8,128)S(1)} fusion(bf16[8,512,672]{2,1,0:T(8,128)(2,1)S(1)} %copy-done, bf16[8,672,1024]{2,1,0:T(8,128)(2,1)} %bitcast.88), kind=kOutput, calls=%fused_computation.17 | convolution fusion | flops 2818572288 | bytes 12058624 | tf_op jit(solution)/shard_map/jrc,jcn->rn/dot_general | solution.py:82
  155.8 0.1 multiply_reduce_fusion
  155.9 0.2 multiply_multiply_fusion
  156.1 0.2 subtract_convert_fusion
  156.4 8.5 %fusion.35 = (f32[2,2,512]{2,1,0:T(2,128)S(1)}, bf16[2,2,512,1536]{2,3,1,0:T(8,128)(2,1)}) fusion(pred[512,1536]{0,1:T(8,128)(4,1)S(1)} %and_and_fusion, bf16[1536,2,128,1]{0,2,3,1:T(8,128)(2,1)S(1)} %bitcast.83, bf16[512,2,2,128]{0,3,2,1:T(8,128)(2,1)S(1)} %bitcast.85), kind=kOutput, calls=%fused_computation.80 | convolution fusion | flops 824182272 | bytes 8396800 | tf_op jit(solution)/shard_map/sub | solution.py:108
  164.9 2.2 collective-permute-done.7
  167.1 3.0 %collective-permute-done.8 = bf16[512,256]{0,1:T(8,128)(2,1)S(1)} collective-permute-done((bf16[512,256]{0,1:T(8,128)(2,1)S(1)}, bf16[512,256]{0,1:T(8,128)(2,1)S(1)}, u32[]{:S(2)}, u32[]{:S(2)}) %collective-permute-start.8) | collective-permute-done | bytes 262176 | tf_op jit(solution)/shard_map/ppermute | solution.py:18
  170.1 3.9 %fusion.25 = bf16[512,2,2,128]{0,3,2,1:T(8,128)(2,1)S(1)} fusion(bf16[1536,2,128,1]{0,2,3,1:T(8,128)(2,1)S(1)} %bitcast.84, bf16[2,2,512,1536]{2,3,1,0:T(8,128)(2,1)} %get-tuple-element.14, f32[512,2,2]{0,2,1:T(2,128)S(1)} %bitcast.92), kind=kOutput, calls=%fused_computation.26 | convolution fusion | flops 805830656 | bytes 7610368 | tf_op jit(solution)/shard_map/kgts,skd->tkgd/dot_general | solution.py:111
  174.0 5.0 %convolution_convert_fusion = bf16[512,5376]{0,1:T(8,128)(2,1)} fusion(bf16[512,512]{0,1:T(8,128)(2,1)S(1)} %bitcast.91, bf16[512,5376]{1,0:T(8,128)(2,1)S(1)} %bitcast.90), kind=kOutput, calls=%fused_computation.10 | convolution fusion | flops 2821324800 | bytes 11534336 | tf_op jit(solution)/shard_map/dot_general | solution.py:116
  179.0 42.2 %reduce-scatter.2.cloned.1.call-done = bf16[512,672]{0,1:T(8,128)(2,1)} async-done(((bf16[512,5376]{0,1:T(8,128)(2,1)}), bf16[512,672]{0,1:T(8,128)(2,1)}) %reduce-scatter.2.cloned.1.call-update) | async-done | bytes 688144 | tf_op jit(solution)/shard_map/reduce_scatter | solution.py:117
  (37 shorter events, 0.4 us)
Async XLA Ops:
  6.5 116.2 %all-gather.2.cloned.1.call-start = ((), (), s32[]{:S(2)}) async-start(), calls=%async_computation.1 | async-start | bytes 11354112 | tf_op jit(solution)/shard_map/all_gather | solution.py:65
  8.3 212.9 %reduce-scatter.2.cloned.1.call-start = ((), (), s32[]{:S(2)}) async-start(), calls=%async_computation.2 | async-start | bytes 6193152 | tf_op jit(solution)/shard_map/reduce_scatter | solution.py:117
  10.5 20.8 %collective-permute-start = (bf16[513,672]{1,0:T(8,128)(2,1)S(1)}, bf16[513,672]{1,0:T(8,128)(2,1)}, u32[]{:S(2)}, u32[]{:S(2)}) collective-permute-start(bf16[513,672]{1,0:T(8,128)(2,1)S(1)} %pad_maximum_fusion), channel_id=1, source_target_pairs={{0,1},{1,2},{2,3},{3,4},{4,5},{5,6},{6,7},{7,0},{8,9},{9,10},{10,1... | collective-permute-start | bytes 2068424 | tf_op jit(solution)/shard_map/ppermute | solution.py:53
  10.6 24.6 %collective-permute-start.1 = (bf16[513,672]{1,0:T(8,128)(2,1)S(1)}, bf16[513,672]{1,0:T(8,128)(2,1)}, u32[]{:S(2)}, u32[]{:S(2)}) collective-permute-start(bf16[513,672]{1,0:T(8,128)(2,1)S(1)} %pad_maximum_fusion), channel_id=1, source_target_pairs={{0,2},{1,3},{2,4},{3,5},{4,6},{5,7},{6,0},{7,1},{8,10},{9,11},{10,... | collective-permute-start | bytes 2068424 | tf_op jit(solution)/shard_map/ppermute | solution.py:53
  12.2 54.6 %collective-permute-start.2 = (bf16[513,672]{1,0:T(8,128)(2,1)S(1)}, bf16[513,672]{1,0:T(8,128)(2,1)}, u32[]{:S(2)}, u32[]{:S(2)}) collective-permute-start(bf16[513,672]{1,0:T(8,128)(2,1)S(1)} %pad_maximum_fusion), channel_id=1, source_target_pairs={{0,3},{1,4},{2,5},{3,6},{4,7},{5,0},{6,1},{7,2},{8,11},{9,12},{10,... | collective-permute-start | bytes 2068424 | tf_op jit(solution)/shard_map/ppermute | solution.py:53
  14.4 54.4 %collective-permute-start.3 = (bf16[513,672]{1,0:T(8,128)(2,1)S(1)}, bf16[513,672]{1,0:T(8,128)(2,1)S(1)}, u32[]{:S(2)}, u32[]{:S(2)}) collective-permute-start(bf16[513,672]{1,0:T(8,128)(2,1)S(1)} %pad_maximum_fusion), channel_id=1, source_target_pairs={{0,4},{1,5},{2,6},{3,7},{4,0},{5,1},{6,2},{7,3},{8,12},{9,13},{10,... | collective-permute-start | bytes 2068424 | tf_op jit(solution)/shard_map/ppermute | solution.py:53
  16.3 64.9 %collective-permute-start.4 = (bf16[513,672]{1,0:T(8,128)(2,1)S(1)}, bf16[513,672]{1,0:T(8,128)(2,1)S(1)}, u32[]{:S(2)}, u32[]{:S(2)}) collective-permute-start(bf16[513,672]{1,0:T(8,128)(2,1)S(1)} %pad_maximum_fusion), channel_id=1, source_target_pairs={{0,5},{1,6},{2,7},{3,0},{4,1},{5,2},{6,3},{7,4},{8,13},{9,14},{10,... | collective-permute-start | bytes 2068424 | tf_op jit(solution)/shard_map/ppermute | solution.py:53
  31.3 50.8 %collective-permute-start.5 = (bf16[513,672]{1,0:T(8,128)(2,1)S(1)}, bf16[513,672]{1,0:T(8,128)(2,1)S(1)}, u32[]{:S(2)}, u32[]{:S(2)}) collective-permute-start(bf16[513,672]{1,0:T(8,128)(2,1)S(1)} %pad_maximum_fusion), channel_id=1, source_target_pairs={{0,6},{1,7},{2,0},{3,1},{4,2},{5,3},{6,4},{7,5},{8,14},{9,15},{10,... | collective-permute-start | bytes 2068424 | tf_op jit(solution)/shard_map/ppermute | solution.py:53
  35.2 47.9 %collective-permute-start.6 = (bf16[513,672]{1,0:T(8,128)(2,1)S(1)}, bf16[513,672]{1,0:T(8,128)(2,1)S(1)}, u32[]{:S(2)}, u32[]{:S(2)}) collective-permute-start(bf16[513,672]{1,0:T(8,128)(2,1)S(1)} %pad_maximum_fusion), channel_id=1, source_target_pairs={{0,7},{1,0},{2,1},{3,2},{4,3},{5,4},{6,5},{7,6},{8,15},{9,8},{10,9... | collective-permute-start | bytes 2068424 | tf_op jit(solution)/shard_map/ppermute | solution.py:53
  122.7 12.5 %copy-start.1 = (bf16[1,128]{1,0:T(2,128)(2,1)S(1)}, bf16[1,128]{1,0:T(2,128)(2,1)}, u32[]{:S(2)}) copy-start(bf16[1,128]{1,0:T(2,128)(2,1)} %param.13) | copy-start | bytes 772
  122.7 27.5 %copy-start = (bf16[8,512,672]{2,1,0:T(8,128)(2,1)S(1)}, bf16[8,512,672]{2,1,0:T(8,128)(2,1)}, u32[]{:S(2)}) copy-start(bf16[8,512,672]{2,1,0:T(8,128)(2,1)} %fusion.3) | copy-start | bytes 16515076
  131.4 18.8 %collective-permute-start.9 = (bf16[512,256]{0,1:T(8,128)(2,1)S(1)}, bf16[512,256]{0,1:T(8,128)(2,1)S(1)}, u32[]{:S(2)}, u32[]{:S(2)}) collective-permute-start(bf16[512,256]{0,1:T(8,128)(2,1)S(1)} %bitcast.80), channel_id=1, source_target_pairs={{0,16},{8,24},{16,32},{24,40},{32,48},{40,56},{48,64},{56,72},{64,... | collective-permute-start | bytes 786440 | tf_op jit(solution)/shard_map/ppermute | solution.py:18
  135.3 21.1 %collective-permute-start.10 = (bf16[512,256]{0,1:T(8,128)(2,1)S(1)}, bf16[512,256]{0,1:T(8,128)(2,1)S(1)}, u32[]{:S(2)}, u32[]{:S(2)}) collective-permute-start(bf16[512,256]{0,1:T(8,128)(2,1)S(1)} %bitcast.81), channel_id=1, source_target_pairs={{0,8},{8,16},{16,24},{24,32},{32,40},{40,48},{48,56},{56,64},{64,7... | collective-permute-start | bytes 786440 | tf_op jit(solution)/shard_map/ppermute | solution.py:18
  140.0 27.1 %collective-permute-start.7 = (bf16[512,256]{0,1:T(8,128)(2,1)S(1)}, bf16[512,256]{0,1:T(8,128)(2,1)S(1)}, u32[]{:S(2)}, u32[]{:S(2)}) collective-permute-start(bf16[512,256]{0,1:T(8,128)(2,1)S(1)} %slice.73), channel_id=1, source_target_pairs={{0,16},{8,24},{16,32},{24,40},{32,48},{40,56},{48,64},{56,72},{64,... | collective-permute-start | bytes 786440 | tf_op jit(solution)/shard_map/ppermute | solution.py:18
  143.4 26.7 %collective-permute-start.8 = (bf16[512,256]{0,1:T(8,128)(2,1)S(1)}, bf16[512,256]{0,1:T(8,128)(2,1)S(1)}, u32[]{:S(2)}, u32[]{:S(2)}) collective-permute-start(bf16[512,256]{0,1:T(8,128)(2,1)S(1)} %slice.73), channel_id=1, source_target_pairs={{0,8},{8,16},{16,24},{24,32},{32,40},{40,48},{48,56},{56,64},{64,7... | collective-permute-start | bytes 786440 | tf_op jit(solution)/shard_map/ppermute | solution.py:18
  164.9 9.1 %slice-start = ((s8[5505024]{0:T(1024)(128)(4,1)}), s8[4194304]{0:T(1024)(128)(4,1)S(1)}, s32[]{:S(2)}) async-start(s8[5505024]{0:T(1024)(128)(4,1)} %bitcast.89), calls=%async_computation.3 | async-start | bytes 8388608
  170.1 3.9 %slice-start.1 = ((s8[5505024]{0:T(1024)(128)(4,1)}), s8[1310720]{0:T(1024)(128)(4,1)S(1)}, s32[]{:S(2)}) async-start(s8[5505024]{0:T(1024)(128)(4,1)} %bitcast.89), calls=%async_computation.4 | async-start | bytes 2621440
Sparse Core Ops, SparseCore 0:
  9.9 112.7 all-gather.1
  179.1 42.0 reduce-scatter.1

commit v8 on v7

--- a/solution.py
+++ b/solution.py
@@ -66,19 +66,27 @@
         jnp.concatenate([w_query, w_key, value_matrix], axis=1), "tok", axis=0, tiled=True
     )
     weights3 = stacked.reshape(n_hid, normed.shape[2], stacked.shape[1])
-    projected_kv = jnp.einsum(
-        "jrc,jcn->rn", normed, weights3[:, :, width_query:], preferred_element_type=jnp.float32
-    )
-    key_raw = projected_kv[:, :width_kv]
-    value_raw = projected_kv[:, width_kv:]
     tok_index = lax.axis_index("tok")
     positions = tok_index * rows + jnp.arange(rows, dtype=jnp.int32)
+    reach = (WINDOW - 1 + rows - 1) // rows
+    key_raw = jnp.einsum(
+        "jrc,jcn->rn",
+        normed,
+        weights3[:, :, width_query : width_query + width_kv],
+        preferred_element_type=jnp.float32,
+    )
     key = rotate(head_norm(key_raw, k_norm_gain), positions).astype(jnp.bfloat16)
+    earlier_keys = [shifted(key, "tok", offset) for offset in range(reach, 0, -1)]
+    normed_mid, _ = lax.optimization_barrier((normed, earlier_keys[0]))
+    value_raw = jnp.einsum(
+        "jrc,jcn->rn",
+        normed_mid,
+        weights3[:, :, width_query + width_kv :],
+        preferred_element_type=jnp.float32,
+    )
     value_rows = value_raw.astype(jnp.bfloat16)
-    reach = (WINDOW - 1 + rows - 1) // rows
-    earlier_keys = [shifted(key, "tok", offset) for offset in range(reach, 0, -1)]
     earlier_values = [shifted(value_rows, "tok", offset) for offset in range(reach, 0, -1)]
-    normed_late, _ = lax.optimization_barrier((normed, earlier_keys[0]))
+    normed_late, _ = lax.optimization_barrier((normed_mid, earlier_values[0]))
     query_raw = jnp.einsum(
         "jrc,jcn->rn", normed_late, weights3[:, :, :width_query], preferred_element_type=jnp.float32
     )

time: 229 us -> 245 us (1.070)
  waiting for transfers between devices: 110 us -> 123 us
  matrix products: 31.2 us -> 35.6 us
    ppermute x4, waiting for transfers between devices: 9.23 us -> 22.7 us  [shifted(): lax.ppermute(value, axis, [(source, source + steps) for source in range(l...]
    dot_general x1, matrix products: 4.95 us -> 8.63 us  [local(): jnp.dot(heads_out, w_out, preferred_element_type=jnp.float32)]
    dot_general x1 -> x2, matrix products: 8.34 us -> 9.17 us  [the longest x1 5.58 us: local(): jnp.einsum('jrc,jcn->rn', normed, weights3[:, :, width_query:width_query...]
    unnamed x16 -> x14, local copies, waits for them, and re-layouts: 10.6 us -> 10.6 us
  transfers between devices with their start and end apart: 13 -> 13, of which waited for: 9 -> 8; matrix products, arithmetic and copies ran while one was open for 21% -> 17% of each run, Pallas kernels for 0% -> 0%
where the time goes in v8:
time: 245 us; the launch traced here: 244 us
  waiting for transfers between devices  123 us (50%)
  starting transfers between devices  35.9 us (15%)
  matrix products  35.6 us (15%)
  local copies, waits for them, and re-layouts  19.3 us (8%)
  other arithmetic  17.3 us (7%)
  between operations  13.7 us (6%)
    reduce_scatter x1, waiting for transfers between devices, local(): lax.psum_scatter(partial_value.astype(jnp.bfloat16), 'hid', scatter_dimen...  41.3 us
    ppermute x7, waiting for transfers between devices, local(): lax.ppermute(with_gain, 'hid', [(i, (i + k) % n_hid) for i in range(n_hid)])  36.3 us
    ppermute x7, starting transfers between devices, local(): lax.ppermute(with_gain, 'hid', [(i, (i + k) % n_hid) for i in range(n_hid)])  24.1 us
    ppermute x4, waiting for transfers between devices, shifted(): lax.ppermute(value, axis, [(source, source + steps) for source in range(l...  22.7 us
    all_gather x1, waiting for transfers between devices, local(): lax.all_gather(jnp.concatenate([w_query, w_key, value_matrix], axis=1), '...  22.4 us
    ppermute x4, starting transfers between devices, shifted(): lax.ppermute(value, axis, [(source, source + steps) for source in range(l...  11.8 us
    unnamed x14, local copies, waits for them, and re-layouts  10.6 us
    dot_general x1, matrix products, local(): jnp.dot(heads_out, w_out, preferred_element_type=jnp.float32)  8.63 us
  transfers between devices with their start and end apart: 13, of which 8 were waited for; matrix products, arithmetic and copies ran while one was open for 17% of the time, Pallas kernels for 0%

profile of v8, /device:TPU:2, one launch (start us, length us, event | category | flops | bytes accessed | tf_op | source)
XLA Modules:
  0.0 244.4 jit_solution(1376296068514875816)
XLA Ops:
  6.5 1.8 pad_maximum_fusion.4
  8.4 1.4 copy.21
  9.8 0.8 pad_maximum_fusion
  10.6 1.7 collective-permute-start.1
  12.2 2.2 collective-permute-start.2
  14.4 1.8 collective-permute-start.3
  16.3 1.8 collective-permute-start.4
  18.2 0.5 multiply_cosine_fusion
  18.7 0.7 bitcast_convert_fusion.1
  19.4 1.7 bitcast_dynamic-update-slice_fusion.7
  21.0 10.2 %collective-permute-done = bf16[513,672]{1,0:T(8,128)(2,1)} collective-permute-done((bf16[513,672]{1,0:T(8,128)(2,1)S(1)}, bf16[513,672]{1,0:T(8,128)(2,1)}, u32[]{:S(2)}, u32[]{:S(2)}) %collective-permute-start) | collective-permute-done | bytes 689504 | tf_op jit(solution)/shard_map/ppermute | solution.py:53
  31.3 1.8 collective-permute-start.5
  33.1 2.1 bitcast_dynamic-update-slice_fusion.6
  35.2 14.7 %collective-permute-start.6 = (bf16[513,672]{1,0:T(8,128)(2,1)S(1)}, bf16[513,672]{1,0:T(8,128)(2,1)S(1)}, u32[]{:S(2)}, u32[]{:S(2)}) collective-permute-start(bf16[513,672]{1,0:T(8,128)(2,1)S(1)} %pad_maximum_fusion), channel_id=1, source_target_pairs={{0,7},{1,0},{2,1},{3,2},{4,3},{5,4},{6,5},{7,6},{8,15},{9,8},{10,9... | collective-permute-start | bytes 2068424 | tf_op jit(solution)/shard_map/ppermute | solution.py:53
  49.9 2.1 bitcast_dynamic-update-slice_fusion.5
  52.1 14.7 %collective-permute-done.2 = bf16[513,672]{1,0:T(8,128)(2,1)} collective-permute-done((bf16[513,672]{1,0:T(8,128)(2,1)S(1)}, bf16[513,672]{1,0:T(8,128)(2,1)}, u32[]{:S(2)}, u32[]{:S(2)}) %collective-permute-start.2) | collective-permute-done | bytes 689504 | tf_op jit(solution)/shard_map/ppermute | solution.py:53
  66.8 2.1 bitcast_dynamic-update-slice_fusion.4
  68.9 1.0 bitcast_dynamic-update-slice_fusion.3
  69.8 11.3 %collective-permute-done.4 = bf16[513,672]{1,0:T(8,128)(2,1)S(1)} collective-permute-done((bf16[513,672]{1,0:T(8,128)(2,1)S(1)}, bf16[513,672]{1,0:T(8,128)(2,1)S(1)}, u32[]{:S(2)}, u32[]{:S(2)}) %collective-permute-start.4) | collective-permute-done | bytes 689504 | tf_op jit(solution)/shard_map/ppermute | solution.py:53
  81.1 1.0 bitcast_dynamic-update-slice_fusion.2
  82.1 1.0 bitcast_dynamic-update-slice_fusion.1
  83.1 0.9 bitcast_dynamic-update-slice_fusion
  84.1 6.5 %gather_fusion = bf16[8,513,672]{2,1,0:T(8,128)(2,1)} fusion(bf16[8,513,672]{2,1,0:T(8,128)(2,1)} %bitcast_dynamic-update-slice_fusion, s32[1024]{0:T(1024)S(1)} %pad_clamp_fusion), kind=kCustom, calls=%fused_computation | custom fusion | bytes 11031584 | tf_op jit(solution)/shard_map/jit(_take)/gather | solution.py:57
  90.6 3.7 %broadcast_select_fusion = bf16[8,513,672]{2,1,0:T(8,128)(2,1)S(1)} fusion(bf16[8,513,672]{2,1,0:T(8,128)(2,1)} %gather_fusion, pred[8]{0:T(512)(128)(4,1)S(1)} %compare_and_fusion), kind=kLoop, calls=%fused_computation.11 | loop fusion | flops 2757888 | bytes 11031560 | tf_op jit(solution)/shard_map/jit(_take)/select_n | solution.py:57
  94.3 1.4 fusion.1
  95.7 4.7 %fusion.3 = bf16[8,512,672]{2,1,0:T(8,128)(2,1)} fusion(f32[8,672]{1,0:T(8,128)S(1)} %bitcast.91, f32[512]{0:T(512)S(1)} %add_rsqrt_fusion.2, bf16[8,513,672]{2,1,0:T(8,128)(2,1)S(1)} %broadcast_select_fusion), kind=kLoop, calls=%fused_computation.6 | loop fusion | flops 11010048 | bytes 11033600 | tf_op jit(solution)/shard_map/convert_element_type | solution.py:62
  100.4 22.4 %all-gather.2.cloned.1.call-done = bf16[5376,1024]{1,0:T(8,128)(2,1)} async-done(((bf16[168,1024]{1,0:T(8,128)(2,1)}), bf16[5376,1024]{1,0:T(8,128)(2,1)}) %all-gather.2.cloned.1.call-update) | async-done | bytes 11010064 | tf_op jit(solution)/shard_map/all_gather | solution.py:65
  122.7 5.6 %fusion.14 = f32[512,256,1]{0,1,2:T(8,128)S(1)} fusion(bf16[8,512,672]{2,1,0:T(8,128)(2,1)} %fusion.3, bf16[8,672,1024]{2,1,0:T(8,128)(2,1)} %bitcast.92), kind=kOutput, calls=%fused_computation.22 | convolution fusion | flops 1409286144 | bytes 9568256 | tf_op jit(solution)/shard_map/jrc,jcn->rn/dot_general | solution.py:72
  128.3 0.1 multiply_reduce_fusion.1
  128.4 0.1 multiply_multiply_fusion.1
  128.5 0.1 subtract_convert_fusion.1
  128.6 2.7 %collective-permute-start.7 = (bf16[512,256]{0,1:T(8,128)(2,1)S(1)}, bf16[512,256]{0,1:T(8,128)(2,1)S(1)}, u32[]{:S(2)}, u32[]{:S(2)}) collective-permute-start(bf16[512,256]{0,1:T(8,128)(2,1)S(1)} %bitcast.85), channel_id=1, source_target_pairs={{0,16},{8,24},{16,32},{24,40},{32,48},{40,56},{48,64},{56,72},{64,... | collective-permute-start | bytes 786440 | tf_op jit(solution)/shard_map/ppermute | solution.py:18
  131.3 1.1 and_and_fusion
  132.5 4.7 %collective-permute-start.10 = (bf16[512,256]{0,1:T(8,128)(2,1)S(1)}, bf16[512,256]{0,1:T(8,128)(2,1)S(1)}, u32[]{:S(2)}, u32[]{:S(2)}) collective-permute-start(bf16[512,256]{0,1:T(8,128)(2,1)S(1)} %bitcast.86), channel_id=1, source_target_pairs={{0,8},{8,16},{16,24},{24,32},{32,40},{40,48},{48,56},{56,64},{64,7... | collective-permute-start | bytes 786440 | tf_op jit(solution)/shard_map/ppermute | solution.py:18
  137.2 10.3 %collective-permute-done.7 = bf16[512,256]{0,1:T(8,128)(2,1)S(1)} collective-permute-done((bf16[512,256]{0,1:T(8,128)(2,1)S(1)}, bf16[512,256]{0,1:T(8,128)(2,1)S(1)}, u32[]{:S(2)}, u32[]{:S(2)}) %collective-permute-start.7) | collective-permute-done | bytes 262176 | tf_op jit(solution)/shard_map/ppermute | solution.py:18
  147.5 3.6 %fusion.30 = bf16[512,256]{1,0:T(8,128)(2,1)S(1)} fusion(bf16[8,512,672]{2,1,0:T(8,128)(2,1)S(1)} %copy-done, bf16[8,672,1024]{2,1,0:T(8,128)(2,1)} %bitcast.93), kind=kOutput, calls=%fused_computation.29 | convolution fusion | flops 1409417216 | bytes 8519680 | tf_op jit(solution)/shard_map/jrc,jcn->rn/dot_general | solution.py:81
  151.1 1.9 collective-permute-start.8
  153.0 2.5 %collective-permute-start.9 = (bf16[512,256]{1,0:T(8,128)(2,1)S(1)}, bf16[512,256]{1,0:T(8,128)(2,1)S(1)}, u32[]{:S(2)}, u32[]{:S(2)}) collective-permute-start(bf16[512,256]{1,0:T(8,128)(2,1)S(1)} %fusion.30), channel_id=1, source_target_pairs={{0,8},{8,16},{16,24},{24,32},{32,40},{40,48},{48,56},{56,64},{64,7... | collective-permute-start | bytes 786440 | tf_op jit(solution)/shard_map/ppermute | solution.py:18
  155.7 12.4 %collective-permute-done.8 = bf16[512,256]{1,0:T(8,128)(2,1)S(1)} collective-permute-done((bf16[512,256]{1,0:T(8,128)(2,1)S(1)}, bf16[512,256]{1,0:T(8,128)(2,1)S(1)}, u32[]{:S(2)}, u32[]{:S(2)}) %collective-permute-start.8) | collective-permute-done | bytes 262176 | tf_op jit(solution)/shard_map/ppermute | solution.py:18
  168.0 5.5 %fusion.10 = f32[512,512,1]{0,1,2:T(8,128)S(1)} fusion(bf16[8,512,672]{2,1,0:T(8,128)(2,1)S(1)} %copy-done, bf16[8,672,1024]{2,1,0:T(8,128)(2,1)} %bitcast.94), kind=kOutput, calls=%fused_computation.17 | convolution fusion | flops 2818572288 | bytes 12058624 | tf_op jit(solution)/shard_map/jrc,jcn->rn/dot_general | solution.py:90
  173.6 0.1 multiply_reduce_fusion
  173.7 0.2 multiply_multiply_fusion
  173.9 0.2 subtract_convert_fusion
  174.1 1.2 copy.35
  175.4 8.5 %fusion.40 = (f32[2,2,512]{2,1,0:T(2,128)S(1)}, bf16[2,2,512,1536]{2,3,1,0:T(8,128)(2,1)}) fusion(pred[512,1536]{0,1:T(8,128)(4,1)S(1)} %and_and_fusion, bf16[1536,2,128,1]{0,2,3,1:T(8,128)(2,1)S(1)} %bitcast.88, bf16[512,2,2,128]{0,3,2,1:T(8,128)(2,1)S(1)} %bitcast.90), kind=kOutput, calls=%fused_computation.82 | convolution fusion | flops 824182272 | bytes 8396800 | tf_op jit(solution)/shard_map/sub | solution.py:116
  183.9 3.8 %fusion.24 = bf16[512,2,2,128]{0,3,2,1:T(8,128)(2,1)S(1)} fusion(bf16[1536,2,128,1]{0,2,3,1:T(8,128)(2,1)S(1)} %bitcast.89, bf16[2,2,512,1536]{2,3,1,0:T(8,128)(2,1)} %get-tuple-element.16, f32[512,2,2]{0,2,1:T(2,128)S(1)} %bitcast.96), kind=kOutput, calls=%fused_computation.27 | convolution fusion | flops 805830656 | bytes 7610368 | tf_op jit(solution)/shard_map/kgts,skd->tkgd/dot_general | solution.py:119
  187.7 8.6 %convolution_convert_fusion = bf16[512,5376]{0,1:T(8,128)(2,1)} fusion(bf16[512,512]{0,1:T(8,128)(2,1)S(1)} %bitcast.95, bf16[512,5376]{1,0:T(8,128)(2,1)} %param.15), kind=kOutput, calls=%fused_computation.10 | convolution fusion | flops 2821324800 | bytes 11534336 | tf_op jit(solution)/shard_map/dot_general | solution.py:124
  196.3 41.3 %reduce-scatter.2.cloned.1.call-done = bf16[512,672]{0,1:T(8,128)(2,1)} async-done(((bf16[512,5376]{0,1:T(8,128)(2,1)}), bf16[512,672]{0,1:T(8,128)(2,1)}) %reduce-scatter.2.cloned.1.call-update) | async-done | bytes 688144 | tf_op jit(solution)/shard_map/reduce_scatter | solution.py:125
  (35 shorter events, 0.5 us)
Async XLA Ops:
  6.5 116.2 %all-gather.2.cloned.1.call-start = ((), (), s32[]{:S(2)}) async-start(), calls=%async_computation.1 | async-start | bytes 11354112 | tf_op jit(solution)/shard_map/all_gather | solution.py:65
  8.3 229.2 %reduce-scatter.2.cloned.1.call-start = ((), (), s32[]{:S(2)}) async-start(), calls=%async_computation.2 | async-start | bytes 6193152 | tf_op jit(solution)/shard_map/reduce_scatter | solution.py:125
  10.5 20.8 %collective-permute-start = (bf16[513,672]{1,0:T(8,128)(2,1)S(1)}, bf16[513,672]{1,0:T(8,128)(2,1)}, u32[]{:S(2)}, u32[]{:S(2)}) collective-permute-start(bf16[513,672]{1,0:T(8,128)(2,1)S(1)} %pad_maximum_fusion), channel_id=1, source_target_pairs={{0,1},{1,2},{2,3},{3,4},{4,5},{5,6},{6,7},{7,0},{8,9},{9,10},{10,1... | collective-permute-start | bytes 2068424 | tf_op jit(solution)/shard_map/ppermute | solution.py:53
  10.6 24.7 %collective-permute-start.1 = (bf16[513,672]{1,0:T(8,128)(2,1)S(1)}, bf16[513,672]{1,0:T(8,128)(2,1)}, u32[]{:S(2)}, u32[]{:S(2)}) collective-permute-start(bf16[513,672]{1,0:T(8,128)(2,1)S(1)} %pad_maximum_fusion), channel_id=1, source_target_pairs={{0,2},{1,3},{2,4},{3,5},{4,6},{5,7},{6,0},{7,1},{8,10},{9,11},{10,... | collective-permute-start | bytes 2068424 | tf_op jit(solution)/shard_map/ppermute | solution.py:53
  12.2 54.6 %collective-permute-start.2 = (bf16[513,672]{1,0:T(8,128)(2,1)S(1)}, bf16[513,672]{1,0:T(8,128)(2,1)}, u32[]{:S(2)}, u32[]{:S(2)}) collective-permute-start(bf16[513,672]{1,0:T(8,128)(2,1)S(1)} %pad_maximum_fusion), channel_id=1, source_target_pairs={{0,3},{1,4},{2,5},{3,6},{4,7},{5,0},{6,1},{7,2},{8,11},{9,12},{10,... | collective-permute-start | bytes 2068424 | tf_op jit(solution)/shard_map/ppermute | solution.py:53
  14.4 54.4 %collective-permute-start.3 = (bf16[513,672]{1,0:T(8,128)(2,1)S(1)}, bf16[513,672]{1,0:T(8,128)(2,1)S(1)}, u32[]{:S(2)}, u32[]{:S(2)}) collective-permute-start(bf16[513,672]{1,0:T(8,128)(2,1)S(1)} %pad_maximum_fusion), channel_id=1, source_target_pairs={{0,4},{1,5},{2,6},{3,7},{4,0},{5,1},{6,2},{7,3},{8,12},{9,13},{10,... | collective-permute-start | bytes 2068424 | tf_op jit(solution)/shard_map/ppermute | solution.py:53
  16.3 64.9 %collective-permute-start.4 = (bf16[513,672]{1,0:T(8,128)(2,1)S(1)}, bf16[513,672]{1,0:T(8,128)(2,1)S(1)}, u32[]{:S(2)}, u32[]{:S(2)}) collective-permute-start(bf16[513,672]{1,0:T(8,128)(2,1)S(1)} %pad_maximum_fusion), channel_id=1, source_target_pairs={{0,5},{1,6},{2,7},{3,0},{4,1},{5,2},{6,3},{7,4},{8,13},{9,14},{10,... | collective-permute-start | bytes 2068424 | tf_op jit(solution)/shard_map/ppermute | solution.py:53
  31.3 50.8 %collective-permute-start.5 = (bf16[513,672]{1,0:T(8,128)(2,1)S(1)}, bf16[513,672]{1,0:T(8,128)(2,1)S(1)}, u32[]{:S(2)}, u32[]{:S(2)}) collective-permute-start(bf16[513,672]{1,0:T(8,128)(2,1)S(1)} %pad_maximum_fusion), channel_id=1, source_target_pairs={{0,6},{1,7},{2,0},{3,1},{4,2},{5,3},{6,4},{7,5},{8,14},{9,15},{10,... | collective-permute-start | bytes 2068424 | tf_op jit(solution)/shard_map/ppermute | solution.py:53
  35.2 47.9 %collective-permute-start.6 = (bf16[513,672]{1,0:T(8,128)(2,1)S(1)}, bf16[513,672]{1,0:T(8,128)(2,1)S(1)}, u32[]{:S(2)}, u32[]{:S(2)}) collective-permute-start(bf16[513,672]{1,0:T(8,128)(2,1)S(1)} %pad_maximum_fusion), channel_id=1, source_target_pairs={{0,7},{1,0},{2,1},{3,2},{4,3},{5,4},{6,5},{7,6},{8,15},{9,8},{10,9... | collective-permute-start | bytes 2068424 | tf_op jit(solution)/shard_map/ppermute | solution.py:53
  122.7 24.7 %copy-start = (bf16[8,512,672]{2,1,0:T(8,128)(2,1)S(1)}, bf16[8,512,672]{2,1,0:T(8,128)(2,1)}, u32[]{:S(2)}) copy-start(bf16[8,512,672]{2,1,0:T(8,128)(2,1)} %fusion.3) | copy-start | bytes 16515076
  128.6 18.8 %collective-permute-start.7 = (bf16[512,256]{0,1:T(8,128)(2,1)S(1)}, bf16[512,256]{0,1:T(8,128)(2,1)S(1)}, u32[]{:S(2)}, u32[]{:S(2)}) collective-permute-start(bf16[512,256]{0,1:T(8,128)(2,1)S(1)} %bitcast.85), channel_id=1, source_target_pairs={{0,16},{8,24},{16,32},{24,40},{32,48},{40,56},{48,64},{56,72},{64,... | collective-permute-start | bytes 786440 | tf_op jit(solution)/shard_map/ppermute | solution.py:18
  132.5 20.5 %copy-start.2 = (bf16[1,128]{1,0:T(2,128)(2,1)S(1)}, bf16[1,128]{1,0:T(2,128)(2,1)}, u32[]{:S(2)}) copy-start(bf16[1,128]{1,0:T(2,128)(2,1)} %param.13) | copy-start | bytes 772
  132.5 23.1 %collective-permute-start.10 = (bf16[512,256]{0,1:T(8,128)(2,1)S(1)}, bf16[512,256]{0,1:T(8,128)(2,1)S(1)}, u32[]{:S(2)}, u32[]{:S(2)}) collective-permute-start(bf16[512,256]{0,1:T(8,128)(2,1)S(1)} %bitcast.86), channel_id=1, source_target_pairs={{0,8},{8,16},{16,24},{24,32},{32,40},{40,48},{48,56},{56,64},{64,7... | collective-permute-start | bytes 786440 | tf_op jit(solution)/shard_map/ppermute | solution.py:18
  151.1 17.0 %collective-permute-start.8 = (bf16[512,256]{1,0:T(8,128)(2,1)S(1)}, bf16[512,256]{1,0:T(8,128)(2,1)S(1)}, u32[]{:S(2)}, u32[]{:S(2)}) collective-permute-start(bf16[512,256]{1,0:T(8,128)(2,1)S(1)} %fusion.30), channel_id=1, source_target_pairs={{0,16},{8,24},{16,32},{24,40},{32,48},{40,56},{48,64},{56,72},{64,... | collective-permute-start | bytes 786440 | tf_op jit(solution)/shard_map/ppermute | solution.py:18
  153.0 21.1 %collective-permute-start.9 = (bf16[512,256]{1,0:T(8,128)(2,1)S(1)}, bf16[512,256]{1,0:T(8,128)(2,1)S(1)}, u32[]{:S(2)}, u32[]{:S(2)}) collective-permute-start(bf16[512,256]{1,0:T(8,128)(2,1)S(1)} %fusion.30), channel_id=1, source_target_pairs={{0,8},{8,16},{16,24},{24,32},{32,40},{40,48},{48,56},{56,64},{64,7... | collective-permute-start | bytes 786440 | tf_op jit(solution)/shard_map/ppermute | solution.py:18
  175.4 8.5 %copy-start.1 = (bf16[1536,256]{0,1:T(8,128)(2,1)S(1)}, bf16[1536,256]{0,1:T(8,128)(2,1)}, u32[]{:S(2)}) copy-start(bf16[1536,256]{0,1:T(8,128)(2,1)} %copy.35) | copy-start | bytes 2359300
Sparse Core Ops, SparseCore 0:
  9.9 112.7 all-gather.1
  196.4 41.0 reduce-scatter.1

commit v9 on v7

--- a/solution.py
+++ b/solution.py
@@ -66,16 +66,23 @@
         jnp.concatenate([w_query, w_key, value_matrix], axis=1), "tok", axis=0, tiled=True
     )
     weights3 = stacked.reshape(n_hid, normed.shape[2], stacked.shape[1])
+    tok_index = lax.axis_index("tok")
+    positions = tok_index * rows + jnp.arange(rows, dtype=jnp.int32)
+    reach = (WINDOW - 1 + rows - 1) // rows
+    key_pos = (tok_index - reach) * rows + jnp.arange((reach + 1) * rows, dtype=jnp.int32)
+    allowed = (
+        (key_pos[None, :] <= positions[:, None])
+        & (key_pos[None, :] > positions[:, None] - WINDOW)
+        & (key_pos[None, :] >= 0)
+    )
+    allowed, normed = lax.optimization_barrier((allowed, normed))
     projected_kv = jnp.einsum(
         "jrc,jcn->rn", normed, weights3[:, :, width_query:], preferred_element_type=jnp.float32
     )
     key_raw = projected_kv[:, :width_kv]
     value_raw = projected_kv[:, width_kv:]
-    tok_index = lax.axis_index("tok")
-    positions = tok_index * rows + jnp.arange(rows, dtype=jnp.int32)
     key = rotate(head_norm(key_raw, k_norm_gain), positions).astype(jnp.bfloat16)
     value_rows = value_raw.astype(jnp.bfloat16)
-    reach = (WINDOW - 1 + rows - 1) // rows
     earlier_keys = [shifted(key, "tok", offset) for offset in range(reach, 0, -1)]
     earlier_values = [shifted(value_rows, "tok", offset) for offset in range(reach, 0, -1)]
     normed_late, _ = lax.optimization_barrier((normed, earlier_keys[0]))
@@ -86,7 +93,6 @@
     window_keys = jnp.concatenate(earlier_keys + [key], axis=0)
     window_values = jnp.concatenate(earlier_values + [value_rows], axis=0)
     window_extent = window_keys.shape[0]
-    key_pos = (tok_index - reach) * rows + jnp.arange(window_extent, dtype=jnp.int32)
     kv_heads = width_kv // HEAD_SIZE
     query_group_count = width_query // HEAD_SIZE // kv_heads
     query_four_axes = query.reshape(rows, kv_heads, query_group_count, HEAD_SIZE)
@@ -97,11 +103,6 @@
             "tkgd,skd->kgts", query_four_axes, keys_three_axes, preferred_element_type=jnp.float32
         )
         * score_scale
-    )
-    allowed = (
-        (key_pos[None, :] <= positions[:, None])
-        & (key_pos[None, :] > positions[:, None] - WINDOW)
-        & (key_pos[None, :] >= 0)
     )
     masked = jnp.where(allowed, scores, -1e30)
     top = jnp.max(masked, axis=-1, keepdims=True)

time: 229 us -> 238 us (1.039)
  waiting for transfers between devices: 110 us -> 118 us
    ppermute x4, waiting for transfers between devices: 9.23 us -> 18.9 us  [shifted(): lax.ppermute(value, axis, [(source, source + steps) for source in range(l...]
    unnamed x16 -> x18, local copies, waits for them, and re-layouts: 10.6 us -> 11 us
  transfers between devices with their start and end apart: 13 -> 13, of which waited for: 9 -> 8; matrix products, arithmetic and copies ran while one was open for 21% -> 20% of each run, Pallas kernels for 0% -> 0%
where the time goes in v9:
time: 238 us; the launch traced here: 237 us
  waiting for transfers between devices  118 us (50%)
  starting transfers between devices  37.6 us (16%)
  matrix products  31.2 us (13%)
  local copies, waits for them, and re-layouts  18.5 us (8%)
  other arithmetic  18 us (8%)
  between operations  13.7 us (6%)
    reduce_scatter x1, waiting for transfers between devices, local(): lax.psum_scatter(partial_value.astype(jnp.bfloat16), 'hid', scatter_dimen...  42.2 us
    ppermute x7, waiting for transfers between devices, local(): lax.ppermute(with_gain, 'hid', [(i, (i + k) % n_hid) for i in range(n_hid)])  34.5 us
    ppermute x7, starting transfers between devices, local(): lax.ppermute(with_gain, 'hid', [(i, (i + k) % n_hid) for i in range(n_hid)])  24.1 us
    all_gather x1, waiting for transfers between devices, local(): lax.all_gather(jnp.concatenate([w_query, w_key, value_matrix], axis=1), '...  22.4 us
    ppermute x4, waiting for transfers between devices, shifted(): lax.ppermute(value, axis, [(source, source + steps) for source in range(l...  18.9 us
    ppermute x4, starting transfers between devices, shifted(): lax.ppermute(value, axis, [(source, source + steps) for source in range(l...  13.5 us
    unnamed x18, local copies, waits for them, and re-layouts  11 us
    sub x1, matrix products, local(): weights = jnp.where(allowed, jnp.exp(masked - top), 0.0)  8.47 us
  transfers between devices with their start and end apart: 13, of which 8 were waited for; matrix products, arithmetic and copies ran while one was open for 20% of the time, Pallas kernels for 0%

profile of v9, /device:TPU:2, one launch (start us, length us, event | category | flops | bytes accessed | tf_op | source)
XLA Modules:
  0.0 237.0 jit_solution(143039951597728458)
XLA Ops:
  6.5 1.8 pad_maximum_fusion.4
  8.4 1.4 copy.18
  9.8 0.8 pad_maximum_fusion
  10.6 1.7 collective-permute-start.1
  12.2 2.2 collective-permute-start.2
  14.4 1.8 collective-permute-start.3
  16.3 1.8 collective-permute-start.4
  18.2 1.9 and_and_fusion
  20.0 0.5 multiply_cosine_fusion
  20.6 0.7 bitcast_convert_fusion.1
  21.3 1.6 bitcast_dynamic-update-slice_fusion.7
  22.9 8.4 %collective-permute-done = bf16[513,672]{1,0:T(8,128)(2,1)} collective-permute-done((bf16[513,672]{1,0:T(8,128)(2,1)S(1)}, bf16[513,672]{1,0:T(8,128)(2,1)}, u32[]{:S(2)}, u32[]{:S(2)}) %collective-permute-start) | collective-permute-done | bytes 689504 | tf_op jit(solution)/shard_map/ppermute | solution.py:53
  31.3 1.8 collective-permute-start.5
  33.1 2.1 bitcast_dynamic-update-slice_fusion.6
  35.2 14.7 %collective-permute-start.6 = (bf16[513,672]{1,0:T(8,128)(2,1)S(1)}, bf16[513,672]{1,0:T(8,128)(2,1)S(1)}, u32[]{:S(2)}, u32[]{:S(2)}) collective-permute-start(bf16[513,672]{1,0:T(8,128)(2,1)S(1)} %pad_maximum_fusion), channel_id=1, source_target_pairs={{0,7},{1,0},{2,1},{3,2},{4,3},{5,4},{6,5},{7,6},{8,15},{9,8},{10,9... | collective-permute-start | bytes 2068424 | tf_op jit(solution)/shard_map/ppermute | solution.py:53
  49.9 2.1 bitcast_dynamic-update-slice_fusion.5
  52.1 14.7 %collective-permute-done.2 = bf16[513,672]{1,0:T(8,128)(2,1)} collective-permute-done((bf16[513,672]{1,0:T(8,128)(2,1)S(1)}, bf16[513,672]{1,0:T(8,128)(2,1)}, u32[]{:S(2)}, u32[]{:S(2)}) %collective-permute-start.2) | collective-permute-done | bytes 689504 | tf_op jit(solution)/shard_map/ppermute | solution.py:53
  66.8 2.1 bitcast_dynamic-update-slice_fusion.4
  68.8 1.0 bitcast_dynamic-update-slice_fusion.3
  69.8 11.3 %collective-permute-done.4 = bf16[513,672]{1,0:T(8,128)(2,1)S(1)} collective-permute-done((bf16[513,672]{1,0:T(8,128)(2,1)S(1)}, bf16[513,672]{1,0:T(8,128)(2,1)S(1)}, u32[]{:S(2)}, u32[]{:S(2)}) %collective-permute-start.4) | collective-permute-done | bytes 689504 | tf_op jit(solution)/shard_map/ppermute | solution.py:53
  81.1 1.0 bitcast_dynamic-update-slice_fusion.2
  82.1 1.0 bitcast_dynamic-update-slice_fusion.1
  83.1 0.1 collective-permute-done.6
  83.1 0.9 bitcast_dynamic-update-slice_fusion
  84.1 6.5 %gather_fusion = bf16[8,513,672]{2,1,0:T(8,128)(2,1)} fusion(bf16[8,513,672]{2,1,0:T(8,128)(2,1)} %bitcast_dynamic-update-slice_fusion, s32[1024]{0:T(1024)S(1)} %pad_clamp_fusion), kind=kCustom, calls=%fused_computation | custom fusion | bytes 11031584 | tf_op jit(solution)/shard_map/jit(_take)/gather | solution.py:57
  90.6 3.7 %broadcast_select_fusion = bf16[8,513,672]{2,1,0:T(8,128)(2,1)S(1)} fusion(bf16[8,513,672]{2,1,0:T(8,128)(2,1)} %gather_fusion, pred[8]{0:T(512)(128)(4,1)S(1)} %compare_and_fusion), kind=kLoop, calls=%fused_computation.11 | loop fusion | flops 2757888 | bytes 11031560 | tf_op jit(solution)/shard_map/jit(_take)/select_n | solution.py:57
  94.3 1.4 fusion.1
  95.7 4.7 %fusion.3 = bf16[8,512,672]{2,1,0:T(8,128)(2,1)} fusion(f32[8,672]{1,0:T(8,128)S(1)} %bitcast.86, f32[512]{0:T(512)S(1)} %add_rsqrt_fusion.2, bf16[8,513,672]{2,1,0:T(8,128)(2,1)S(1)} %broadcast_select_fusion), kind=kLoop, calls=%fused_computation.6 | loop fusion | flops 11010048 | bytes 11033600 | tf_op jit(solution)/shard_map/convert_element_type | solution.py:62
  100.4 22.4 %all-gather.2.cloned.1.call-done = bf16[5376,1024]{1,0:T(8,128)(2,1)} async-done(((bf16[168,1024]{1,0:T(8,128)(2,1)}), bf16[5376,1024]{1,0:T(8,128)(2,1)}) %all-gather.2.cloned.1.call-update) | async-done | bytes 11010064 | tf_op jit(solution)/shard_map/all_gather | solution.py:65
  122.7 8.3 %fusion.14 = f32[512,512]{0,1:T(8,128)S(1)} fusion(bf16[8,512,672]{2,1,0:T(8,128)(2,1)} %fusion.3, bf16[8,672,1024]{2,1,0:T(8,128)(2,1)} %bitcast.87), kind=kOutput, calls=%fused_computation.22 | convolution fusion | flops 2818572288 | bytes 12845056 | tf_op jit(solution)/shard_map/jrc,jcn->rn/dot_general | solution.py:79
  131.1 0.1 multiply_reduce_fusion.1
  131.2 0.1 multiply_multiply_fusion.1
  131.3 0.1 subtract_convert_fusion.1
  131.4 2.7 %collective-permute-start.9 = (bf16[512,256]{0,1:T(8,128)(2,1)S(1)}, bf16[512,256]{0,1:T(8,128)(2,1)S(1)}, u32[]{:S(2)}, u32[]{:S(2)}) collective-permute-start(bf16[512,256]{0,1:T(8,128)(2,1)S(1)} %bitcast.80), channel_id=1, source_target_pairs={{0,16},{8,24},{16,32},{24,40},{32,48},{40,56},{48,64},{56,72},{64,... | collective-permute-start | bytes 786440 | tf_op jit(solution)/shard_map/ppermute | solution.py:18
  134.2 4.7 %collective-permute-start.8 = (bf16[512,256]{0,1:T(8,128)(2,1)S(1)}, bf16[512,256]{0,1:T(8,128)(2,1)S(1)}, u32[]{:S(2)}, u32[]{:S(2)}) collective-permute-start(bf16[512,256]{0,1:T(8,128)(2,1)S(1)} %slice.73), channel_id=1, source_target_pairs={{0,8},{8,16},{16,24},{24,32},{32,40},{40,48},{48,56},{56,64},{64,7... | collective-permute-start | bytes 786440 | tf_op jit(solution)/shard_map/ppermute | solution.py:18
  138.9 3.4 %collective-permute-start.7 = (bf16[512,256]{0,1:T(8,128)(2,1)S(1)}, bf16[512,256]{0,1:T(8,128)(2,1)S(1)}, u32[]{:S(2)}, u32[]{:S(2)}) collective-permute-start(bf16[512,256]{0,1:T(8,128)(2,1)S(1)} %slice.73), channel_id=1, source_target_pairs={{0,16},{8,24},{16,32},{24,40},{32,48},{40,56},{48,64},{56,72},{64,... | collective-permute-start | bytes 786440 | tf_op jit(solution)/shard_map/ppermute | solution.py:18
  142.2 2.8 %collective-permute-start.10 = (bf16[512,256]{0,1:T(8,128)(2,1)S(1)}, bf16[512,256]{0,1:T(8,128)(2,1)S(1)}, u32[]{:S(2)}, u32[]{:S(2)}) collective-permute-start(bf16[512,256]{0,1:T(8,128)(2,1)S(1)} %bitcast.81), channel_id=1, source_target_pairs={{0,8},{8,16},{16,24},{24,32},{32,40},{40,48},{48,56},{56,64},{64,7... | collective-permute-start | bytes 786440 | tf_op jit(solution)/shard_map/ppermute | solution.py:18
  145.0 5.2 %collective-permute-done.9 = bf16[512,256]{0,1:T(8,128)(2,1)S(1)} collective-permute-done((bf16[512,256]{0,1:T(8,128)(2,1)S(1)}, bf16[512,256]{0,1:T(8,128)(2,1)S(1)}, u32[]{:S(2)}, u32[]{:S(2)}) %collective-permute-start.9) | collective-permute-done | bytes 262176 | tf_op jit(solution)/shard_map/ppermute | solution.py:18
  150.2 5.5 %fusion.10 = f32[512,512,1]{0,1,2:T(8,128)S(1)} fusion(bf16[8,512,672]{2,1,0:T(8,128)(2,1)S(1)} %copy-done, bf16[8,672,1024]{2,1,0:T(8,128)(2,1)} %bitcast.88), kind=kOutput, calls=%fused_computation.17 | convolution fusion | flops 2818572288 | bytes 12058624 | tf_op jit(solution)/shard_map/jrc,jcn->rn/dot_general | solution.py:89
  155.8 0.1 multiply_reduce_fusion
  155.9 0.2 multiply_multiply_fusion
  156.1 0.2 subtract_convert_fusion
  156.3 13.7 %collective-permute-done.10 = bf16[512,256]{0,1:T(8,128)(2,1)S(1)} collective-permute-done((bf16[512,256]{0,1:T(8,128)(2,1)S(1)}, bf16[512,256]{0,1:T(8,128)(2,1)S(1)}, u32[]{:S(2)}, u32[]{:S(2)}) %collective-permute-start.10) | collective-permute-done | bytes 262176 | tf_op jit(solution)/shard_map/ppermute | solution.py:18
  170.1 8.5 %fusion.35 = (f32[2,2,512]{2,1,0:T(2,128)S(1)}, bf16[2,2,512,1536]{2,3,1,0:T(8,128)(2,1)}) fusion(pred[512,1536]{0,1:T(8,128)(4,1)S(1)} %copy-done.1, bf16[1536,2,128,1]{0,2,3,1:T(8,128)(2,1)S(1)} %bitcast.83, bf16[512,2,2,128]{0,3,2,1:T(8,128)(2,1)S(1)} %bitcast.85), kind=kOutput, calls=%fused_computation.80 | convolution fusion | flops 824182272 | bytes 8396800 | tf_op jit(solution)/shard_map/sub | solution.py:109
  178.7 3.9 %fusion.25 = bf16[512,2,2,128]{0,3,2,1:T(8,128)(2,1)S(1)} fusion(bf16[1536,2,128,1]{0,2,3,1:T(8,128)(2,1)S(1)} %bitcast.84, bf16[2,2,512,1536]{2,3,1,0:T(8,128)(2,1)} %get-tuple-element.18, f32[512,2,2]{0,2,1:T(2,128)S(1)} %bitcast.92), kind=kOutput, calls=%fused_computation.26 | convolution fusion | flops 805830656 | bytes 7610368 | tf_op jit(solution)/shard_map/kgts,skd->tkgd/dot_general | solution.py:112
  182.6 0.4 slice-done.1
  183.0 4.9 %convolution_convert_fusion = bf16[512,5376]{0,1:T(8,128)(2,1)} fusion(bf16[512,512]{0,1:T(8,128)(2,1)S(1)} %bitcast.91, bf16[512,5376]{1,0:T(8,128)(2,1)S(1)} %bitcast.90), kind=kOutput, calls=%fused_computation.10 | convolution fusion | flops 2821324800 | bytes 11534336 | tf_op jit(solution)/shard_map/dot_general | solution.py:117
  188.0 42.2 %reduce-scatter.2.cloned.1.call-done = bf16[512,672]{0,1:T(8,128)(2,1)} async-done(((bf16[512,5376]{0,1:T(8,128)(2,1)}), bf16[512,672]{0,1:T(8,128)(2,1)}) %reduce-scatter.2.cloned.1.call-update) | async-done | bytes 688144 | tf_op jit(solution)/shard_map/reduce_scatter | solution.py:118
  (39 shorter events, 0.4 us)
Async XLA Ops:
  6.5 116.2 %all-gather.2.cloned.1.call-start = ((), (), s32[]{:S(2)}) async-start(), calls=%async_computation.1 | async-start | bytes 11354112 | tf_op jit(solution)/shard_map/all_gather | solution.py:65
  8.3 221.9 %reduce-scatter.2.cloned.1.call-start = ((), (), s32[]{:S(2)}) async-start(), calls=%async_computation.2 | async-start | bytes 6193152 | tf_op jit(solution)/shard_map/reduce_scatter | solution.py:118
  10.5 20.8 %collective-permute-start = (bf16[513,672]{1,0:T(8,128)(2,1)S(1)}, bf16[513,672]{1,0:T(8,128)(2,1)}, u32[]{:S(2)}, u32[]{:S(2)}) collective-permute-start(bf16[513,672]{1,0:T(8,128)(2,1)S(1)} %pad_maximum_fusion), channel_id=1, source_target_pairs={{0,1},{1,2},{2,3},{3,4},{4,5},{5,6},{6,7},{7,0},{8,9},{9,10},{10,1... | collective-permute-start | bytes 2068424 | tf_op jit(solution)/shard_map/ppermute | solution.py:53
  10.6 24.6 %collective-permute-start.1 = (bf16[513,672]{1,0:T(8,128)(2,1)S(1)}, bf16[513,672]{1,0:T(8,128)(2,1)}, u32[]{:S(2)}, u32[]{:S(2)}) collective-permute-start(bf16[513,672]{1,0:T(8,128)(2,1)S(1)} %pad_maximum_fusion), channel_id=1, source_target_pairs={{0,2},{1,3},{2,4},{3,5},{4,6},{5,7},{6,0},{7,1},{8,10},{9,11},{10,... | collective-permute-start | bytes 2068424 | tf_op jit(solution)/shard_map/ppermute | solution.py:53
  12.2 54.6 %collective-permute-start.2 = (bf16[513,672]{1,0:T(8,128)(2,1)S(1)}, bf16[513,672]{1,0:T(8,128)(2,1)}, u32[]{:S(2)}, u32[]{:S(2)}) collective-permute-start(bf16[513,672]{1,0:T(8,128)(2,1)S(1)} %pad_maximum_fusion), channel_id=1, source_target_pairs={{0,3},{1,4},{2,5},{3,6},{4,7},{5,0},{6,1},{7,2},{8,11},{9,12},{10,... | collective-permute-start | bytes 2068424 | tf_op jit(solution)/shard_map/ppermute | solution.py:53
  14.4 54.4 %collective-permute-start.3 = (bf16[513,672]{1,0:T(8,128)(2,1)S(1)}, bf16[513,672]{1,0:T(8,128)(2,1)S(1)}, u32[]{:S(2)}, u32[]{:S(2)}) collective-permute-start(bf16[513,672]{1,0:T(8,128)(2,1)S(1)} %pad_maximum_fusion), channel_id=1, source_target_pairs={{0,4},{1,5},{2,6},{3,7},{4,0},{5,1},{6,2},{7,3},{8,12},{9,13},{10,... | collective-permute-start | bytes 2068424 | tf_op jit(solution)/shard_map/ppermute | solution.py:53
  16.3 64.9 %collective-permute-start.4 = (bf16[513,672]{1,0:T(8,128)(2,1)S(1)}, bf16[513,672]{1,0:T(8,128)(2,1)S(1)}, u32[]{:S(2)}, u32[]{:S(2)}) collective-permute-start(bf16[513,672]{1,0:T(8,128)(2,1)S(1)} %pad_maximum_fusion), channel_id=1, source_target_pairs={{0,5},{1,6},{2,7},{3,0},{4,1},{5,2},{6,3},{7,4},{8,13},{9,14},{10,... | collective-permute-start | bytes 2068424 | tf_op jit(solution)/shard_map/ppermute | solution.py:53
  31.3 50.8 %collective-permute-start.5 = (bf16[513,672]{1,0:T(8,128)(2,1)S(1)}, bf16[513,672]{1,0:T(8,128)(2,1)S(1)}, u32[]{:S(2)}, u32[]{:S(2)}) collective-permute-start(bf16[513,672]{1,0:T(8,128)(2,1)S(1)} %pad_maximum_fusion), channel_id=1, source_target_pairs={{0,6},{1,7},{2,0},{3,1},{4,2},{5,3},{6,4},{7,5},{8,14},{9,15},{10,... | collective-permute-start | bytes 2068424 | tf_op jit(solution)/shard_map/ppermute | solution.py:53
  35.2 47.9 %collective-permute-start.6 = (bf16[513,672]{1,0:T(8,128)(2,1)S(1)}, bf16[513,672]{1,0:T(8,128)(2,1)S(1)}, u32[]{:S(2)}, u32[]{:S(2)}) collective-permute-start(bf16[513,672]{1,0:T(8,128)(2,1)S(1)} %pad_maximum_fusion), channel_id=1, source_target_pairs={{0,7},{1,0},{2,1},{3,2},{4,3},{5,4},{6,5},{7,6},{8,15},{9,8},{10,9... | collective-permute-start | bytes 2068424 | tf_op jit(solution)/shard_map/ppermute | solution.py:53
  122.7 11.4 %copy-start.2 = (bf16[1,128]{1,0:T(2,128)(2,1)S(1)}, bf16[1,128]{1,0:T(2,128)(2,1)}, u32[]{:S(2)}) copy-start(bf16[1,128]{1,0:T(2,128)(2,1)} %param.13) | copy-start | bytes 772
  122.7 27.5 %copy-start = (bf16[8,512,672]{2,1,0:T(8,128)(2,1)S(1)}, bf16[8,512,672]{2,1,0:T(8,128)(2,1)}, u32[]{:S(2)}) copy-start(bf16[8,512,672]{2,1,0:T(8,128)(2,1)} %fusion.3) | copy-start | bytes 16515076
  131.4 18.8 %collective-permute-start.9 = (bf16[512,256]{0,1:T(8,128)(2,1)S(1)}, bf16[512,256]{0,1:T(8,128)(2,1)S(1)}, u32[]{:S(2)}, u32[]{:S(2)}) collective-permute-start(bf16[512,256]{0,1:T(8,128)(2,1)S(1)} %bitcast.80), channel_id=1, source_target_pairs={{0,16},{8,24},{16,32},{24,40},{32,48},{40,56},{48,64},{56,72},{64,... | collective-permute-start | bytes 786440 | tf_op jit(solution)/shard_map/ppermute | solution.py:18
  134.2 44.4 %collective-permute-start.8 = (bf16[512,256]{0,1:T(8,128)(2,1)S(1)}, bf16[512,256]{0,1:T(8,128)(2,1)S(1)}, u32[]{:S(2)}, u32[]{:S(2)}) collective-permute-start(bf16[512,256]{0,1:T(8,128)(2,1)S(1)} %slice.73), channel_id=1, source_target_pairs={{0,8},{8,16},{16,24},{24,32},{32,40},{40,48},{48,56},{56,64},{64,7... | collective-permute-start | bytes 786440 | tf_op jit(solution)/shard_map/ppermute | solution.py:18
  138.9 39.8 %collective-permute-start.7 = (bf16[512,256]{0,1:T(8,128)(2,1)S(1)}, bf16[512,256]{0,1:T(8,128)(2,1)S(1)}, u32[]{:S(2)}, u32[]{:S(2)}) collective-permute-start(bf16[512,256]{0,1:T(8,128)(2,1)S(1)} %slice.73), channel_id=1, source_target_pairs={{0,16},{8,24},{16,32},{24,40},{32,48},{40,56},{48,64},{56,72},{64,... | collective-permute-start | bytes 786440 | tf_op jit(solution)/shard_map/ppermute | solution.py:18
  142.2 27.8 %collective-permute-start.10 = (bf16[512,256]{0,1:T(8,128)(2,1)S(1)}, bf16[512,256]{0,1:T(8,128)(2,1)S(1)}, u32[]{:S(2)}, u32[]{:S(2)}) collective-permute-start(bf16[512,256]{0,1:T(8,128)(2,1)S(1)} %bitcast.81), channel_id=1, source_target_pairs={{0,8},{8,16},{16,24},{24,32},{32,40},{40,48},{48,56},{56,64},{64,7... | collective-permute-start | bytes 786440 | tf_op jit(solution)/shard_map/ppermute | solution.py:18
  155.8 14.4 %copy-start.1 = (pred[512,1536]{0,1:T(8,128)(4,1)S(1)}, pred[512,1536]{0,1:T(8,128)(4,1)}, u32[]{:S(2)}) copy-start(pred[512,1536]{0,1:T(8,128)(4,1)} %and_and_fusion) | copy-start | bytes 2359300
  178.6 4.0 %slice-start = ((s8[5505024]{0:T(1024)(128)(4,1)}), s8[4194304]{0:T(1024)(128)(4,1)S(1)}, s32[]{:S(2)}) async-start(s8[5505024]{0:T(1024)(128)(4,1)} %bitcast.89), calls=%async_computation.3 | async-start | bytes 8388608
  178.7 4.3 %slice-start.1 = ((s8[5505024]{0:T(1024)(128)(4,1)}), s8[1310720]{0:T(1024)(128)(4,1)S(1)}, s32[]{:S(2)}) async-start(s8[5505024]{0:T(1024)(128)(4,1)} %bitcast.89), calls=%async_computation.4 | async-start | bytes 2621440
Sparse Core Ops, SparseCore 0:
  9.9 112.7 all-gather.1
  188.1 42.0 reduce-scatter.1

commit v10 on v8

--- a/solution.py
+++ b/solution.py
@@ -69,6 +69,13 @@
     tok_index = lax.axis_index("tok")
     positions = tok_index * rows + jnp.arange(rows, dtype=jnp.int32)
     reach = (WINDOW - 1 + rows - 1) // rows
+    key_pos = (tok_index - reach) * rows + jnp.arange((reach + 1) * rows, dtype=jnp.int32)
+    allowed = (
+        (key_pos[None, :] <= positions[:, None])
+        & (key_pos[None, :] > positions[:, None] - WINDOW)
+        & (key_pos[None, :] >= 0)
+    )
+    allowed, normed = lax.optimization_barrier((allowed, normed))
     key_raw = jnp.einsum(
         "jrc,jcn->rn",
         normed,
@@ -76,8 +83,8 @@
         preferred_element_type=jnp.float32,
     )
     key = rotate(head_norm(key_raw, k_norm_gain), positions).astype(jnp.bfloat16)
-    earlier_keys = [shifted(key, "tok", offset) for offset in range(reach, 0, -1)]
-    normed_mid, _ = lax.optimization_barrier((normed, earlier_keys[0]))
+    earlier_keys = [shifted(key, "tok", offset) for offset in range(1, reach + 1)][::-1]
+    normed_mid, _ = lax.optimization_barrier((normed, key))
     value_raw = jnp.einsum(
         "jrc,jcn->rn",
         normed_mid,
@@ -86,7 +93,7 @@
     )
     value_rows = value_raw.astype(jnp.bfloat16)
     earlier_values = [shifted(value_rows, "tok", offset) for offset in range(reach, 0, -1)]
-    normed_late, _ = lax.optimization_barrier((normed_mid, earlier_values[0]))
+    normed_late, _ = lax.optimization_barrier((normed_mid, value_rows))
     query_raw = jnp.einsum(
         "jrc,jcn->rn", normed_late, weights3[:, :, :width_query], preferred_element_type=jnp.float32
     )
@@ -94,7 +101,6 @@
     window_keys = jnp.concatenate(earlier_keys + [key], axis=0)
     window_values = jnp.concatenate(earlier_values + [value_rows], axis=0)
     window_extent = window_keys.shape[0]
-    key_pos = (tok_index - reach) * rows + jnp.arange(window_extent, dtype=jnp.int32)
     kv_heads = width_kv // HEAD_SIZE
     query_group_count = width_query // HEAD_SIZE // kv_heads
     query_four_axes = query.reshape(rows, kv_heads, query_group_count, HEAD_SIZE)
@@ -105,11 +111,6 @@
             "tkgd,skd->kgts", query_four_axes, keys_three_axes, preferred_element_type=jnp.float32
         )
         * score_scale
-    )
-    allowed = (
-        (key_pos[None, :] <= positions[:, None])
-        & (key_pos[None, :] > positions[:, None] - WINDOW)
-        & (key_pos[None, :] >= 0)
     )
     masked = jnp.where(allowed, scores, -1e30)
     top = jnp.max(masked, axis=-1, keepdims=True)

time: 245 us -> 239 us (0.976)
  waiting for transfers between devices: 123 us -> 113 us
    ppermute x4, waiting for transfers between devices: 22.7 us -> 16.1 us  [shifted(): lax.ppermute(value, axis, [(source, source + steps) for source in range(l...]
    ppermute x7, waiting for transfers between devices: 36.3 us -> 33.8 us  [local(): lax.ppermute(with_gain, 'hid', [(i, (i + k) % n_hid) for i in range(n_hid)])]
    unnamed x14 -> x12, local copies, waits for them, and re-layouts: 10.6 us -> 10.6 us
  transfers between devices with their start and end apart: 13 -> 13, of which waited for: 8 -> 8; matrix products, arithmetic and copies ran while one was open for 17% -> 18% of each run, Pallas kernels for 0% -> 0%
where the time goes in v10:
time: 239 us; the launch traced here: 238 us
  waiting for transfers between devices  113 us (47%)
  starting transfers between devices  37.7 us (16%)
  matrix products  35.6 us (15%)
  other arithmetic  19.7 us (8%)
  local copies, waits for them, and re-layouts  18.3 us (8%)
  between operations  13.7 us (6%)
    reduce_scatter x1, waiting for transfers between devices, local(): lax.psum_scatter(partial_value.astype(jnp.bfloat16), 'hid', scatter_dimen...  40.8 us
    ppermute x7, waiting for transfers between devices, local(): lax.ppermute(with_gain, 'hid', [(i, (i + k) % n_hid) for i in range(n_hid)])  33.8 us
    ppermute x7, starting transfers between devices, local(): lax.ppermute(with_gain, 'hid', [(i, (i + k) % n_hid) for i in range(n_hid)])  24.1 us
    all_gather x1, waiting for transfers between devices, local(): lax.all_gather(jnp.concatenate([w_query, w_key, value_matrix], axis=1), '...  22.4 us
    ppermute x4, waiting for transfers between devices, shifted(): lax.ppermute(value, axis, [(source, source + steps) for source in range(l...  16.1 us
    ppermute x4, starting transfers between devices, shifted(): lax.ppermute(value, axis, [(source, source + steps) for source in range(l...  13.5 us
    unnamed x12, local copies, waits for them, and re-layouts  10.6 us
    dot_general x1, matrix products, local(): jnp.dot(heads_out, w_out, preferred_element_type=jnp.float32)  8.64 us
  transfers between devices with their start and end apart: 13, of which 8 were waited for; matrix products, arithmetic and copies ran while one was open for 18% of the time, Pallas kernels for 0%

profile of v10, /device:TPU:2, one launch (start us, length us, event | category | flops | bytes accessed | tf_op | source)
XLA Modules:
  0.0 238.1 jit_solution(11876646816429715588)
XLA Ops:
  6.5 1.8 pad_maximum_fusion.4
  8.4 1.4 copy.21
  9.8 0.8 pad_maximum_fusion
  10.6 1.7 collective-permute-start.1
  12.2 2.2 collective-permute-start.2
  14.4 1.8 collective-permute-start.3
  16.3 1.8 collective-permute-start.4
  18.2 0.5 multiply_cosine_fusion
  18.7 1.9 and_and_fusion
  20.6 0.7 bitcast_convert_fusion.1
  21.2 0.7 bitcast_convert_fusion
  21.9 1.7 bitcast_dynamic-update-slice_fusion.7
  23.6 7.7 %collective-permute-done = bf16[513,672]{1,0:T(8,128)(2,1)} collective-permute-done((bf16[513,672]{1,0:T(8,128)(2,1)S(1)}, bf16[513,672]{1,0:T(8,128)(2,1)}, u32[]{:S(2)}, u32[]{:S(2)}) %collective-permute-start) | collective-permute-done | bytes 689504 | tf_op jit(solution)/shard_map/ppermute | solution.py:53
  31.3 1.8 collective-permute-start.5
  33.1 2.1 bitcast_dynamic-update-slice_fusion.6
  35.2 14.7 %collective-permute-start.6 = (bf16[513,672]{1,0:T(8,128)(2,1)S(1)}, bf16[513,672]{1,0:T(8,128)(2,1)S(1)}, u32[]{:S(2)}, u32[]{:S(2)}) collective-permute-start(bf16[513,672]{1,0:T(8,128)(2,1)S(1)} %pad_maximum_fusion), channel_id=1, source_target_pairs={{0,7},{1,0},{2,1},{3,2},{4,3},{5,4},{6,5},{7,6},{8,15},{9,8},{10,9... | collective-permute-start | bytes 2068424 | tf_op jit(solution)/shard_map/ppermute | solution.py:53
  49.9 2.1 bitcast_dynamic-update-slice_fusion.5
  52.1 14.7 %collective-permute-done.2 = bf16[513,672]{1,0:T(8,128)(2,1)} collective-permute-done((bf16[513,672]{1,0:T(8,128)(2,1)S(1)}, bf16[513,672]{1,0:T(8,128)(2,1)}, u32[]{:S(2)}, u32[]{:S(2)}) %collective-permute-start.2) | collective-permute-done | bytes 689504 | tf_op jit(solution)/shard_map/ppermute | solution.py:53
  66.8 2.1 bitcast_dynamic-update-slice_fusion.4
  68.8 1.0 bitcast_dynamic-update-slice_fusion.3
  69.8 11.3 %collective-permute-done.4 = bf16[513,672]{1,0:T(8,128)(2,1)S(1)} collective-permute-done((bf16[513,672]{1,0:T(8,128)(2,1)S(1)}, bf16[513,672]{1,0:T(8,128)(2,1)S(1)}, u32[]{:S(2)}, u32[]{:S(2)}) %collective-permute-start.4) | collective-permute-done | bytes 689504 | tf_op jit(solution)/shard_map/ppermute | solution.py:53
  81.1 0.9 bitcast_dynamic-update-slice_fusion.2
  82.1 1.0 bitcast_dynamic-update-slice_fusion.1
  83.1 1.0 bitcast_dynamic-update-slice_fusion
  84.1 6.5 %gather_fusion = bf16[8,513,672]{2,1,0:T(8,128)(2,1)} fusion(bf16[8,513,672]{2,1,0:T(8,128)(2,1)} %bitcast_dynamic-update-slice_fusion, s32[1024]{0:T(1024)S(1)} %pad_clamp_fusion), kind=kCustom, calls=%fused_computation | custom fusion | bytes 11031584 | tf_op jit(solution)/shard_map/jit(_take)/gather | solution.py:57
  90.6 3.7 %broadcast_select_fusion = bf16[8,513,672]{2,1,0:T(8,128)(2,1)S(1)} fusion(bf16[8,513,672]{2,1,0:T(8,128)(2,1)} %gather_fusion, pred[8]{0:T(512)(128)(4,1)S(1)} %compare_and_fusion), kind=kLoop, calls=%fused_computation.11 | loop fusion | flops 2757888 | bytes 11031560 | tf_op jit(solution)/shard_map/jit(_take)/select_n | solution.py:57
  94.3 1.4 fusion.1
  95.7 4.7 %fusion.3 = bf16[8,512,672]{2,1,0:T(8,128)(2,1)} fusion(f32[8,672]{1,0:T(8,128)S(1)} %bitcast.91, f32[512]{0:T(512)S(1)} %add_rsqrt_fusion.2, bf16[8,513,672]{2,1,0:T(8,128)(2,1)S(1)} %broadcast_select_fusion), kind=kLoop, calls=%fused_computation.6 | loop fusion | flops 11010048 | bytes 11033600 | tf_op jit(solution)/shard_map/convert_element_type | solution.py:62
  100.4 22.4 %all-gather.2.cloned.1.call-done = bf16[5376,1024]{1,0:T(8,128)(2,1)} async-done(((bf16[168,1024]{1,0:T(8,128)(2,1)}), bf16[5376,1024]{1,0:T(8,128)(2,1)}) %all-gather.2.cloned.1.call-update) | async-done | bytes 11010064 | tf_op jit(solution)/shard_map/all_gather | solution.py:65
  122.7 5.6 %fusion.14 = f32[512,256,1]{0,1,2:T(8,128)S(1)} fusion(bf16[8,512,672]{2,1,0:T(8,128)(2,1)} %fusion.3, bf16[8,672,1024]{2,1,0:T(8,128)(2,1)} %bitcast.92), kind=kOutput, calls=%fused_computation.22 | convolution fusion | flops 1409286144 | bytes 9568256 | tf_op jit(solution)/shard_map/jrc,jcn->rn/dot_general | solution.py:79
  128.4 0.1 multiply_multiply_fusion.1
  128.6 1.9 collective-permute-start.10
  130.6 5.4 %collective-permute-start.9 = (bf16[512,256]{0,1:T(8,128)(2,1)S(1)}, bf16[512,256]{0,1:T(8,128)(2,1)}, u32[]{:S(2)}, u32[]{:S(2)}) collective-permute-start(bf16[512,256]{0,1:T(8,128)(2,1)S(1)} %bitcast.86), channel_id=1, source_target_pairs={{0,16},{8,24},{16,32},{24,40},{32,48},{40,56},{48,64},{56,72},{64,... | collective-permute-start | bytes 786440 | tf_op jit(solution)/shard_map/ppermute | solution.py:18
  136.0 3.6 %fusion.30 = bf16[512,256]{1,0:T(8,128)(2,1)S(1)} fusion(bf16[8,512,672]{2,1,0:T(8,128)(2,1)S(1)} %copy-done, bf16[8,672,1024]{2,1,0:T(8,128)(2,1)} %bitcast.93), kind=kOutput, calls=%fused_computation.29 | convolution fusion | flops 1409417216 | bytes 8519680 | tf_op jit(solution)/shard_map/jrc,jcn->rn/dot_general | solution.py:88
  139.6 3.4 %collective-permute-start.7 = (bf16[512,256]{1,0:T(8,128)(2,1)S(1)}, bf16[512,256]{1,0:T(8,128)(2,1)S(1)}, u32[]{:S(2)}, u32[]{:S(2)}) collective-permute-start(bf16[512,256]{1,0:T(8,128)(2,1)S(1)} %fusion.30), channel_id=1, source_target_pairs={{0,16},{8,24},{16,32},{24,40},{32,48},{40,56},{48,64},{56,72},{64,... | collective-permute-start | bytes 786440 | tf_op jit(solution)/shard_map/ppermute | solution.py:18
  143.0 2.8 %collective-permute-start.8 = (bf16[512,256]{1,0:T(8,128)(2,1)S(1)}, bf16[512,256]{1,0:T(8,128)(2,1)S(1)}, u32[]{:S(2)}, u32[]{:S(2)}) collective-permute-start(bf16[512,256]{1,0:T(8,128)(2,1)S(1)} %fusion.30), channel_id=1, source_target_pairs={{0,8},{8,16},{16,24},{24,32},{32,40},{40,48},{48,56},{56,64},{64,7... | collective-permute-start | bytes 786440 | tf_op jit(solution)/shard_map/ppermute | solution.py:18
  145.8 5.5 %fusion.10 = f32[512,512,1]{0,1,2:T(8,128)S(1)} fusion(bf16[8,512,672]{2,1,0:T(8,128)(2,1)S(1)} %copy-done, bf16[8,672,1024]{2,1,0:T(8,128)(2,1)} %bitcast.94), kind=kOutput, calls=%fused_computation.17 | convolution fusion | flops 2818572288 | bytes 12058624 | tf_op jit(solution)/shard_map/jrc,jcn->rn/dot_general | solution.py:97
  151.4 0.1 multiply_reduce_fusion
  151.5 0.2 multiply_multiply_fusion
  151.7 0.2 subtract_convert_fusion
  151.9 12.0 %collective-permute-done.7 = bf16[512,256]{1,0:T(8,128)(2,1)S(1)} collective-permute-done((bf16[512,256]{1,0:T(8,128)(2,1)S(1)}, bf16[512,256]{1,0:T(8,128)(2,1)S(1)}, u32[]{:S(2)}, u32[]{:S(2)}) %collective-permute-start.7) | collective-permute-done | bytes 262176 | tf_op jit(solution)/shard_map/ppermute | solution.py:18
  163.9 4.1 %collective-permute-done.8 = bf16[512,256]{1,0:T(8,128)(2,1)S(1)} collective-permute-done((bf16[512,256]{1,0:T(8,128)(2,1)S(1)}, bf16[512,256]{1,0:T(8,128)(2,1)S(1)}, u32[]{:S(2)}, u32[]{:S(2)}) %collective-permute-start.8) | collective-permute-done | bytes 262176 | tf_op jit(solution)/shard_map/ppermute | solution.py:18
  168.1 0.3 copy.35
  168.4 1.1 pad_maximum_fusion.2
  169.5 8.5 %fusion.40 = (f32[2,2,512]{2,1,0:T(2,128)S(1)}, bf16[2,2,512,1536]{2,3,1,0:T(8,128)(2,1)}) fusion(pred[512,1536]{0,1:T(8,128)(4,1)S(1)} %copy-done.1, bf16[1536,2,128,1]{0,2,3,1:T(8,128)(2,1)S(1)} %bitcast.89, bf16[512,2,2,128]{0,3,2,1:T(8,128)(2,1)S(1)} %bitcast.90), kind=kOutput, calls=%fused_computation.82 | convolution fusion | flops 824182272 | bytes 8396800 | tf_op jit(solution)/shard_map/sub | solution.py:117
  178.0 3.8 %fusion.24 = bf16[512,2,2,128]{0,3,2,1:T(8,128)(2,1)S(1)} fusion(bf16[1536,2,128,1]{0,2,3,1:T(8,128)(2,1)S(1)} %bitcast.88, bf16[2,2,512,1536]{2,3,1,0:T(8,128)(2,1)} %get-tuple-element.20, f32[512,2,2]{0,2,1:T(2,128)S(1)} %bitcast.96), kind=kOutput, calls=%fused_computation.27 | convolution fusion | flops 805830656 | bytes 7610368 | tf_op jit(solution)/shard_map/kgts,skd->tkgd/dot_general | solution.py:120
  181.8 8.6 %convolution_convert_fusion = bf16[512,5376]{0,1:T(8,128)(2,1)} fusion(bf16[512,512]{0,1:T(8,128)(2,1)S(1)} %bitcast.95, bf16[512,5376]{1,0:T(8,128)(2,1)} %param.15), kind=kOutput, calls=%fused_computation.10 | convolution fusion | flops 2821324800 | bytes 11534336 | tf_op jit(solution)/shard_map/dot_general | solution.py:125
  190.5 40.8 %reduce-scatter.2.cloned.1.call-done = bf16[512,672]{0,1:T(8,128)(2,1)} async-done(((bf16[512,5376]{0,1:T(8,128)(2,1)}), bf16[512,672]{0,1:T(8,128)(2,1)}) %reduce-scatter.2.cloned.1.call-update) | async-done | bytes 688144 | tf_op jit(solution)/shard_map/reduce_scatter | solution.py:126
  (33 shorter events, 0.6 us)
Async XLA Ops:
  6.5 116.2 %all-gather.2.cloned.1.call-start = ((), (), s32[]{:S(2)}) async-start(), calls=%async_computation.1 | async-start | bytes 11354112 | tf_op jit(solution)/shard_map/all_gather | solution.py:65
  8.3 222.9 %reduce-scatter.2.cloned.1.call-start = ((), (), s32[]{:S(2)}) async-start(), calls=%async_computation.2 | async-start | bytes 6193152 | tf_op jit(solution)/shard_map/reduce_scatter | solution.py:126
  10.5 20.8 %collective-permute-start = (bf16[513,672]{1,0:T(8,128)(2,1)S(1)}, bf16[513,672]{1,0:T(8,128)(2,1)}, u32[]{:S(2)}, u32[]{:S(2)}) collective-permute-start(bf16[513,672]{1,0:T(8,128)(2,1)S(1)} %pad_maximum_fusion), channel_id=1, source_target_pairs={{0,1},{1,2},{2,3},{3,4},{4,5},{5,6},{6,7},{7,0},{8,9},{9,10},{10,1... | collective-permute-start | bytes 2068424 | tf_op jit(solution)/shard_map/ppermute | solution.py:53
  10.6 24.6 %collective-permute-start.1 = (bf16[513,672]{1,0:T(8,128)(2,1)S(1)}, bf16[513,672]{1,0:T(8,128)(2,1)}, u32[]{:S(2)}, u32[]{:S(2)}) collective-permute-start(bf16[513,672]{1,0:T(8,128)(2,1)S(1)} %pad_maximum_fusion), channel_id=1, source_target_pairs={{0,2},{1,3},{2,4},{3,5},{4,6},{5,7},{6,0},{7,1},{8,10},{9,11},{10,... | collective-permute-start | bytes 2068424 | tf_op jit(solution)/shard_map/ppermute | solution.py:53
  12.2 54.6 %collective-permute-start.2 = (bf16[513,672]{1,0:T(8,128)(2,1)S(1)}, bf16[513,672]{1,0:T(8,128)(2,1)}, u32[]{:S(2)}, u32[]{:S(2)}) collective-permute-start(bf16[513,672]{1,0:T(8,128)(2,1)S(1)} %pad_maximum_fusion), channel_id=1, source_target_pairs={{0,3},{1,4},{2,5},{3,6},{4,7},{5,0},{6,1},{7,2},{8,11},{9,12},{10,... | collective-permute-start | bytes 2068424 | tf_op jit(solution)/shard_map/ppermute | solution.py:53
  14.4 54.4 %collective-permute-start.3 = (bf16[513,672]{1,0:T(8,128)(2,1)S(1)}, bf16[513,672]{1,0:T(8,128)(2,1)S(1)}, u32[]{:S(2)}, u32[]{:S(2)}) collective-permute-start(bf16[513,672]{1,0:T(8,128)(2,1)S(1)} %pad_maximum_fusion), channel_id=1, source_target_pairs={{0,4},{1,5},{2,6},{3,7},{4,0},{5,1},{6,2},{7,3},{8,12},{9,13},{10,... | collective-permute-start | bytes 2068424 | tf_op jit(solution)/shard_map/ppermute | solution.py:53
  16.3 64.9 %collective-permute-start.4 = (bf16[513,672]{1,0:T(8,128)(2,1)S(1)}, bf16[513,672]{1,0:T(8,128)(2,1)S(1)}, u32[]{:S(2)}, u32[]{:S(2)}) collective-permute-start(bf16[513,672]{1,0:T(8,128)(2,1)S(1)} %pad_maximum_fusion), channel_id=1, source_target_pairs={{0,5},{1,6},{2,7},{3,0},{4,1},{5,2},{6,3},{7,4},{8,13},{9,14},{10,... | collective-permute-start | bytes 2068424 | tf_op jit(solution)/shard_map/ppermute | solution.py:53
  31.3 50.8 %collective-permute-start.5 = (bf16[513,672]{1,0:T(8,128)(2,1)S(1)}, bf16[513,672]{1,0:T(8,128)(2,1)S(1)}, u32[]{:S(2)}, u32[]{:S(2)}) collective-permute-start(bf16[513,672]{1,0:T(8,128)(2,1)S(1)} %pad_maximum_fusion), channel_id=1, source_target_pairs={{0,6},{1,7},{2,0},{3,1},{4,2},{5,3},{6,4},{7,5},{8,14},{9,15},{10,... | collective-permute-start | bytes 2068424 | tf_op jit(solution)/shard_map/ppermute | solution.py:53
  35.2 47.9 %collective-permute-start.6 = (bf16[513,672]{1,0:T(8,128)(2,1)S(1)}, bf16[513,672]{1,0:T(8,128)(2,1)S(1)}, u32[]{:S(2)}, u32[]{:S(2)}) collective-permute-start(bf16[513,672]{1,0:T(8,128)(2,1)S(1)} %pad_maximum_fusion), channel_id=1, source_target_pairs={{0,7},{1,0},{2,1},{3,2},{4,3},{5,4},{6,5},{7,6},{8,15},{9,8},{10,9... | collective-permute-start | bytes 2068424 | tf_op jit(solution)/shard_map/ppermute | solution.py:53
  122.7 13.3 %copy-start = (bf16[8,512,672]{2,1,0:T(8,128)(2,1)S(1)}, bf16[8,512,672]{2,1,0:T(8,128)(2,1)}, u32[]{:S(2)}) copy-start(bf16[8,512,672]{2,1,0:T(8,128)(2,1)} %fusion.3) | copy-start | bytes 16515076
  128.6 39.7 %collective-permute-start.10 = (bf16[512,256]{0,1:T(8,128)(2,1)S(1)}, bf16[512,256]{0,1:T(8,128)(2,1)}, u32[]{:S(2)}, u32[]{:S(2)}) collective-permute-start(bf16[512,256]{0,1:T(8,128)(2,1)S(1)} %bitcast.85), channel_id=1, source_target_pairs={{0,8},{8,16},{16,24},{24,32},{32,40},{40,48},{48,56},{56,64},{64,7... | collective-permute-start | bytes 786440 | tf_op jit(solution)/shard_map/ppermute | solution.py:18
  130.6 37.8 %collective-permute-start.9 = (bf16[512,256]{0,1:T(8,128)(2,1)S(1)}, bf16[512,256]{0,1:T(8,128)(2,1)}, u32[]{:S(2)}, u32[]{:S(2)}) collective-permute-start(bf16[512,256]{0,1:T(8,128)(2,1)S(1)} %bitcast.86), channel_id=1, source_target_pairs={{0,16},{8,24},{16,32},{24,40},{32,48},{40,56},{48,64},{56,72},{64,... | collective-permute-start | bytes 786440 | tf_op jit(solution)/shard_map/ppermute | solution.py:18
  139.6 24.3 %collective-permute-start.7 = (bf16[512,256]{1,0:T(8,128)(2,1)S(1)}, bf16[512,256]{1,0:T(8,128)(2,1)S(1)}, u32[]{:S(2)}, u32[]{:S(2)}) collective-permute-start(bf16[512,256]{1,0:T(8,128)(2,1)S(1)} %fusion.30), channel_id=1, source_target_pairs={{0,16},{8,24},{16,32},{24,40},{32,48},{40,56},{48,64},{56,72},{64,... | collective-permute-start | bytes 786440 | tf_op jit(solution)/shard_map/ppermute | solution.py:18
  143.0 25.0 %collective-permute-start.8 = (bf16[512,256]{1,0:T(8,128)(2,1)S(1)}, bf16[512,256]{1,0:T(8,128)(2,1)S(1)}, u32[]{:S(2)}, u32[]{:S(2)}) collective-permute-start(bf16[512,256]{1,0:T(8,128)(2,1)S(1)} %fusion.30), channel_id=1, source_target_pairs={{0,8},{8,16},{16,24},{24,32},{32,40},{40,48},{48,56},{56,64},{64,7... | collective-permute-start | bytes 786440 | tf_op jit(solution)/shard_map/ppermute | solution.py:18
  151.3 18.2 %copy-start.1 = (pred[512,1536]{0,1:T(8,128)(4,1)S(1)}, pred[512,1536]{0,1:T(8,128)(4,1)}, u32[]{:S(2)}) copy-start(pred[512,1536]{0,1:T(8,128)(4,1)} %and_and_fusion) | copy-start | bytes 2359300
Sparse Core Ops, SparseCore 0:
  9.9 112.7 all-gather.1
  190.6 40.5 reduce-scatter.1

commit v11 on v7

--- a/solution.py
+++ b/solution.py
@@ -76,8 +76,9 @@
     key = rotate(head_norm(key_raw, k_norm_gain), positions).astype(jnp.bfloat16)
     value_rows = value_raw.astype(jnp.bfloat16)
     reach = (WINDOW - 1 + rows - 1) // rows
-    earlier_keys = [shifted(key, "tok", offset) for offset in range(reach, 0, -1)]
-    earlier_values = [shifted(value_rows, "tok", offset) for offset in range(reach, 0, -1)]
+    far = [shifted(jnp.concatenate([key, value_rows], axis=1), "tok", offset) for offset in range(reach, 1, -1)]
+    earlier_keys = [block[:, :width_kv] for block in far] + [shifted(key, "tok", 1)]
+    earlier_values = [block[:, width_kv:] for block in far] + [shifted(value_rows, "tok", 1)]
     normed_late, _ = lax.optimization_barrier((normed, earlier_keys[0]))
     query_raw = jnp.einsum(
         "jrc,jcn->rn", normed_late, weights3[:, :, :width_query], preferred_element_type=jnp.float32

time: 229 us -> 241 us (1.052)
  waiting for transfers between devices: 110 us -> 122 us
  matrix products: 31.2 us -> 34.7 us
  starting transfers between devices: 37.7 us -> 34.5 us
    ppermute x4 -> x3, waiting for transfers between devices: 9.23 us -> 21.2 us  [shifted(): lax.ppermute(value, axis, [(source, source + steps) for source in range(l...]
    dot_general x1, matrix products: 4.95 us -> 8.64 us  [local(): jnp.dot(heads_out, w_out, preferred_element_type=jnp.float32)]
    ppermute x4 -> x3, starting transfers between devices: 13.5 us -> 10.4 us  [shifted(): lax.ppermute(value, axis, [(source, source + steps) for source in range(l...]
    unnamed x16 -> x10, local copies, waits for them, and re-layouts: 10.6 us -> 10.6 us
  transfers between devices with their start and end apart: 13 -> 12, of which waited for: 9 -> 8; matrix products, arithmetic and copies ran while one was open for 21% -> 16% of each run, Pallas kernels for 0% -> 0%
where the time goes in v11:
time: 241 us
  waiting for transfers between devices  122 us (51%)
  matrix products  34.7 us (14%)
  starting transfers between devices  34.5 us (14%)
  local copies, waits for them, and re-layouts  18.1 us (8%)
  other arithmetic  18 us (7%)
  between operations  13.7 us (6%)
    reduce_scatter x1, waiting for transfers between devices, local(): lax.psum_scatter(partial_value.astype(jnp.bfloat16), 'hid', scatter_dimen...  42.3 us
    ppermute x7, waiting for transfers between devices, local(): lax.ppermute(with_gain, 'hid', [(i, (i + k) % n_hid) for i in range(n_hid)])  35.7 us
    ppermute x7, starting transfers between devices, local(): lax.ppermute(with_gain, 'hid', [(i, (i + k) % n_hid) for i in range(n_hid)])  24.1 us
    all_gather x1, waiting for transfers between devices, local(): lax.all_gather(jnp.concatenate([w_query, w_key, value_matrix], axis=1), '...  22.4 us
    ppermute x3, waiting for transfers between devices, shifted(): lax.ppermute(value, axis, [(source, source + steps) for source in range(l...  21.2 us
    unnamed x10, local copies, waits for them, and re-layouts  10.6 us
    ppermute x3, starting transfers between devices, shifted(): lax.ppermute(value, axis, [(source, source + steps) for source in range(l...  10.4 us
    dot_general x1, matrix products, local(): jnp.dot(heads_out, w_out, preferred_element_type=jnp.float32)  8.64 us
  transfers between devices with their start and end apart: 12, of which 8 were waited for; matrix products, arithmetic and copies ran while one was open for 16% of the time, Pallas kernels for 0%

profile of v11, /device:TPU:2, one launch (start us, length us, event | category | flops | bytes accessed | tf_op | source)
XLA Modules:
  0.0 240.6 jit_solution(11416252050022073863)
XLA Ops:
  6.5 1.8 pad_maximum_fusion.5
  8.4 1.4 copy.19
  9.8 0.8 pad_maximum_fusion
  10.6 1.7 collective-permute-start.1
  12.2 2.2 collective-permute-start.2
  14.4 1.8 collective-permute-start.3
  16.3 1.8 collective-permute-start.4
  18.2 0.5 multiply_cosine_fusion
  18.7 0.7 bitcast_convert_fusion.1
  19.4 0.7 bitcast_convert_fusion
  20.0 1.7 bitcast_dynamic-update-slice_fusion.7
  21.7 9.6 %collective-permute-done = bf16[513,672]{1,0:T(8,128)(2,1)} collective-permute-done((bf16[513,672]{1,0:T(8,128)(2,1)S(1)}, bf16[513,672]{1,0:T(8,128)(2,1)}, u32[]{:S(2)}, u32[]{:S(2)}) %collective-permute-start) | collective-permute-done | bytes 689504 | tf_op jit(solution)/shard_map/ppermute | solution.py:53
  31.3 1.8 collective-permute-start.5
  33.1 2.1 bitcast_dynamic-update-slice_fusion.6
  35.2 14.7 %collective-permute-start.6 = (bf16[513,672]{1,0:T(8,128)(2,1)S(1)}, bf16[513,672]{1,0:T(8,128)(2,1)S(1)}, u32[]{:S(2)}, u32[]{:S(2)}) collective-permute-start(bf16[513,672]{1,0:T(8,128)(2,1)S(1)} %pad_maximum_fusion), channel_id=1, source_target_pairs={{0,7},{1,0},{2,1},{3,2},{4,3},{5,4},{6,5},{7,6},{8,15},{9,8},{10,9... | collective-permute-start | bytes 2068424 | tf_op jit(solution)/shard_map/ppermute | solution.py:53
  49.9 2.1 bitcast_dynamic-update-slice_fusion.5
  52.1 14.7 %collective-permute-done.2 = bf16[513,672]{1,0:T(8,128)(2,1)} collective-permute-done((bf16[513,672]{1,0:T(8,128)(2,1)S(1)}, bf16[513,672]{1,0:T(8,128)(2,1)}, u32[]{:S(2)}, u32[]{:S(2)}) %collective-permute-start.2) | collective-permute-done | bytes 689504 | tf_op jit(solution)/shard_map/ppermute | solution.py:53
  66.8 2.1 bitcast_dynamic-update-slice_fusion.4
  68.8 1.0 bitcast_dynamic-update-slice_fusion.3
  69.8 11.3 %collective-permute-done.4 = bf16[513,672]{1,0:T(8,128)(2,1)S(1)} collective-permute-done((bf16[513,672]{1,0:T(8,128)(2,1)S(1)}, bf16[513,672]{1,0:T(8,128)(2,1)S(1)}, u32[]{:S(2)}, u32[]{:S(2)}) %collective-permute-start.4) | collective-permute-done | bytes 689504 | tf_op jit(solution)/shard_map/ppermute | solution.py:53
  81.1 0.9 bitcast_dynamic-update-slice_fusion.2
  82.1 1.0 bitcast_dynamic-update-slice_fusion.1
  83.1 0.1 collective-permute-done.6
  83.1 1.0 bitcast_dynamic-update-slice_fusion
  84.1 6.5 %gather_fusion = bf16[8,513,672]{2,1,0:T(8,128)(2,1)} fusion(bf16[8,513,672]{2,1,0:T(8,128)(2,1)} %bitcast_dynamic-update-slice_fusion, s32[1024]{0:T(1024)S(1)} %pad_clamp_fusion), kind=kCustom, calls=%fused_computation | custom fusion | bytes 11031584 | tf_op jit(solution)/shard_map/jit(_take)/gather | solution.py:57
  90.6 3.7 %broadcast_select_fusion = bf16[8,513,672]{2,1,0:T(8,128)(2,1)S(1)} fusion(bf16[8,513,672]{2,1,0:T(8,128)(2,1)} %gather_fusion, pred[8]{0:T(512)(128)(4,1)S(1)} %compare_and_fusion), kind=kLoop, calls=%fused_computation.11 | loop fusion | flops 2757888 | bytes 11031560 | tf_op jit(solution)/shard_map/jit(_take)/select_n | solution.py:57
  94.3 1.4 fusion.1
  95.7 4.7 %fusion.3 = bf16[8,512,672]{2,1,0:T(8,128)(2,1)} fusion(f32[8,672]{1,0:T(8,128)S(1)} %bitcast.86, f32[512]{0:T(512)S(1)} %add_rsqrt_fusion.2, bf16[8,513,672]{2,1,0:T(8,128)(2,1)S(1)} %broadcast_select_fusion), kind=kLoop, calls=%fused_computation.6 | loop fusion | flops 11010048 | bytes 11033600 | tf_op jit(solution)/shard_map/convert_element_type | solution.py:62
  100.4 22.4 %all-gather.2.cloned.1.call-done = bf16[5376,1024]{1,0:T(8,128)(2,1)} async-done(((bf16[168,1024]{1,0:T(8,128)(2,1)}), bf16[5376,1024]{1,0:T(8,128)(2,1)}) %all-gather.2.cloned.1.call-update) | async-done | bytes 11010064 | tf_op jit(solution)/shard_map/all_gather | solution.py:65
  122.7 8.2 %fusion.14 = f32[512,512]{0,1:T(8,128)S(1)} fusion(bf16[8,512,672]{2,1,0:T(8,128)(2,1)} %fusion.3, bf16[8,672,1024]{2,1,0:T(8,128)(2,1)} %bitcast.87), kind=kOutput, calls=%fused_computation.22 | convolution fusion | flops 2818572288 | bytes 12845056 | tf_op jit(solution)/shard_map/jrc,jcn->rn/dot_general | solution.py:69
  131.0 0.1 multiply_reduce_fusion.1
  131.1 0.1 multiply_multiply_fusion.1
  131.2 0.1 subtract_convert_fusion.1
  131.4 3.0 %collective-permute-start.7 = (bf16[512,512]{0,1:T(8,128)(2,1)S(1)}, bf16[512,512]{0,1:T(8,128)(2,1)S(1)}, u32[]{:S(2)}, u32[]{:S(2)}) collective-permute-start(bf16[512,512]{0,1:T(8,128)(2,1)S(1)} %pad_maximum_fusion.3), channel_id=1, source_target_pairs={{0,16},{8,24},{16,32},{24,40},{32,48},{40,56},{48,64},{56,72},{64,... | collective-permute-start | bytes 1572872 | tf_op jit(solution)/shard_map/ppermute | solution.py:18
  134.4 1.1 and_and_fusion
  135.5 4.7 %collective-permute-start.9 = (bf16[512,256]{0,1:T(8,128)(2,1)S(1)}, bf16[512,256]{0,1:T(8,128)(2,1)S(1)}, u32[]{:S(2)}, u32[]{:S(2)}) collective-permute-start(bf16[512,256]{0,1:T(8,128)(2,1)S(1)} %bitcast.81), channel_id=1, source_target_pairs={{0,8},{8,16},{16,24},{24,32},{32,40},{40,48},{48,56},{56,64},{64,7... | collective-permute-start | bytes 786440 | tf_op jit(solution)/shard_map/ppermute | solution.py:18
  140.2 2.8 %collective-permute-start.8 = (bf16[512,256]{0,1:T(8,128)(2,1)S(1)}, bf16[512,256]{0,1:T(8,128)(2,1)S(1)}, u32[]{:S(2)}, u32[]{:S(2)}) collective-permute-start(bf16[512,256]{0,1:T(8,128)(2,1)S(1)} %slice.83), channel_id=1, source_target_pairs={{0,8},{8,16},{16,24},{24,32},{32,40},{40,48},{48,56},{56,64},{64,7... | collective-permute-start | bytes 786440 | tf_op jit(solution)/shard_map/ppermute | solution.py:18
  143.0 18.8 %collective-permute-done.7 = bf16[512,512]{0,1:T(8,128)(2,1)S(1)} collective-permute-done((bf16[512,512]{0,1:T(8,128)(2,1)S(1)}, bf16[512,512]{0,1:T(8,128)(2,1)S(1)}, u32[]{:S(2)}, u32[]{:S(2)}) %collective-permute-start.7) | collective-permute-done | bytes 524320 | tf_op jit(solution)/shard_map/ppermute | solution.py:18
  161.9 5.5 %fusion.10 = f32[512,512,1]{0,1,2:T(8,128)S(1)} fusion(bf16[8,512,672]{2,1,0:T(8,128)(2,1)S(1)} %copy-done, bf16[8,672,1024]{2,1,0:T(8,128)(2,1)} %bitcast.88), kind=kOutput, calls=%fused_computation.17 | convolution fusion | flops 2818572288 | bytes 12058624 | tf_op jit(solution)/shard_map/jrc,jcn->rn/dot_general | solution.py:83
  167.4 0.1 multiply_reduce_fusion
  167.5 0.2 multiply_multiply_fusion
  167.7 0.2 subtract_convert_fusion
  168.0 2.3 collective-permute-done.8
  170.3 0.1 pad_maximum_fusion.1
  170.4 8.5 %fusion.36 = (f32[2,2,512]{2,1,0:T(2,128)S(1)}, bf16[2,2,512,1536]{2,3,1,0:T(8,128)(2,1)}) fusion(pred[512,1536]{0,1:T(8,128)(4,1)S(1)} %and_and_fusion, bf16[1536,2,128,1]{0,2,3,1:T(8,128)(2,1)S(1)} %bitcast.84, bf16[512,2,2,128]{0,3,2,1:T(8,128)(2,1)S(1)} %bitcast.85), kind=kOutput, calls=%fused_computation.82 | convolution fusion | flops 824182272 | bytes 8396800 | tf_op jit(solution)/shard_map/sub | solution.py:109
  178.9 3.8 %fusion.25 = bf16[512,2,2,128]{0,3,2,1:T(8,128)(2,1)S(1)} fusion(bf16[1536,2,128,1]{0,2,3,1:T(8,128)(2,1)S(1)} %bitcast.83, bf16[2,2,512,1536]{2,3,1,0:T(8,128)(2,1)} %get-tuple-element.16, f32[512,2,2]{0,2,1:T(2,128)S(1)} %bitcast.90), kind=kOutput, calls=%fused_computation.26 | convolution fusion | flops 805830656 | bytes 7610368 | tf_op jit(solution)/shard_map/kgts,skd->tkgd/dot_general | solution.py:112
  182.7 8.6 %convolution_convert_fusion = bf16[512,5376]{0,1:T(8,128)(2,1)} fusion(bf16[512,512]{0,1:T(8,128)(2,1)S(1)} %bitcast.89, bf16[512,5376]{1,0:T(8,128)(2,1)} %param.15), kind=kOutput, calls=%fused_computation.10 | convolution fusion | flops 2821324800 | bytes 11534336 | tf_op jit(solution)/shard_map/dot_general | solution.py:117
  191.4 42.3 %reduce-scatter.2.cloned.1.call-done = bf16[512,672]{0,1:T(8,128)(2,1)} async-done(((bf16[512,5376]{0,1:T(8,128)(2,1)}), bf16[512,672]{0,1:T(8,128)(2,1)}) %reduce-scatter.2.cloned.1.call-update) | async-done | bytes 688144 | tf_op jit(solution)/shard_map/reduce_scatter | solution.py:118
  (29 shorter events, 0.4 us)
Async XLA Ops:
  6.5 116.2 %all-gather.2.cloned.1.call-start = ((), (), s32[]{:S(2)}) async-start(), calls=%async_computation.1 | async-start | bytes 11354112 | tf_op jit(solution)/shard_map/all_gather | solution.py:65
  8.3 225.4 %reduce-scatter.2.cloned.1.call-start = ((), (), s32[]{:S(2)}) async-start(), calls=%async_computation.2 | async-start | bytes 6193152 | tf_op jit(solution)/shard_map/reduce_scatter | solution.py:118
  10.5 20.8 %collective-permute-start = (bf16[513,672]{1,0:T(8,128)(2,1)S(1)}, bf16[513,672]{1,0:T(8,128)(2,1)}, u32[]{:S(2)}, u32[]{:S(2)}) collective-permute-start(bf16[513,672]{1,0:T(8,128)(2,1)S(1)} %pad_maximum_fusion), channel_id=1, source_target_pairs={{0,1},{1,2},{2,3},{3,4},{4,5},{5,6},{6,7},{7,0},{8,9},{9,10},{10,1... | collective-permute-start | bytes 2068424 | tf_op jit(solution)/shard_map/ppermute | solution.py:53
  10.6 24.6 %collective-permute-start.1 = (bf16[513,672]{1,0:T(8,128)(2,1)S(1)}, bf16[513,672]{1,0:T(8,128)(2,1)}, u32[]{:S(2)}, u32[]{:S(2)}) collective-permute-start(bf16[513,672]{1,0:T(8,128)(2,1)S(1)} %pad_maximum_fusion), channel_id=1, source_target_pairs={{0,2},{1,3},{2,4},{3,5},{4,6},{5,7},{6,0},{7,1},{8,10},{9,11},{10,... | collective-permute-start | bytes 2068424 | tf_op jit(solution)/shard_map/ppermute | solution.py:53
  12.2 54.6 %collective-permute-start.2 = (bf16[513,672]{1,0:T(8,128)(2,1)S(1)}, bf16[513,672]{1,0:T(8,128)(2,1)}, u32[]{:S(2)}, u32[]{:S(2)}) collective-permute-start(bf16[513,672]{1,0:T(8,128)(2,1)S(1)} %pad_maximum_fusion), channel_id=1, source_target_pairs={{0,3},{1,4},{2,5},{3,6},{4,7},{5,0},{6,1},{7,2},{8,11},{9,12},{10,... | collective-permute-start | bytes 2068424 | tf_op jit(solution)/shard_map/ppermute | solution.py:53
  14.4 54.4 %collective-permute-start.3 = (bf16[513,672]{1,0:T(8,128)(2,1)S(1)}, bf16[513,672]{1,0:T(8,128)(2,1)S(1)}, u32[]{:S(2)}, u32[]{:S(2)}) collective-permute-start(bf16[513,672]{1,0:T(8,128)(2,1)S(1)} %pad_maximum_fusion), channel_id=1, source_target_pairs={{0,4},{1,5},{2,6},{3,7},{4,0},{5,1},{6,2},{7,3},{8,12},{9,13},{10,... | collective-permute-start | bytes 2068424 | tf_op jit(solution)/shard_map/ppermute | solution.py:53
  16.3 64.9 %collective-permute-start.4 = (bf16[513,672]{1,0:T(8,128)(2,1)S(1)}, bf16[513,672]{1,0:T(8,128)(2,1)S(1)}, u32[]{:S(2)}, u32[]{:S(2)}) collective-permute-start(bf16[513,672]{1,0:T(8,128)(2,1)S(1)} %pad_maximum_fusion), channel_id=1, source_target_pairs={{0,5},{1,6},{2,7},{3,0},{4,1},{5,2},{6,3},{7,4},{8,13},{9,14},{10,... | collective-permute-start | bytes 2068424 | tf_op jit(solution)/shard_map/ppermute | solution.py:53
  31.3 50.8 %collective-permute-start.5 = (bf16[513,672]{1,0:T(8,128)(2,1)S(1)}, bf16[513,672]{1,0:T(8,128)(2,1)S(1)}, u32[]{:S(2)}, u32[]{:S(2)}) collective-permute-start(bf16[513,672]{1,0:T(8,128)(2,1)S(1)} %pad_maximum_fusion), channel_id=1, source_target_pairs={{0,6},{1,7},{2,0},{3,1},{4,2},{5,3},{6,4},{7,5},{8,14},{9,15},{10,... | collective-permute-start | bytes 2068424 | tf_op jit(solution)/shard_map/ppermute | solution.py:53
  35.2 47.9 %collective-permute-start.6 = (bf16[513,672]{1,0:T(8,128)(2,1)S(1)}, bf16[513,672]{1,0:T(8,128)(2,1)S(1)}, u32[]{:S(2)}, u32[]{:S(2)}) collective-permute-start(bf16[513,672]{1,0:T(8,128)(2,1)S(1)} %pad_maximum_fusion), channel_id=1, source_target_pairs={{0,7},{1,0},{2,1},{3,2},{4,3},{5,4},{6,5},{7,6},{8,15},{9,8},{10,9... | collective-permute-start | bytes 2068424 | tf_op jit(solution)/shard_map/ppermute | solution.py:53
  131.0 30.9 %copy-start = (bf16[8,512,672]{2,1,0:T(8,128)(2,1)S(1)}, bf16[8,512,672]{2,1,0:T(8,128)(2,1)}, u32[]{:S(2)}) copy-start(bf16[8,512,672]{2,1,0:T(8,128)(2,1)} %fusion.3) | copy-start | bytes 16515076
  131.4 30.4 %collective-permute-start.7 = (bf16[512,512]{0,1:T(8,128)(2,1)S(1)}, bf16[512,512]{0,1:T(8,128)(2,1)S(1)}, u32[]{:S(2)}, u32[]{:S(2)}) collective-permute-start(bf16[512,512]{0,1:T(8,128)(2,1)S(1)} %pad_maximum_fusion.3), channel_id=1, source_target_pairs={{0,16},{8,24},{16,32},{24,40},{32,48},{40,56},{48,64},{56,72},{64,... | collective-permute-start | bytes 1572872 | tf_op jit(solution)/shard_map/ppermute | solution.py:18
  135.5 32.4 %collective-permute-start.9 = (bf16[512,256]{0,1:T(8,128)(2,1)S(1)}, bf16[512,256]{0,1:T(8,128)(2,1)S(1)}, u32[]{:S(2)}, u32[]{:S(2)}) collective-permute-start(bf16[512,256]{0,1:T(8,128)(2,1)S(1)} %bitcast.81), channel_id=1, source_target_pairs={{0,8},{8,16},{16,24},{24,32},{32,40},{40,48},{48,56},{56,64},{64,7... | collective-permute-start | bytes 786440 | tf_op jit(solution)/shard_map/ppermute | solution.py:18
  140.2 30.1 %collective-permute-start.8 = (bf16[512,256]{0,1:T(8,128)(2,1)S(1)}, bf16[512,256]{0,1:T(8,128)(2,1)S(1)}, u32[]{:S(2)}, u32[]{:S(2)}) collective-permute-start(bf16[512,256]{0,1:T(8,128)(2,1)S(1)} %slice.83), channel_id=1, source_target_pairs={{0,8},{8,16},{16,24},{24,32},{32,40},{40,48},{48,56},{56,64},{64,7... | collective-permute-start | bytes 786440 | tf_op jit(solution)/shard_map/ppermute | solution.py:18
Sparse Core Ops, SparseCore 0:
  9.9 112.7 all-gather.1
  191.5 42.1 reduce-scatter.1

commit v12 on v7

--- a/solution.py
+++ b/solution.py
@@ -78,7 +78,7 @@
     reach = (WINDOW - 1 + rows - 1) // rows
     earlier_keys = [shifted(key, "tok", offset) for offset in range(reach, 0, -1)]
     earlier_values = [shifted(value_rows, "tok", offset) for offset in range(reach, 0, -1)]
-    normed_late, _ = lax.optimization_barrier((normed, earlier_keys[0]))
+    normed_late, _ = lax.optimization_barrier((normed, value_rows))
     query_raw = jnp.einsum(
         "jrc,jcn->rn", normed_late, weights3[:, :, :width_query], preferred_element_type=jnp.float32
     )

time: 229 us -> 228 us (level)
    ppermute x7, waiting for transfers between devices: 36.3 us -> 33.8 us  [local(): lax.ppermute(with_gain, 'hid', [(i, (i + k) % n_hid) for i in range(n_hid)])]
where the time goes in v12:
time: 228 us; the launch traced here: 227 us
  waiting for transfers between devices  108 us (47%)
  starting transfers between devices  37.7 us (17%)
  matrix products  31.2 us (14%)
  other arithmetic  18.7 us (8%)
  local copies, waits for them, and re-layouts  18.1 us (8%)
  between operations  13.7 us (6%)
    reduce_scatter x1, waiting for transfers between devices, local(): lax.psum_scatter(partial_value.astype(jnp.bfloat16), 'hid', scatter_dimen...  40.7 us
    ppermute x7, waiting for transfers between devices, local(): lax.ppermute(with_gain, 'hid', [(i, (i + k) % n_hid) for i in range(n_hid)])  33.8 us
    ppermute x7, starting transfers between devices, local(): lax.ppermute(with_gain, 'hid', [(i, (i + k) % n_hid) for i in range(n_hid)])  24.1 us
    all_gather x1, waiting for transfers between devices, local(): lax.all_gather(jnp.concatenate([w_query, w_key, value_matrix], axis=1), '...  22.4 us
    ppermute x4, starting transfers between devices, shifted(): lax.ppermute(value, axis, [(source, source + steps) for source in range(l...  13.5 us
    ppermute x4, waiting for transfers between devices, shifted(): lax.ppermute(value, axis, [(source, source + steps) for source in range(l...  11.2 us
    unnamed x16, local copies, waits for them, and re-layouts  10.6 us
    sub x1, matrix products, local(): weights = jnp.where(allowed, jnp.exp(masked - top), 0.0)  8.49 us
  transfers between devices with their start and end apart: 13, of which 9 were waited for; matrix products, arithmetic and copies ran while one was open for 21% of the time, Pallas kernels for 0%

profile of v12, /device:TPU:2, one launch (start us, length us, event | category | flops | bytes accessed | tf_op | source)
XLA Modules:
  0.0 227.4 jit_solution(2095363195359412151)
XLA Ops:
  6.5 1.8 pad_maximum_fusion.4
  8.4 1.4 copy.18
  9.8 0.8 pad_maximum_fusion
  10.6 1.7 collective-permute-start.1
  12.2 2.2 collective-permute-start.2
  14.4 1.8 collective-permute-start.3
  16.3 1.8 collective-permute-start.4
  18.2 0.5 multiply_cosine_fusion
  18.7 1.9 and_and_fusion
  20.6 0.7 bitcast_convert_fusion
  21.2 0.7 bitcast_convert_fusion.1
  21.9 1.6 bitcast_dynamic-update-slice_fusion.7
  23.6 7.7 %collective-permute-done = bf16[513,672]{1,0:T(8,128)(2,1)} collective-permute-done((bf16[513,672]{1,0:T(8,128)(2,1)S(1)}, bf16[513,672]{1,0:T(8,128)(2,1)}, u32[]{:S(2)}, u32[]{:S(2)}) %collective-permute-start) | collective-permute-done | bytes 689504 | tf_op jit(solution)/shard_map/ppermute | solution.py:53
  31.3 1.8 collective-permute-start.5
  33.1 2.1 bitcast_dynamic-update-slice_fusion.6
  35.2 14.7 %collective-permute-start.6 = (bf16[513,672]{1,0:T(8,128)(2,1)S(1)}, bf16[513,672]{1,0:T(8,128)(2,1)S(1)}, u32[]{:S(2)}, u32[]{:S(2)}) collective-permute-start(bf16[513,672]{1,0:T(8,128)(2,1)S(1)} %pad_maximum_fusion), channel_id=1, source_target_pairs={{0,7},{1,0},{2,1},{3,2},{4,3},{5,4},{6,5},{7,6},{8,15},{9,8},{10,9... | collective-permute-start | bytes 2068424 | tf_op jit(solution)/shard_map/ppermute | solution.py:53
  49.9 2.1 bitcast_dynamic-update-slice_fusion.5
  52.1 14.7 %collective-permute-done.2 = bf16[513,672]{1,0:T(8,128)(2,1)} collective-permute-done((bf16[513,672]{1,0:T(8,128)(2,1)S(1)}, bf16[513,672]{1,0:T(8,128)(2,1)}, u32[]{:S(2)}, u32[]{:S(2)}) %collective-permute-start.2) | collective-permute-done | bytes 689504 | tf_op jit(solution)/shard_map/ppermute | solution.py:53
  66.8 2.1 bitcast_dynamic-update-slice_fusion.4
  68.9 0.9 bitcast_dynamic-update-slice_fusion.3
  69.8 11.3 %collective-permute-done.4 = bf16[513,672]{1,0:T(8,128)(2,1)S(1)} collective-permute-done((bf16[513,672]{1,0:T(8,128)(2,1)S(1)}, bf16[513,672]{1,0:T(8,128)(2,1)S(1)}, u32[]{:S(2)}, u32[]{:S(2)}) %collective-permute-start.4) | collective-permute-done | bytes 689504 | tf_op jit(solution)/shard_map/ppermute | solution.py:53
  81.1 1.0 bitcast_dynamic-update-slice_fusion.2
  82.1 1.0 bitcast_dynamic-update-slice_fusion.1
  83.1 1.0 bitcast_dynamic-update-slice_fusion
  84.1 6.5 %gather_fusion = bf16[8,513,672]{2,1,0:T(8,128)(2,1)} fusion(bf16[8,513,672]{2,1,0:T(8,128)(2,1)} %bitcast_dynamic-update-slice_fusion, s32[1024]{0:T(1024)S(1)} %pad_clamp_fusion), kind=kCustom, calls=%fused_computation | custom fusion | bytes 11031584 | tf_op jit(solution)/shard_map/jit(_take)/gather | solution.py:57
  90.6 3.7 %broadcast_select_fusion = bf16[8,513,672]{2,1,0:T(8,128)(2,1)S(1)} fusion(bf16[8,513,672]{2,1,0:T(8,128)(2,1)} %gather_fusion, pred[8]{0:T(512)(128)(4,1)S(1)} %compare_and_fusion), kind=kLoop, calls=%fused_computation.11 | loop fusion | flops 2757888 | bytes 11031560 | tf_op jit(solution)/shard_map/jit(_take)/select_n | solution.py:57
  94.3 1.4 fusion.1
  95.7 4.7 %fusion.3 = bf16[8,512,672]{2,1,0:T(8,128)(2,1)} fusion(f32[8,672]{1,0:T(8,128)S(1)} %bitcast.86, f32[512]{0:T(512)S(1)} %add_rsqrt_fusion.2, bf16[8,513,672]{2,1,0:T(8,128)(2,1)S(1)} %broadcast_select_fusion), kind=kLoop, calls=%fused_computation.6 | loop fusion | flops 11010048 | bytes 11033600 | tf_op jit(solution)/shard_map/convert_element_type | solution.py:62
  100.4 22.4 %all-gather.2.cloned.1.call-done = bf16[5376,1024]{1,0:T(8,128)(2,1)} async-done(((bf16[168,1024]{1,0:T(8,128)(2,1)}), bf16[5376,1024]{1,0:T(8,128)(2,1)}) %all-gather.2.cloned.1.call-update) | async-done | bytes 11010064 | tf_op jit(solution)/shard_map/all_gather | solution.py:65
  122.7 8.4 %fusion.14 = f32[512,512]{0,1:T(8,128)S(1)} fusion(bf16[8,512,672]{2,1,0:T(8,128)(2,1)} %fusion.3, bf16[8,672,1024]{2,1,0:T(8,128)(2,1)} %bitcast.87), kind=kOutput, calls=%fused_computation.22 | convolution fusion | flops 2818572288 | bytes 12845056 | tf_op jit(solution)/shard_map/jrc,jcn->rn/dot_general | solution.py:69
  131.1 0.1 multiply_reduce_fusion.1
  131.2 0.1 multiply_multiply_fusion.1
  131.3 0.1 subtract_convert_fusion.1
  131.5 1.9 collective-permute-start.10
  133.4 5.4 %collective-permute-start.9 = (bf16[512,256]{0,1:T(8,128)(2,1)S(1)}, bf16[512,256]{0,1:T(8,128)(2,1)S(1)}, u32[]{:S(2)}, u32[]{:S(2)}) collective-permute-start(bf16[512,256]{0,1:T(8,128)(2,1)S(1)} %bitcast.81), channel_id=1, source_target_pairs={{0,16},{8,24},{16,32},{24,40},{32,48},{40,56},{48,64},{56,72},{64,... | collective-permute-start | bytes 786440 | tf_op jit(solution)/shard_map/ppermute | solution.py:18
  138.8 3.4 %collective-permute-start.7 = (bf16[512,256]{0,1:T(8,128)(2,1)S(1)}, bf16[512,256]{0,1:T(8,128)(2,1)S(1)}, u32[]{:S(2)}, u32[]{:S(2)}) collective-permute-start(bf16[512,256]{0,1:T(8,128)(2,1)S(1)} %slice.73), channel_id=1, source_target_pairs={{0,16},{8,24},{16,32},{24,40},{32,48},{40,56},{48,64},{56,72},{64,... | collective-permute-start | bytes 786440 | tf_op jit(solution)/shard_map/ppermute | solution.py:18
  142.2 2.8 %collective-permute-start.8 = (bf16[512,256]{0,1:T(8,128)(2,1)S(1)}, bf16[512,256]{0,1:T(8,128)(2,1)S(1)}, u32[]{:S(2)}, u32[]{:S(2)}) collective-permute-start(bf16[512,256]{0,1:T(8,128)(2,1)S(1)} %slice.73), channel_id=1, source_target_pairs={{0,8},{8,16},{16,24},{24,32},{32,40},{40,48},{48,56},{56,64},{64,7... | collective-permute-start | bytes 786440 | tf_op jit(solution)/shard_map/ppermute | solution.py:18
  145.0 5.5 %fusion.10 = f32[512,512,1]{0,1,2:T(8,128)S(1)} fusion(bf16[8,512,672]{2,1,0:T(8,128)(2,1)S(1)} %copy-done, bf16[8,672,1024]{2,1,0:T(8,128)(2,1)} %bitcast.88), kind=kOutput, calls=%fused_computation.17 | convolution fusion | flops 2818572288 | bytes 12058624 | tf_op jit(solution)/shard_map/jrc,jcn->rn/dot_general | solution.py:82
  150.6 0.1 multiply_reduce_fusion
  150.7 0.2 multiply_multiply_fusion
  150.9 0.2 subtract_convert_fusion
  151.1 3.3 %collective-permute-done.9 = bf16[512,256]{0,1:T(8,128)(2,1)S(1)} collective-permute-done((bf16[512,256]{0,1:T(8,128)(2,1)S(1)}, bf16[512,256]{0,1:T(8,128)(2,1)S(1)}, u32[]{:S(2)}, u32[]{:S(2)}) %collective-permute-start.9) | collective-permute-done | bytes 262176 | tf_op jit(solution)/shard_map/ppermute | solution.py:18
  154.5 8.5 %fusion.35 = (f32[2,2,512]{2,1,0:T(2,128)S(1)}, bf16[2,2,512,1536]{2,3,1,0:T(8,128)(2,1)}) fusion(pred[512,1536]{0,1:T(8,128)(4,1)S(1)} %copy-done.1, bf16[1536,2,128,1]{0,2,3,1:T(8,128)(2,1)S(1)} %bitcast.83, bf16[512,2,2,128]{0,3,2,1:T(8,128)(2,1)S(1)} %bitcast.85), kind=kOutput, calls=%fused_computation.80 | convolution fusion | flops 824182272 | bytes 8396800 | tf_op jit(solution)/shard_map/sub | solution.py:108
  163.0 3.7 %collective-permute-done.7 = bf16[512,256]{0,1:T(8,128)(2,1)S(1)} collective-permute-done((bf16[512,256]{0,1:T(8,128)(2,1)S(1)}, bf16[512,256]{0,1:T(8,128)(2,1)S(1)}, u32[]{:S(2)}, u32[]{:S(2)}) %collective-permute-start.7) | collective-permute-done | bytes 262176 | tf_op jit(solution)/shard_map/ppermute | solution.py:18
  166.8 4.1 %collective-permute-done.8 = bf16[512,256]{0,1:T(8,128)(2,1)S(1)} collective-permute-done((bf16[512,256]{0,1:T(8,128)(2,1)S(1)}, bf16[512,256]{0,1:T(8,128)(2,1)S(1)}, u32[]{:S(2)}, u32[]{:S(2)}) %collective-permute-start.8) | collective-permute-done | bytes 262176 | tf_op jit(solution)/shard_map/ppermute | solution.py:18
  170.9 3.9 %fusion.25 = bf16[512,2,2,128]{0,3,2,1:T(8,128)(2,1)S(1)} fusion(bf16[1536,2,128,1]{0,2,3,1:T(8,128)(2,1)S(1)} %bitcast.84, bf16[2,2,512,1536]{2,3,1,0:T(8,128)(2,1)} %get-tuple-element.14, f32[512,2,2]{0,2,1:T(2,128)S(1)} %bitcast.92), kind=kOutput, calls=%fused_computation.26 | convolution fusion | flops 805830656 | bytes 7610368 | tf_op jit(solution)/shard_map/kgts,skd->tkgd/dot_general | solution.py:111
  174.9 5.0 %convolution_convert_fusion = bf16[512,5376]{0,1:T(8,128)(2,1)} fusion(bf16[512,512]{0,1:T(8,128)(2,1)S(1)} %bitcast.91, bf16[512,5376]{1,0:T(8,128)(2,1)S(1)} %bitcast.90), kind=kOutput, calls=%fused_computation.10 | convolution fusion | flops 2821324800 | bytes 11534336 | tf_op jit(solution)/shard_map/dot_general | solution.py:116
  179.8 40.7 %reduce-scatter.2.cloned.1.call-done = bf16[512,672]{0,1:T(8,128)(2,1)} async-done(((bf16[512,5376]{0,1:T(8,128)(2,1)}), bf16[512,672]{0,1:T(8,128)(2,1)}) %reduce-scatter.2.cloned.1.call-update) | async-done | bytes 688144 | tf_op jit(solution)/shard_map/reduce_scatter | solution.py:117
  (37 shorter events, 0.5 us)
Async XLA Ops:
  6.5 116.2 %all-gather.2.cloned.1.call-start = ((), (), s32[]{:S(2)}) async-start(), calls=%async_computation.1 | async-start | bytes 11354112 | tf_op jit(solution)/shard_map/all_gather | solution.py:65
  8.3 212.2 %reduce-scatter.2.cloned.1.call-start = ((), (), s32[]{:S(2)}) async-start(), calls=%async_computation.2 | async-start | bytes 6193152 | tf_op jit(solution)/shard_map/reduce_scatter | solution.py:117
  10.5 20.8 %collective-permute-start = (bf16[513,672]{1,0:T(8,128)(2,1)S(1)}, bf16[513,672]{1,0:T(8,128)(2,1)}, u32[]{:S(2)}, u32[]{:S(2)}) collective-permute-start(bf16[513,672]{1,0:T(8,128)(2,1)S(1)} %pad_maximum_fusion), channel_id=1, source_target_pairs={{0,1},{1,2},{2,3},{3,4},{4,5},{5,6},{6,7},{7,0},{8,9},{9,10},{10,1... | collective-permute-start | bytes 2068424 | tf_op jit(solution)/shard_map/ppermute | solution.py:53
  10.6 24.6 %collective-permute-start.1 = (bf16[513,672]{1,0:T(8,128)(2,1)S(1)}, bf16[513,672]{1,0:T(8,128)(2,1)}, u32[]{:S(2)}, u32[]{:S(2)}) collective-permute-start(bf16[513,672]{1,0:T(8,128)(2,1)S(1)} %pad_maximum_fusion), channel_id=1, source_target_pairs={{0,2},{1,3},{2,4},{3,5},{4,6},{5,7},{6,0},{7,1},{8,10},{9,11},{10,... | collective-permute-start | bytes 2068424 | tf_op jit(solution)/shard_map/ppermute | solution.py:53
  12.2 54.6 %collective-permute-start.2 = (bf16[513,672]{1,0:T(8,128)(2,1)S(1)}, bf16[513,672]{1,0:T(8,128)(2,1)}, u32[]{:S(2)}, u32[]{:S(2)}) collective-permute-start(bf16[513,672]{1,0:T(8,128)(2,1)S(1)} %pad_maximum_fusion), channel_id=1, source_target_pairs={{0,3},{1,4},{2,5},{3,6},{4,7},{5,0},{6,1},{7,2},{8,11},{9,12},{10,... | collective-permute-start | bytes 2068424 | tf_op jit(solution)/shard_map/ppermute | solution.py:53
  14.4 54.4 %collective-permute-start.3 = (bf16[513,672]{1,0:T(8,128)(2,1)S(1)}, bf16[513,672]{1,0:T(8,128)(2,1)S(1)}, u32[]{:S(2)}, u32[]{:S(2)}) collective-permute-start(bf16[513,672]{1,0:T(8,128)(2,1)S(1)} %pad_maximum_fusion), channel_id=1, source_target_pairs={{0,4},{1,5},{2,6},{3,7},{4,0},{5,1},{6,2},{7,3},{8,12},{9,13},{10,... | collective-permute-start | bytes 2068424 | tf_op jit(solution)/shard_map/ppermute | solution.py:53
  16.3 64.9 %collective-permute-start.4 = (bf16[513,672]{1,0:T(8,128)(2,1)S(1)}, bf16[513,672]{1,0:T(8,128)(2,1)S(1)}, u32[]{:S(2)}, u32[]{:S(2)}) collective-permute-start(bf16[513,672]{1,0:T(8,128)(2,1)S(1)} %pad_maximum_fusion), channel_id=1, source_target_pairs={{0,5},{1,6},{2,7},{3,0},{4,1},{5,2},{6,3},{7,4},{8,13},{9,14},{10,... | collective-permute-start | bytes 2068424 | tf_op jit(solution)/shard_map/ppermute | solution.py:53
  31.3 50.8 %collective-permute-start.5 = (bf16[513,672]{1,0:T(8,128)(2,1)S(1)}, bf16[513,672]{1,0:T(8,128)(2,1)S(1)}, u32[]{:S(2)}, u32[]{:S(2)}) collective-permute-start(bf16[513,672]{1,0:T(8,128)(2,1)S(1)} %pad_maximum_fusion), channel_id=1, source_target_pairs={{0,6},{1,7},{2,0},{3,1},{4,2},{5,3},{6,4},{7,5},{8,14},{9,15},{10,... | collective-permute-start | bytes 2068424 | tf_op jit(solution)/shard_map/ppermute | solution.py:53
  35.2 47.9 %collective-permute-start.6 = (bf16[513,672]{1,0:T(8,128)(2,1)S(1)}, bf16[513,672]{1,0:T(8,128)(2,1)S(1)}, u32[]{:S(2)}, u32[]{:S(2)}) collective-permute-start(bf16[513,672]{1,0:T(8,128)(2,1)S(1)} %pad_maximum_fusion), channel_id=1, source_target_pairs={{0,7},{1,0},{2,1},{3,2},{4,3},{5,4},{6,5},{7,6},{8,15},{9,8},{10,9... | collective-permute-start | bytes 2068424 | tf_op jit(solution)/shard_map/ppermute | solution.py:53
  122.7 22.3 %copy-start = (bf16[8,512,672]{2,1,0:T(8,128)(2,1)S(1)}, bf16[8,512,672]{2,1,0:T(8,128)(2,1)}, u32[]{:S(2)}) copy-start(bf16[8,512,672]{2,1,0:T(8,128)(2,1)} %fusion.3) | copy-start | bytes 16515076
  131.5 19.7 %collective-permute-start.10 = (bf16[512,256]{0,1:T(8,128)(2,1)S(1)}, bf16[512,256]{0,1:T(8,128)(2,1)S(1)}, u32[]{:S(2)}, u32[]{:S(2)}) collective-permute-start(bf16[512,256]{0,1:T(8,128)(2,1)S(1)} %bitcast.80), channel_id=1, source_target_pairs={{0,8},{8,16},{16,24},{24,32},{32,40},{40,48},{48,56},{56,64},{64,7... | collective-permute-start | bytes 786440 | tf_op jit(solution)/shard_map/ppermute | solution.py:18
  133.4 21.1 %collective-permute-start.9 = (bf16[512,256]{0,1:T(8,128)(2,1)S(1)}, bf16[512,256]{0,1:T(8,128)(2,1)S(1)}, u32[]{:S(2)}, u32[]{:S(2)}) collective-permute-start(bf16[512,256]{0,1:T(8,128)(2,1)S(1)} %bitcast.81), channel_id=1, source_target_pairs={{0,16},{8,24},{16,32},{24,40},{32,48},{40,56},{48,64},{56,72},{64,... | collective-permute-start | bytes 786440 | tf_op jit(solution)/shard_map/ppermute | solution.py:18
  138.8 27.9 %collective-permute-start.7 = (bf16[512,256]{0,1:T(8,128)(2,1)S(1)}, bf16[512,256]{0,1:T(8,128)(2,1)S(1)}, u32[]{:S(2)}, u32[]{:S(2)}) collective-permute-start(bf16[512,256]{0,1:T(8,128)(2,1)S(1)} %slice.73), channel_id=1, source_target_pairs={{0,16},{8,24},{16,32},{24,40},{32,48},{40,56},{48,64},{56,72},{64,... | collective-permute-start | bytes 786440 | tf_op jit(solution)/shard_map/ppermute | solution.py:18
  142.2 28.7 %collective-permute-start.8 = (bf16[512,256]{0,1:T(8,128)(2,1)S(1)}, bf16[512,256]{0,1:T(8,128)(2,1)S(1)}, u32[]{:S(2)}, u32[]{:S(2)}) collective-permute-start(bf16[512,256]{0,1:T(8,128)(2,1)S(1)} %slice.73), channel_id=1, source_target_pairs={{0,8},{8,16},{16,24},{24,32},{32,40},{40,48},{48,56},{56,64},{64,7... | collective-permute-start | bytes 786440 | tf_op jit(solution)/shard_map/ppermute | solution.py:18
  150.6 4.0 %copy-start.1 = (pred[512,1536]{0,1:T(8,128)(4,1)S(1)}, pred[512,1536]{0,1:T(8,128)(4,1)}, u32[]{:S(2)}) copy-start(pred[512,1536]{0,1:T(8,128)(4,1)} %and_and_fusion) | copy-start | bytes 2359300
  163.0 11.8 %slice-start = ((s8[5505024]{0:T(1024)(128)(4,1)}), s8[4194304]{0:T(1024)(128)(4,1)S(1)}, s32[]{:S(2)}) async-start(s8[5505024]{0:T(1024)(128)(4,1)} %bitcast.89), calls=%async_computation.3 | async-start | bytes 8388608
  170.9 3.9 %slice-start.1 = ((s8[5505024]{0:T(1024)(128)(4,1)}), s8[1310720]{0:T(1024)(128)(4,1)S(1)}, s32[]{:S(2)}) async-start(s8[5505024]{0:T(1024)(128)(4,1)} %bitcast.89), calls=%async_computation.4 | async-start | bytes 2621440
Sparse Core Ops, SparseCore 0:
  9.9 112.7 all-gather.1
  180.0 40.5 reduce-scatter.1

commit v13 on v12

--- a/solution.py
+++ b/solution.py
@@ -108,8 +108,15 @@
     weights = jnp.where(allowed, jnp.exp(masked - top), 0.0)
     total = jnp.sum(weights, axis=-1)
     probs = weights.astype(jnp.bfloat16)
-    mixed = jnp.einsum(
-        "kgts,skd->tkgd", probs, values_three_axes, preferred_element_type=jnp.float32
+    value_blocks = earlier_values + [value_rows]
+    mixed = sum(
+        jnp.einsum(
+            "kgts,skd->tkgd",
+            probs[..., index * rows : (index + 1) * rows],
+            block.reshape(rows, kv_heads, HEAD_SIZE),
+            preferred_element_type=jnp.float32,
+        )
+        for index, block in enumerate(value_blocks)
     )
     mixed = mixed / jnp.transpose(total, (2, 0, 1))[..., None]
     heads_out = mixed.reshape(rows, width_query).astype(jnp.bfloat16)

time: 228 us -> 231 us (1.013)
  matrix products: 31.2 us -> 37.2 us
  waiting for transfers between devices: 108 us -> 105 us
    dot_general x1, matrix products: 4.96 us -> 8.64 us  [local(): jnp.dot(heads_out, w_out, preferred_element_type=jnp.float32)]
    ppermute x4, waiting for transfers between devices: 11.2 us -> 7.95 us  [shifted(): lax.ppermute(value, axis, [(source, source + steps) for source in range(l...]
    dot_general x1 -> x3, matrix products: 3.89 us -> 6.15 us  [local(): jnp.einsum('kgts,skd->tkgd', probs[..., index * rows:(index + 1) * rows],...]
    unnamed x16 -> x12, local copies, waits for them, and re-layouts: 10.6 us -> 10.6 us
  transfers between devices with their start and end apart: 13 -> 13, of which waited for: 9 -> 8; matrix products, arithmetic and copies ran while one was open for 21% -> 23% of each run, Pallas kernels for 0% -> 0%
where the time goes in v13:
time: 231 us; the launch traced here: 230 us
  waiting for transfers between devices  105 us (45%)
  starting transfers between devices  37.7 us (16%)
  matrix products  37.2 us (16%)
  other arithmetic  18.6 us (8%)
  local copies, waits for them, and re-layouts  18.1 us (8%)
  between operations  13.7 us (6%)
    reduce_scatter x1, waiting for transfers between devices, local(): lax.psum_scatter(partial_value.astype(jnp.bfloat16), 'hid', scatter_dimen...  40.8 us
    ppermute x7, waiting for transfers between devices, local(): lax.ppermute(with_gain, 'hid', [(i, (i + k) % n_hid) for i in range(n_hid)])  33.8 us
    ppermute x7, starting transfers between devices, local(): lax.ppermute(with_gain, 'hid', [(i, (i + k) % n_hid) for i in range(n_hid)])  24.1 us
    all_gather x1, waiting for transfers between devices, local(): lax.all_gather(jnp.concatenate([w_query, w_key, value_matrix], axis=1), '...  22.4 us
    ppermute x4, starting transfers between devices, shifted(): lax.ppermute(value, axis, [(source, source + steps) for source in range(l...  13.5 us
    unnamed x12, local copies, waits for them, and re-layouts  10.6 us
    dot_general x1, matrix products, local(): jnp.dot(heads_out, w_out, preferred_element_type=jnp.float32)  8.64 us
    sub x1, matrix products, local(): weights = jnp.where(allowed, jnp.exp(masked - top), 0.0)  8.5 us
  transfers between devices with their start and end apart: 13, of which 8 were waited for; matrix products, arithmetic and copies ran while one was open for 23% of the time, Pallas kernels for 0%

profile of v13, /device:TPU:2, one launch (start us, length us, event | category | flops | bytes accessed | tf_op | source)
XLA Modules:
  0.0 230.2 jit_solution(14522035944178073101)
XLA Ops:
  6.5 1.8 pad_maximum_fusion.3
  8.4 1.4 copy.22
  9.8 0.8 pad_maximum_fusion
  10.6 1.7 collective-permute-start.1
  12.2 2.2 collective-permute-start.2
  14.4 1.8 collective-permute-start.3
  16.3 1.8 collective-permute-start.4
  18.2 0.5 multiply_cosine_fusion
  18.7 1.9 and_and_fusion
  20.6 0.7 bitcast_convert_fusion
  21.2 0.7 bitcast_convert_fusion.1
  21.9 1.7 bitcast_dynamic-update-slice_fusion.7
  23.6 7.7 %collective-permute-done = bf16[513,672]{1,0:T(8,128)(2,1)} collective-permute-done((bf16[513,672]{1,0:T(8,128)(2,1)S(1)}, bf16[513,672]{1,0:T(8,128)(2,1)}, u32[]{:S(2)}, u32[]{:S(2)}) %collective-permute-start) | collective-permute-done | bytes 689504 | tf_op jit(solution)/shard_map/ppermute | solution.py:53
  31.3 1.8 collective-permute-start.5
  33.1 2.1 bitcast_dynamic-update-slice_fusion.6
  35.2 14.7 %collective-permute-start.6 = (bf16[513,672]{1,0:T(8,128)(2,1)S(1)}, bf16[513,672]{1,0:T(8,128)(2,1)S(1)}, u32[]{:S(2)}, u32[]{:S(2)}) collective-permute-start(bf16[513,672]{1,0:T(8,128)(2,1)S(1)} %pad_maximum_fusion), channel_id=1, source_target_pairs={{0,7},{1,0},{2,1},{3,2},{4,3},{5,4},{6,5},{7,6},{8,15},{9,8},{10,9... | collective-permute-start | bytes 2068424 | tf_op jit(solution)/shard_map/ppermute | solution.py:53
  49.9 2.1 bitcast_dynamic-update-slice_fusion.5
  52.1 14.7 %collective-permute-done.2 = bf16[513,672]{1,0:T(8,128)(2,1)} collective-permute-done((bf16[513,672]{1,0:T(8,128)(2,1)S(1)}, bf16[513,672]{1,0:T(8,128)(2,1)}, u32[]{:S(2)}, u32[]{:S(2)}) %collective-permute-start.2) | collective-permute-done | bytes 689504 | tf_op jit(solution)/shard_map/ppermute | solution.py:53
  66.8 2.1 bitcast_dynamic-update-slice_fusion.4
  68.8 1.0 bitcast_dynamic-update-slice_fusion.3
  69.8 11.3 %collective-permute-done.4 = bf16[513,672]{1,0:T(8,128)(2,1)S(1)} collective-permute-done((bf16[513,672]{1,0:T(8,128)(2,1)S(1)}, bf16[513,672]{1,0:T(8,128)(2,1)S(1)}, u32[]{:S(2)}, u32[]{:S(2)}) %collective-permute-start.4) | collective-permute-done | bytes 689504 | tf_op jit(solution)/shard_map/ppermute | solution.py:53
  81.1 0.9 bitcast_dynamic-update-slice_fusion.2
  82.1 1.0 bitcast_dynamic-update-slice_fusion.1
  83.1 1.0 bitcast_dynamic-update-slice_fusion
  84.1 6.5 %gather_fusion = bf16[8,513,672]{2,1,0:T(8,128)(2,1)} fusion(bf16[8,513,672]{2,1,0:T(8,128)(2,1)} %bitcast_dynamic-update-slice_fusion, s32[1024]{0:T(1024)S(1)} %pad_clamp_fusion), kind=kCustom, calls=%fused_computation | custom fusion | bytes 11031584 | tf_op jit(solution)/shard_map/jit(_take)/gather | solution.py:57
  90.6 3.7 %broadcast_select_fusion = bf16[8,513,672]{2,1,0:T(8,128)(2,1)S(1)} fusion(bf16[8,513,672]{2,1,0:T(8,128)(2,1)} %gather_fusion, pred[8]{0:T(512)(128)(4,1)S(1)} %compare_and_fusion), kind=kLoop, calls=%fused_computation.11 | loop fusion | flops 2757888 | bytes 11031560 | tf_op jit(solution)/shard_map/jit(_take)/select_n | solution.py:57
  94.3 1.4 fusion.1
  95.7 4.7 %fusion.3 = bf16[8,512,672]{2,1,0:T(8,128)(2,1)} fusion(f32[8,672]{1,0:T(8,128)S(1)} %bitcast.98, f32[512]{0:T(512)S(1)} %add_rsqrt_fusion.2, bf16[8,513,672]{2,1,0:T(8,128)(2,1)S(1)} %broadcast_select_fusion), kind=kLoop, calls=%fused_computation.6 | loop fusion | flops 11010048 | bytes 11033600 | tf_op jit(solution)/shard_map/convert_element_type | solution.py:62
  100.4 22.4 %all-gather.2.cloned.1.call-done = bf16[5376,1024]{1,0:T(8,128)(2,1)} async-done(((bf16[168,1024]{1,0:T(8,128)(2,1)}), bf16[5376,1024]{1,0:T(8,128)(2,1)}) %all-gather.2.cloned.1.call-update) | async-done | bytes 11010064 | tf_op jit(solution)/shard_map/all_gather | solution.py:65
  122.7 8.4 %fusion.18 = f32[512,512]{0,1:T(8,128)S(1)} fusion(bf16[8,512,672]{2,1,0:T(8,128)(2,1)} %fusion.3, bf16[8,672,1024]{2,1,0:T(8,128)(2,1)} %bitcast.99), kind=kOutput, calls=%fused_computation.26 | convolution fusion | flops 2818572288 | bytes 12845056 | tf_op jit(solution)/shard_map/jrc,jcn->rn/dot_general | solution.py:69
  131.2 0.1 multiply_multiply_fusion.1
  131.3 0.1 subtract_convert_fusion.1
  131.5 2.7 %collective-permute-start.8 = (bf16[512,256]{0,1:T(8,128)(2,1)S(1)}, bf16[512,256]{0,1:T(8,128)(2,1)S(1)}, u32[]{:S(2)}, u32[]{:S(2)}) collective-permute-start(bf16[512,256]{0,1:T(8,128)(2,1)S(1)} %bitcast.91), channel_id=1, source_target_pairs={{0,16},{8,24},{16,32},{24,40},{32,48},{40,56},{48,64},{56,72},{64,... | collective-permute-start | bytes 786440 | tf_op jit(solution)/shard_map/ppermute | solution.py:18
  134.2 4.7 %collective-permute-start.9 = (bf16[512,256]{0,1:T(8,128)(2,1)S(1)}, bf16[512,256]{0,1:T(8,128)(2,1)S(1)}, u32[]{:S(2)}, u32[]{:S(2)}) collective-permute-start(bf16[512,256]{0,1:T(8,128)(2,1)S(1)} %bitcast.92), channel_id=1, source_target_pairs={{0,8},{8,16},{16,24},{24,32},{32,40},{40,48},{48,56},{56,64},{64,7... | collective-permute-start | bytes 786440 | tf_op jit(solution)/shard_map/ppermute | solution.py:18
  138.8 2.6 %collective-permute-start.10 = (bf16[512,256]{0,1:T(8,128)(2,1)S(1)}, bf16[512,256]{0,1:T(8,128)(2,1)S(1)}, u32[]{:S(2)}, u32[]{:S(2)}) collective-permute-start(bf16[512,256]{0,1:T(8,128)(2,1)S(1)} %slice.104), channel_id=1, source_target_pairs={{0,8},{8,16},{16,24},{24,32},{32,40},{40,48},{48,56},{56,64},{64,7... | collective-permute-start | bytes 786440 | tf_op jit(solution)/shard_map/ppermute | solution.py:18
  141.4 3.6 %collective-permute-start.7 = (bf16[512,256]{0,1:T(8,128)(2,1)S(1)}, bf16[512,256]{0,1:T(8,128)(2,1)S(1)}, u32[]{:S(2)}, u32[]{:S(2)}) collective-permute-start(bf16[512,256]{0,1:T(8,128)(2,1)S(1)} %slice.104), channel_id=1, source_target_pairs={{0,16},{8,24},{16,32},{24,40},{32,48},{40,56},{48,64},{56,72},{64,... | collective-permute-start | bytes 786440 | tf_op jit(solution)/shard_map/ppermute | solution.py:18
  145.0 5.5 %fusion.8 = f32[512,512,1]{0,1,2:T(8,128)S(1)} fusion(bf16[8,512,672]{2,1,0:T(8,128)(2,1)S(1)} %copy-done, bf16[8,672,1024]{2,1,0:T(8,128)(2,1)} %bitcast.100), kind=kOutput, calls=%fused_computation.15 | convolution fusion | flops 2818572288 | bytes 12058624 | tf_op jit(solution)/shard_map/jrc,jcn->rn/dot_general | solution.py:82
  150.6 0.1 multiply_reduce_fusion
  150.7 0.2 multiply_multiply_fusion
  150.9 0.2 subtract_convert_fusion
  151.1 4.0 %collective-permute-done.9 = bf16[512,256]{0,1:T(8,128)(2,1)S(1)} collective-permute-done((bf16[512,256]{0,1:T(8,128)(2,1)S(1)}, bf16[512,256]{0,1:T(8,128)(2,1)S(1)}, u32[]{:S(2)}, u32[]{:S(2)}) %collective-permute-start.9) | collective-permute-done | bytes 262176 | tf_op jit(solution)/shard_map/ppermute | solution.py:18
  155.2 8.5 %fusion.45 = (f32[2,2,512]{2,1,0:T(2,128)S(1)}, bf16[2,2,512,1536]{2,3,1,0:T(8,128)(2,1)}) fusion(pred[512,1536]{0,1:T(8,128)(4,1)S(1)} %copy-done.1, bf16[1536,2,128,1]{0,2,3,1:T(8,128)(2,1)S(1)} %bitcast.95, bf16[512,2,2,128]{0,3,2,1:T(8,128)(2,1)S(1)} %bitcast.96), kind=kOutput, calls=%fused_computation.85 | convolution fusion | flops 824182272 | bytes 8396800 | tf_op jit(solution)/shard_map/sub | solution.py:108
  163.7 2.0 fusion.14
  165.7 2.0 fusion.12
  167.7 4.0 %collective-permute-done.7 = bf16[512,256]{0,1:T(8,128)(2,1)S(1)} collective-permute-done((bf16[512,256]{0,1:T(8,128)(2,1)S(1)}, bf16[512,256]{0,1:T(8,128)(2,1)S(1)}, u32[]{:S(2)}, u32[]{:S(2)}) %collective-permute-start.7) | collective-permute-done | bytes 262176 | tf_op jit(solution)/shard_map/ppermute | solution.py:18
  171.7 2.1 fusion.35
  173.8 8.6 %convolution_convert_fusion = bf16[512,5376]{0,1:T(8,128)(2,1)} fusion(bf16[512,512]{0,1:T(8,128)(2,1)S(1)} %bitcast.102, bf16[512,5376]{1,0:T(8,128)(2,1)} %param.15), kind=kOutput, calls=%fused_computation.10 | convolution fusion | flops 2821324800 | bytes 11534336 | tf_op jit(solution)/shard_map/dot_general | solution.py:123
  182.5 40.8 %reduce-scatter.2.cloned.1.call-done = bf16[512,672]{0,1:T(8,128)(2,1)} async-done(((bf16[512,5376]{0,1:T(8,128)(2,1)}), bf16[512,672]{0,1:T(8,128)(2,1)}) %reduce-scatter.2.cloned.1.call-update) | async-done | bytes 688144 | tf_op jit(solution)/shard_map/reduce_scatter | solution.py:124
  (33 shorter events, 0.5 us)
Async XLA Ops:
  6.5 116.2 %all-gather.2.cloned.1.call-start = ((), (), s32[]{:S(2)}) async-start(), calls=%async_computation.1 | async-start | bytes 11354112 | tf_op jit(solution)/shard_map/all_gather | solution.py:65
  8.3 215.0 %reduce-scatter.2.cloned.1.call-start = ((), (), s32[]{:S(2)}) async-start(), calls=%async_computation.2 | async-start | bytes 6193152 | tf_op jit(solution)/shard_map/reduce_scatter | solution.py:124
  10.5 20.8 %collective-permute-start = (bf16[513,672]{1,0:T(8,128)(2,1)S(1)}, bf16[513,672]{1,0:T(8,128)(2,1)}, u32[]{:S(2)}, u32[]{:S(2)}) collective-permute-start(bf16[513,672]{1,0:T(8,128)(2,1)S(1)} %pad_maximum_fusion), channel_id=1, source_target_pairs={{0,1},{1,2},{2,3},{3,4},{4,5},{5,6},{6,7},{7,0},{8,9},{9,10},{10,1... | collective-permute-start | bytes 2068424 | tf_op jit(solution)/shard_map/ppermute | solution.py:53
  10.6 24.6 %collective-permute-start.1 = (bf16[513,672]{1,0:T(8,128)(2,1)S(1)}, bf16[513,672]{1,0:T(8,128)(2,1)}, u32[]{:S(2)}, u32[]{:S(2)}) collective-permute-start(bf16[513,672]{1,0:T(8,128)(2,1)S(1)} %pad_maximum_fusion), channel_id=1, source_target_pairs={{0,2},{1,3},{2,4},{3,5},{4,6},{5,7},{6,0},{7,1},{8,10},{9,11},{10,... | collective-permute-start | bytes 2068424 | tf_op jit(solution)/shard_map/ppermute | solution.py:53
  12.2 54.6 %collective-permute-start.2 = (bf16[513,672]{1,0:T(8,128)(2,1)S(1)}, bf16[513,672]{1,0:T(8,128)(2,1)}, u32[]{:S(2)}, u32[]{:S(2)}) collective-permute-start(bf16[513,672]{1,0:T(8,128)(2,1)S(1)} %pad_maximum_fusion), channel_id=1, source_target_pairs={{0,3},{1,4},{2,5},{3,6},{4,7},{5,0},{6,1},{7,2},{8,11},{9,12},{10,... | collective-permute-start | bytes 2068424 | tf_op jit(solution)/shard_map/ppermute | solution.py:53
  14.4 54.4 %collective-permute-start.3 = (bf16[513,672]{1,0:T(8,128)(2,1)S(1)}, bf16[513,672]{1,0:T(8,128)(2,1)S(1)}, u32[]{:S(2)}, u32[]{:S(2)}) collective-permute-start(bf16[513,672]{1,0:T(8,128)(2,1)S(1)} %pad_maximum_fusion), channel_id=1, source_target_pairs={{0,4},{1,5},{2,6},{3,7},{4,0},{5,1},{6,2},{7,3},{8,12},{9,13},{10,... | collective-permute-start | bytes 2068424 | tf_op jit(solution)/shard_map/ppermute | solution.py:53
  16.3 64.9 %collective-permute-start.4 = (bf16[513,672]{1,0:T(8,128)(2,1)S(1)}, bf16[513,672]{1,0:T(8,128)(2,1)S(1)}, u32[]{:S(2)}, u32[]{:S(2)}) collective-permute-start(bf16[513,672]{1,0:T(8,128)(2,1)S(1)} %pad_maximum_fusion), channel_id=1, source_target_pairs={{0,5},{1,6},{2,7},{3,0},{4,1},{5,2},{6,3},{7,4},{8,13},{9,14},{10,... | collective-permute-start | bytes 2068424 | tf_op jit(solution)/shard_map/ppermute | solution.py:53
  31.3 50.8 %collective-permute-start.5 = (bf16[513,672]{1,0:T(8,128)(2,1)S(1)}, bf16[513,672]{1,0:T(8,128)(2,1)S(1)}, u32[]{:S(2)}, u32[]{:S(2)}) collective-permute-start(bf16[513,672]{1,0:T(8,128)(2,1)S(1)} %pad_maximum_fusion), channel_id=1, source_target_pairs={{0,6},{1,7},{2,0},{3,1},{4,2},{5,3},{6,4},{7,5},{8,14},{9,15},{10,... | collective-permute-start | bytes 2068424 | tf_op jit(solution)/shard_map/ppermute | solution.py:53
  35.2 47.9 %collective-permute-start.6 = (bf16[513,672]{1,0:T(8,128)(2,1)S(1)}, bf16[513,672]{1,0:T(8,128)(2,1)S(1)}, u32[]{:S(2)}, u32[]{:S(2)}) collective-permute-start(bf16[513,672]{1,0:T(8,128)(2,1)S(1)} %pad_maximum_fusion), channel_id=1, source_target_pairs={{0,7},{1,0},{2,1},{3,2},{4,3},{5,4},{6,5},{7,6},{8,15},{9,8},{10,9... | collective-permute-start | bytes 2068424 | tf_op jit(solution)/shard_map/ppermute | solution.py:53
  122.7 22.3 %copy-start = (bf16[8,512,672]{2,1,0:T(8,128)(2,1)S(1)}, bf16[8,512,672]{2,1,0:T(8,128)(2,1)}, u32[]{:S(2)}) copy-start(bf16[8,512,672]{2,1,0:T(8,128)(2,1)} %fusion.3) | copy-start | bytes 16515076
  131.5 19.7 %collective-permute-start.8 = (bf16[512,256]{0,1:T(8,128)(2,1)S(1)}, bf16[512,256]{0,1:T(8,128)(2,1)S(1)}, u32[]{:S(2)}, u32[]{:S(2)}) collective-permute-start(bf16[512,256]{0,1:T(8,128)(2,1)S(1)} %bitcast.91), channel_id=1, source_target_pairs={{0,16},{8,24},{16,32},{24,40},{32,48},{40,56},{48,64},{56,72},{64,... | collective-permute-start | bytes 786440 | tf_op jit(solution)/shard_map/ppermute | solution.py:18
  134.2 20.9 %collective-permute-start.9 = (bf16[512,256]{0,1:T(8,128)(2,1)S(1)}, bf16[512,256]{0,1:T(8,128)(2,1)S(1)}, u32[]{:S(2)}, u32[]{:S(2)}) collective-permute-start(bf16[512,256]{0,1:T(8,128)(2,1)S(1)} %bitcast.92), channel_id=1, source_target_pairs={{0,8},{8,16},{16,24},{24,32},{32,40},{40,48},{48,56},{56,64},{64,7... | collective-permute-start | bytes 786440 | tf_op jit(solution)/shard_map/ppermute | solution.py:18
  138.8 24.8 %collective-permute-start.10 = (bf16[512,256]{0,1:T(8,128)(2,1)S(1)}, bf16[512,256]{0,1:T(8,128)(2,1)S(1)}, u32[]{:S(2)}, u32[]{:S(2)}) collective-permute-start(bf16[512,256]{0,1:T(8,128)(2,1)S(1)} %slice.104), channel_id=1, source_target_pairs={{0,8},{8,16},{16,24},{24,32},{32,40},{40,48},{48,56},{56,64},{64,7... | collective-permute-start | bytes 786440 | tf_op jit(solution)/shard_map/ppermute | solution.py:18
  141.4 30.3 %collective-permute-start.7 = (bf16[512,256]{0,1:T(8,128)(2,1)S(1)}, bf16[512,256]{0,1:T(8,128)(2,1)S(1)}, u32[]{:S(2)}, u32[]{:S(2)}) collective-permute-start(bf16[512,256]{0,1:T(8,128)(2,1)S(1)} %slice.104), channel_id=1, source_target_pairs={{0,16},{8,24},{16,32},{24,40},{32,48},{40,56},{48,64},{56,72},{64,... | collective-permute-start | bytes 786440 | tf_op jit(solution)/shard_map/ppermute | solution.py:18
  150.6 4.6 %copy-start.1 = (pred[512,1536]{0,1:T(8,128)(4,1)S(1)}, pred[512,1536]{0,1:T(8,128)(4,1)}, u32[]{:S(2)}) copy-start(pred[512,1536]{0,1:T(8,128)(4,1)} %and_and_fusion) | copy-start | bytes 2359300
Sparse Core Ops, SparseCore 0:
  9.9 112.7 all-gather.1
  182.6 40.6 reduce-scatter.1

commit v14 on v12

--- a/solution.py
+++ b/solution.py
@@ -108,8 +108,15 @@
     weights = jnp.where(allowed, jnp.exp(masked - top), 0.0)
     total = jnp.sum(weights, axis=-1)
     probs = weights.astype(jnp.bfloat16)
+    first_block = earlier_values[0].reshape(rows, kv_heads, HEAD_SIZE)
+    rest = jnp.concatenate(earlier_values[1:] + [value_rows], axis=0)
     mixed = jnp.einsum(
-        "kgts,skd->tkgd", probs, values_three_axes, preferred_element_type=jnp.float32
+        "kgts,skd->tkgd", probs[..., :rows], first_block, preferred_element_type=jnp.float32
+    ) + jnp.einsum(
+        "kgts,skd->tkgd",
+        probs[..., rows:],
+        rest.reshape(window_extent - rows, kv_heads, HEAD_SIZE),
+        preferred_element_type=jnp.float32,
     )
     mixed = mixed / jnp.transpose(total, (2, 0, 1))[..., None]
     heads_out = mixed.reshape(rows, width_query).astype(jnp.bfloat16)

time: 228 us -> 227 us (level)
    ppermute x4, waiting for transfers between devices: 11.2 us -> 8.88 us  [shifted(): lax.ppermute(value, axis, [(source, source + steps) for source in range(l...]
    dot_general x1 -> x2, matrix products: 3.89 us -> 5.13 us  [the longest x1 3.07 us: local(): jnp.einsum('kgts,skd->tkgd', probs[..., rows:], rest.reshape(window_exten...]
  transfers between devices with their start and end apart: 13 -> 13, of which waited for: 9 -> 8; matrix products, arithmetic and copies ran while one was open for 21% -> 23% of each run, Pallas kernels for 0% -> 0%
where the time goes in v14:
time: 227 us; the launch traced here: 226 us
  waiting for transfers between devices  106 us (47%)
  starting transfers between devices  37.7 us (17%)
  matrix products  32.5 us (14%)
  other arithmetic  18.7 us (8%)
  local copies, waits for them, and re-layouts  18.1 us (8%)
  between operations  13.7 us (6%)
    reduce_scatter x1, waiting for transfers between devices, local(): lax.psum_scatter(partial_value.astype(jnp.bfloat16), 'hid', scatter_dimen...  40.8 us
    ppermute x7, waiting for transfers between devices, local(): lax.ppermute(with_gain, 'hid', [(i, (i + k) % n_hid) for i in range(n_hid)])  33.8 us
    ppermute x7, starting transfers between devices, local(): lax.ppermute(with_gain, 'hid', [(i, (i + k) % n_hid) for i in range(n_hid)])  24.1 us
    all_gather x1, waiting for transfers between devices, local(): lax.all_gather(jnp.concatenate([w_query, w_key, value_matrix], axis=1), '...  22.4 us
    ppermute x4, starting transfers between devices, shifted(): lax.ppermute(value, axis, [(source, source + steps) for source in range(l...  13.5 us
    unnamed x16, local copies, waits for them, and re-layouts  10.6 us
    ppermute x4, waiting for transfers between devices, shifted(): lax.ppermute(value, axis, [(source, source + steps) for source in range(l...  8.88 us
    sub x1, matrix products, local(): weights = jnp.where(allowed, jnp.exp(masked - top), 0.0)  8.49 us
  transfers between devices with their start and end apart: 13, of which 8 were waited for; matrix products, arithmetic and copies ran while one was open for 23% of the time, Pallas kernels for 0%

profile of v14, /device:TPU:2, one launch (start us, length us, event | category | flops | bytes accessed | tf_op | source)
XLA Modules:
  0.0 226.5 jit_solution(8821352414712873685)
XLA Ops:
  6.5 1.8 pad_maximum_fusion.4
  8.4 1.4 copy.20
  9.8 0.8 pad_maximum_fusion
  10.6 1.7 collective-permute-start.1
  12.2 2.2 collective-permute-start.2
  14.4 1.8 collective-permute-start.3
  16.3 1.8 collective-permute-start.4
  18.2 0.5 multiply_cosine_fusion
  18.7 1.9 and_and_fusion
  20.6 0.7 bitcast_convert_fusion
  21.2 0.7 bitcast_convert_fusion.1
  21.9 1.6 bitcast_dynamic-update-slice_fusion.7
  23.6 7.7 %collective-permute-done = bf16[513,672]{1,0:T(8,128)(2,1)} collective-permute-done((bf16[513,672]{1,0:T(8,128)(2,1)S(1)}, bf16[513,672]{1,0:T(8,128)(2,1)}, u32[]{:S(2)}, u32[]{:S(2)}) %collective-permute-start) | collective-permute-done | bytes 689504 | tf_op jit(solution)/shard_map/ppermute | solution.py:53
  31.3 1.8 collective-permute-start.5
  33.1 2.1 bitcast_dynamic-update-slice_fusion.6
  35.2 14.7 %collective-permute-start.6 = (bf16[513,672]{1,0:T(8,128)(2,1)S(1)}, bf16[513,672]{1,0:T(8,128)(2,1)S(1)}, u32[]{:S(2)}, u32[]{:S(2)}) collective-permute-start(bf16[513,672]{1,0:T(8,128)(2,1)S(1)} %pad_maximum_fusion), channel_id=1, source_target_pairs={{0,7},{1,0},{2,1},{3,2},{4,3},{5,4},{6,5},{7,6},{8,15},{9,8},{10,9... | collective-permute-start | bytes 2068424 | tf_op jit(solution)/shard_map/ppermute | solution.py:53
  49.9 2.1 bitcast_dynamic-update-slice_fusion.5
  52.1 14.7 %collective-permute-done.2 = bf16[513,672]{1,0:T(8,128)(2,1)} collective-permute-done((bf16[513,672]{1,0:T(8,128)(2,1)S(1)}, bf16[513,672]{1,0:T(8,128)(2,1)}, u32[]{:S(2)}, u32[]{:S(2)}) %collective-permute-start.2) | collective-permute-done | bytes 689504 | tf_op jit(solution)/shard_map/ppermute | solution.py:53
  66.8 2.1 bitcast_dynamic-update-slice_fusion.4
  68.9 0.9 bitcast_dynamic-update-slice_fusion.3
  69.8 11.3 %collective-permute-done.4 = bf16[513,672]{1,0:T(8,128)(2,1)S(1)} collective-permute-done((bf16[513,672]{1,0:T(8,128)(2,1)S(1)}, bf16[513,672]{1,0:T(8,128)(2,1)S(1)}, u32[]{:S(2)}, u32[]{:S(2)}) %collective-permute-start.4) | collective-permute-done | bytes 689504 | tf_op jit(solution)/shard_map/ppermute | solution.py:53
  81.1 1.0 bitcast_dynamic-update-slice_fusion.2
  82.1 1.0 bitcast_dynamic-update-slice_fusion.1
  83.1 1.0 bitcast_dynamic-update-slice_fusion
  84.1 6.5 %gather_fusion = bf16[8,513,672]{2,1,0:T(8,128)(2,1)} fusion(bf16[8,513,672]{2,1,0:T(8,128)(2,1)} %bitcast_dynamic-update-slice_fusion, s32[1024]{0:T(1024)S(1)} %pad_clamp_fusion), kind=kCustom, calls=%fused_computation | custom fusion | bytes 11031584 | tf_op jit(solution)/shard_map/jit(_take)/gather | solution.py:57
  90.6 3.7 %broadcast_select_fusion = bf16[8,513,672]{2,1,0:T(8,128)(2,1)S(1)} fusion(bf16[8,513,672]{2,1,0:T(8,128)(2,1)} %gather_fusion, pred[8]{0:T(512)(128)(4,1)S(1)} %compare_and_fusion), kind=kLoop, calls=%fused_computation.11 | loop fusion | flops 2757888 | bytes 11031560 | tf_op jit(solution)/shard_map/jit(_take)/select_n | solution.py:57
  94.3 1.4 fusion.1
  95.7 4.7 %fusion.3 = bf16[8,512,672]{2,1,0:T(8,128)(2,1)} fusion(f32[8,672]{1,0:T(8,128)S(1)} %bitcast.91, f32[512]{0:T(512)S(1)} %add_rsqrt_fusion.2, bf16[8,513,672]{2,1,0:T(8,128)(2,1)S(1)} %broadcast_select_fusion), kind=kLoop, calls=%fused_computation.6 | loop fusion | flops 11010048 | bytes 11033600 | tf_op jit(solution)/shard_map/convert_element_type | solution.py:62
  100.4 22.4 %all-gather.2.cloned.1.call-done = bf16[5376,1024]{1,0:T(8,128)(2,1)} async-done(((bf16[168,1024]{1,0:T(8,128)(2,1)}), bf16[5376,1024]{1,0:T(8,128)(2,1)}) %all-gather.2.cloned.1.call-update) | async-done | bytes 11010064 | tf_op jit(solution)/shard_map/all_gather | solution.py:65
  122.7 8.4 %fusion.16 = f32[512,512]{0,1:T(8,128)S(1)} fusion(bf16[8,512,672]{2,1,0:T(8,128)(2,1)} %fusion.3, bf16[8,672,1024]{2,1,0:T(8,128)(2,1)} %bitcast.92), kind=kOutput, calls=%fused_computation.24 | convolution fusion | flops 2818572288 | bytes 12845056 | tf_op jit(solution)/shard_map/jrc,jcn->rn/dot_general | solution.py:69
  131.1 0.1 multiply_reduce_fusion.1
  131.2 0.1 multiply_multiply_fusion.1
  131.3 0.1 subtract_convert_fusion.1
  131.5 2.7 %collective-permute-start.8 = (bf16[512,256]{0,1:T(8,128)(2,1)S(1)}, bf16[512,256]{0,1:T(8,128)(2,1)S(1)}, u32[]{:S(2)}, u32[]{:S(2)}) collective-permute-start(bf16[512,256]{0,1:T(8,128)(2,1)S(1)} %bitcast.85), channel_id=1, source_target_pairs={{0,16},{8,24},{16,32},{24,40},{32,48},{40,56},{48,64},{56,72},{64,... | collective-permute-start | bytes 786440 | tf_op jit(solution)/shard_map/ppermute | solution.py:18
  134.2 4.7 %collective-permute-start.9 = (bf16[512,256]{0,1:T(8,128)(2,1)S(1)}, bf16[512,256]{0,1:T(8,128)(2,1)S(1)}, u32[]{:S(2)}, u32[]{:S(2)}) collective-permute-start(bf16[512,256]{0,1:T(8,128)(2,1)S(1)} %bitcast.86), channel_id=1, source_target_pairs={{0,8},{8,16},{16,24},{24,32},{32,40},{40,48},{48,56},{56,64},{64,7... | collective-permute-start | bytes 786440 | tf_op jit(solution)/shard_map/ppermute | solution.py:18
  138.8 2.6 %collective-permute-start.10 = (bf16[512,256]{0,1:T(8,128)(2,1)S(1)}, bf16[512,256]{0,1:T(8,128)(2,1)S(1)}, u32[]{:S(2)}, u32[]{:S(2)}) collective-permute-start(bf16[512,256]{0,1:T(8,128)(2,1)S(1)} %slice.95), channel_id=1, source_target_pairs={{0,8},{8,16},{16,24},{24,32},{32,40},{40,48},{48,56},{56,64},{64,7... | collective-permute-start | bytes 786440 | tf_op jit(solution)/shard_map/ppermute | solution.py:18
  141.4 3.6 %collective-permute-start.7 = (bf16[512,256]{0,1:T(8,128)(2,1)S(1)}, bf16[512,256]{0,1:T(8,128)(2,1)S(1)}, u32[]{:S(2)}, u32[]{:S(2)}) collective-permute-start(bf16[512,256]{0,1:T(8,128)(2,1)S(1)} %slice.95), channel_id=1, source_target_pairs={{0,16},{8,24},{16,32},{24,40},{32,48},{40,56},{48,64},{56,72},{64,... | collective-permute-start | bytes 786440 | tf_op jit(solution)/shard_map/ppermute | solution.py:18
  145.0 5.5 %fusion.8 = f32[512,512,1]{0,1,2:T(8,128)S(1)} fusion(bf16[8,512,672]{2,1,0:T(8,128)(2,1)S(1)} %copy-done, bf16[8,672,1024]{2,1,0:T(8,128)(2,1)} %bitcast.93), kind=kOutput, calls=%fused_computation.15 | convolution fusion | flops 2818572288 | bytes 12058624 | tf_op jit(solution)/shard_map/jrc,jcn->rn/dot_general | solution.py:82
  150.6 0.1 multiply_reduce_fusion
  150.7 0.2 multiply_multiply_fusion
  150.9 0.2 subtract_convert_fusion
  151.1 4.0 %collective-permute-done.9 = bf16[512,256]{0,1:T(8,128)(2,1)S(1)} collective-permute-done((bf16[512,256]{0,1:T(8,128)(2,1)S(1)}, bf16[512,256]{0,1:T(8,128)(2,1)S(1)}, u32[]{:S(2)}, u32[]{:S(2)}) %collective-permute-start.9) | collective-permute-done | bytes 262176 | tf_op jit(solution)/shard_map/ppermute | solution.py:18
  155.2 8.5 %fusion.40 = (f32[2,2,512]{2,1,0:T(2,128)S(1)}, bf16[2,2,512,1536]{2,3,1,0:T(8,128)(2,1)}) fusion(pred[512,1536]{0,1:T(8,128)(4,1)S(1)} %copy-done.1, bf16[1536,2,128,1]{0,2,3,1:T(8,128)(2,1)S(1)} %bitcast.88, bf16[512,2,2,128]{0,3,2,1:T(8,128)(2,1)S(1)} %bitcast.89), kind=kOutput, calls=%fused_computation.83 | convolution fusion | flops 824182272 | bytes 8396800 | tf_op jit(solution)/shard_map/sub | solution.py:108
  163.7 3.1 %fusion.12 = f32[2,128,2,512]{3,1,2,0:T(8,128)S(1)} fusion(bf16[1024,2,128,1]{0,2,3,1:T(8,128)(2,1)S(1)} %bitcast.90, bf16[2,2,512,1536]{2,3,1,0:T(8,128)(2,1)} %get-tuple-element.8), kind=kOutput, calls=%fused_computation.19 | convolution fusion | flops 536870912 | bytes 5767168 | tf_op jit(solution)/shard_map/kgts,skd->tkgd/dot_general | solution.py:115
  166.8 4.9 %collective-permute-done.7 = bf16[512,256]{0,1:T(8,128)(2,1)S(1)} collective-permute-done((bf16[512,256]{0,1:T(8,128)(2,1)S(1)}, bf16[512,256]{0,1:T(8,128)(2,1)S(1)}, u32[]{:S(2)}, u32[]{:S(2)}) %collective-permute-start.7) | collective-permute-done | bytes 262176 | tf_op jit(solution)/shard_map/ppermute | solution.py:18
  171.7 2.1 fusion.30
  173.8 5.0 %convolution_convert_fusion = bf16[512,5376]{0,1:T(8,128)(2,1)} fusion(bf16[512,512]{0,1:T(8,128)(2,1)S(1)} %bitcast.97, bf16[512,5376]{1,0:T(8,128)(2,1)S(1)} %bitcast.95), kind=kOutput, calls=%fused_computation.10 | convolution fusion | flops 2821324800 | bytes 11534336 | tf_op jit(solution)/shard_map/dot_general | solution.py:123
  178.8 40.8 %reduce-scatter.2.cloned.1.call-done = bf16[512,672]{0,1:T(8,128)(2,1)} async-done(((bf16[512,5376]{0,1:T(8,128)(2,1)}), bf16[512,672]{0,1:T(8,128)(2,1)}) %reduce-scatter.2.cloned.1.call-update) | async-done | bytes 688144 | tf_op jit(solution)/shard_map/reduce_scatter | solution.py:124
  (38 shorter events, 0.5 us)
Async XLA Ops:
  6.5 116.2 %all-gather.2.cloned.1.call-start = ((), (), s32[]{:S(2)}) async-start(), calls=%async_computation.1 | async-start | bytes 11354112 | tf_op jit(solution)/shard_map/all_gather | solution.py:65
  8.3 211.3 %reduce-scatter.2.cloned.1.call-start = ((), (), s32[]{:S(2)}) async-start(), calls=%async_computation.2 | async-start | bytes 6193152 | tf_op jit(solution)/shard_map/reduce_scatter | solution.py:124
  10.5 20.8 %collective-permute-start = (bf16[513,672]{1,0:T(8,128)(2,1)S(1)}, bf16[513,672]{1,0:T(8,128)(2,1)}, u32[]{:S(2)}, u32[]{:S(2)}) collective-permute-start(bf16[513,672]{1,0:T(8,128)(2,1)S(1)} %pad_maximum_fusion), channel_id=1, source_target_pairs={{0,1},{1,2},{2,3},{3,4},{4,5},{5,6},{6,7},{7,0},{8,9},{9,10},{10,1... | collective-permute-start | bytes 2068424 | tf_op jit(solution)/shard_map/ppermute | solution.py:53
  10.6 24.6 %collective-permute-start.1 = (bf16[513,672]{1,0:T(8,128)(2,1)S(1)}, bf16[513,672]{1,0:T(8,128)(2,1)}, u32[]{:S(2)}, u32[]{:S(2)}) collective-permute-start(bf16[513,672]{1,0:T(8,128)(2,1)S(1)} %pad_maximum_fusion), channel_id=1, source_target_pairs={{0,2},{1,3},{2,4},{3,5},{4,6},{5,7},{6,0},{7,1},{8,10},{9,11},{10,... | collective-permute-start | bytes 2068424 | tf_op jit(solution)/shard_map/ppermute | solution.py:53
  12.2 54.6 %collective-permute-start.2 = (bf16[513,672]{1,0:T(8,128)(2,1)S(1)}, bf16[513,672]{1,0:T(8,128)(2,1)}, u32[]{:S(2)}, u32[]{:S(2)}) collective-permute-start(bf16[513,672]{1,0:T(8,128)(2,1)S(1)} %pad_maximum_fusion), channel_id=1, source_target_pairs={{0,3},{1,4},{2,5},{3,6},{4,7},{5,0},{6,1},{7,2},{8,11},{9,12},{10,... | collective-permute-start | bytes 2068424 | tf_op jit(solution)/shard_map/ppermute | solution.py:53
  14.4 54.4 %collective-permute-start.3 = (bf16[513,672]{1,0:T(8,128)(2,1)S(1)}, bf16[513,672]{1,0:T(8,128)(2,1)S(1)}, u32[]{:S(2)}, u32[]{:S(2)}) collective-permute-start(bf16[513,672]{1,0:T(8,128)(2,1)S(1)} %pad_maximum_fusion), channel_id=1, source_target_pairs={{0,4},{1,5},{2,6},{3,7},{4,0},{5,1},{6,2},{7,3},{8,12},{9,13},{10,... | collective-permute-start | bytes 2068424 | tf_op jit(solution)/shard_map/ppermute | solution.py:53
  16.3 64.9 %collective-permute-start.4 = (bf16[513,672]{1,0:T(8,128)(2,1)S(1)}, bf16[513,672]{1,0:T(8,128)(2,1)S(1)}, u32[]{:S(2)}, u32[]{:S(2)}) collective-permute-start(bf16[513,672]{1,0:T(8,128)(2,1)S(1)} %pad_maximum_fusion), channel_id=1, source_target_pairs={{0,5},{1,6},{2,7},{3,0},{4,1},{5,2},{6,3},{7,4},{8,13},{9,14},{10,... | collective-permute-start | bytes 2068424 | tf_op jit(solution)/shard_map/ppermute | solution.py:53
  31.3 50.8 %collective-permute-start.5 = (bf16[513,672]{1,0:T(8,128)(2,1)S(1)}, bf16[513,672]{1,0:T(8,128)(2,1)S(1)}, u32[]{:S(2)}, u32[]{:S(2)}) collective-permute-start(bf16[513,672]{1,0:T(8,128)(2,1)S(1)} %pad_maximum_fusion), channel_id=1, source_target_pairs={{0,6},{1,7},{2,0},{3,1},{4,2},{5,3},{6,4},{7,5},{8,14},{9,15},{10,... | collective-permute-start | bytes 2068424 | tf_op jit(solution)/shard_map/ppermute | solution.py:53
  35.2 47.9 %collective-permute-start.6 = (bf16[513,672]{1,0:T(8,128)(2,1)S(1)}, bf16[513,672]{1,0:T(8,128)(2,1)S(1)}, u32[]{:S(2)}, u32[]{:S(2)}) collective-permute-start(bf16[513,672]{1,0:T(8,128)(2,1)S(1)} %pad_maximum_fusion), channel_id=1, source_target_pairs={{0,7},{1,0},{2,1},{3,2},{4,3},{5,4},{6,5},{7,6},{8,15},{9,8},{10,9... | collective-permute-start | bytes 2068424 | tf_op jit(solution)/shard_map/ppermute | solution.py:53
  122.7 22.3 %copy-start = (bf16[8,512,672]{2,1,0:T(8,128)(2,1)S(1)}, bf16[8,512,672]{2,1,0:T(8,128)(2,1)}, u32[]{:S(2)}) copy-start(bf16[8,512,672]{2,1,0:T(8,128)(2,1)} %fusion.3) | copy-start | bytes 16515076
  131.5 19.7 %collective-permute-start.8 = (bf16[512,256]{0,1:T(8,128)(2,1)S(1)}, bf16[512,256]{0,1:T(8,128)(2,1)S(1)}, u32[]{:S(2)}, u32[]{:S(2)}) collective-permute-start(bf16[512,256]{0,1:T(8,128)(2,1)S(1)} %bitcast.85), channel_id=1, source_target_pairs={{0,16},{8,24},{16,32},{24,40},{32,48},{40,56},{48,64},{56,72},{64,... | collective-permute-start | bytes 786440 | tf_op jit(solution)/shard_map/ppermute | solution.py:18
  134.2 20.9 %collective-permute-start.9 = (bf16[512,256]{0,1:T(8,128)(2,1)S(1)}, bf16[512,256]{0,1:T(8,128)(2,1)S(1)}, u32[]{:S(2)}, u32[]{:S(2)}) collective-permute-start(bf16[512,256]{0,1:T(8,128)(2,1)S(1)} %bitcast.86), channel_id=1, source_target_pairs={{0,8},{8,16},{16,24},{24,32},{32,40},{40,48},{48,56},{56,64},{64,7... | collective-permute-start | bytes 786440 | tf_op jit(solution)/shard_map/ppermute | solution.py:18
  138.8 24.8 %collective-permute-start.10 = (bf16[512,256]{0,1:T(8,128)(2,1)S(1)}, bf16[512,256]{0,1:T(8,128)(2,1)S(1)}, u32[]{:S(2)}, u32[]{:S(2)}) collective-permute-start(bf16[512,256]{0,1:T(8,128)(2,1)S(1)} %slice.95), channel_id=1, source_target_pairs={{0,8},{8,16},{16,24},{24,32},{32,40},{40,48},{48,56},{56,64},{64,7... | collective-permute-start | bytes 786440 | tf_op jit(solution)/shard_map/ppermute | solution.py:18
  141.4 30.3 %collective-permute-start.7 = (bf16[512,256]{0,1:T(8,128)(2,1)S(1)}, bf16[512,256]{0,1:T(8,128)(2,1)S(1)}, u32[]{:S(2)}, u32[]{:S(2)}) collective-permute-start(bf16[512,256]{0,1:T(8,128)(2,1)S(1)} %slice.95), channel_id=1, source_target_pairs={{0,16},{8,24},{16,32},{24,40},{32,48},{40,56},{48,64},{56,72},{64,... | collective-permute-start | bytes 786440 | tf_op jit(solution)/shard_map/ppermute | solution.py:18
  150.6 4.6 %copy-start.1 = (pred[512,1536]{0,1:T(8,128)(4,1)S(1)}, pred[512,1536]{0,1:T(8,128)(4,1)}, u32[]{:S(2)}) copy-start(pred[512,1536]{0,1:T(8,128)(4,1)} %and_and_fusion) | copy-start | bytes 2359300
  163.7 10.2 %slice-start = ((s8[5505024]{0:T(1024)(128)(4,1)}), s8[4194304]{0:T(1024)(128)(4,1)S(1)}, s32[]{:S(2)}) async-start(s8[5505024]{0:T(1024)(128)(4,1)} %bitcast.94), calls=%async_computation.3 | async-start | bytes 8388608
  163.7 10.1 %slice-start.1 = ((s8[5505024]{0:T(1024)(128)(4,1)}), s8[1310720]{0:T(1024)(128)(4,1)S(1)}, s32[]{:S(2)}) async-start(s8[5505024]{0:T(1024)(128)(4,1)} %bitcast.94), calls=%async_computation.4 | async-start | bytes 2621440
Sparse Core Ops, SparseCore 0:
  9.9 112.7 all-gather.1
  178.9 40.6 reduce-scatter.1
